TPU v7x, 32 devices: a whole 2x2x4 slice. The times are simulated.
32 devices in a mesh: expert: 8 (over z, x), rep: 4 (over y, core).
Axes of the slice: x: 2, y: 2, z: 4, core: 2. Of those that a mesh axis runs over, the one named last changes fastest.
Arguments:
- tokens: bfloat16 [4, 2048, 2, 2048], P('rep', 'expert'), may hold values from -6 to 6
- expert_ids: int32 [4, 2048, 2, 2], P('rep', 'expert'), may hold values from 0 to 15, all different within a row; in each aligned block of 512 rows (0 to 511, 512 to 1023, ..., all dimensions but the last counted through in order) at most 80 rows name the same one
- gate_probs: float32 [4, 2048, 2, 2], P('rep', 'expert'), may hold values from 0.1 to 1
- norm_gain: float32 [2048], replicated, may hold values from 0.25 to 1.75
- expert_gate: bfloat16 [16, 2048, 1408], P('expert', None, 'rep'), may hold values from -0.125 to 0.125
- expert_up: bfloat16 [16, 2048, 1408], P('expert', None, 'rep'), may hold values from -0.125 to 0.125
- expert_down: bfloat16 [16, 1408, 2048], P('expert', 'rep'), may hold values from -0.15625 to 0.15625
- teacher_gain: float32 [2048], replicated, may hold values from 0.25 to 1.75
- teacher_qkv: bfloat16 [2048, 3, 16, 128], P(None, None, 'rep')
- qk_gain: float32 [2, 16, 128], P(None, 'rep'), may hold values from 0.5 to 7.5
- teacher_out: bfloat16 [16, 128, 2048], P('rep'), may hold values from -0.125 to 0.125
- critic_in: bfloat16 [2048, 1024], replicated, may hold values from -0.125 to 0.125
- critic_out: float32 [1024], replicated, may hold values from -0.1875 to 0.1875
Outputs:
- teacher_features: bfloat16 [4, 2048, 2, 2048], P('rep', 'expert')
- critic_logits: float32 [4, 2048, 2], P('rep', 'expert')
Inputs may be any that keep to these rules, and one draw needn't show every extreme that they name: `expert_ids`: the 512 rows of one device name one expert at most 80 times in all, and some device reaches 80; the two experts of a token differ.
All inputs are finite; a program needn't handle non-finite values.
Results may differ from a plain program's by a relative error of at most 0.033.
Values may be sent and summed in bfloat16 or wider, within the bound.
No kernel may reach another device: no remote copies, remote signals or barrier semaphores. Data moves between devices by JAX's collectives and lax.ppermute only.
A program may use at most 192 MiB of HBM per device.

v0:
```python
import jax
import jax.numpy as jnp
from jax import lax
from jax.sharding import PartitionSpec as P


def norm_rows(values, gain):
    return values * lax.rsqrt(jnp.mean(values * values, axis=-1, keepdims=True) + 1e-06) * gain


def slot_numbers(chosen, count):
    onehot = (chosen[..., None] == jnp.arange(count, dtype=jnp.int32)).astype(jnp.int32)
    before = jnp.cumsum(onehot, axis=-2) - onehot
    return jnp.sum(before * onehot, axis=-1)


def local(
    tokens,
    expert_ids,
    gate_probs,
    norm_gain,
    expert_gate,
    expert_up,
    expert_down,
    teacher_gain,
    teacher_qkv,
    qk_gain,
    teacher_out,
    critic_in,
    critic_out,
):
    seq_dev = tokens.shape[1]
    images = tokens.shape[2]
    width = tokens.shape[3]
    tok_count = seq_dev * images
    n_owner = lax.axis_size("expert")
    n_replica = lax.axis_size("rep")
    exp_local = expert_gate.shape[0]
    expert_total = exp_local * n_owner
    capacity = max(2, tok_count * 10 // (4 * expert_total))
    residual = tokens.reshape(tok_count, width).astype(jnp.float32)
    normed = norm_rows(residual, norm_gain).astype(jnp.bfloat16)
    chosen = expert_ids.reshape(2 * tok_count)
    slot_index = slot_numbers(chosen, expert_total)
    gate_value = gate_probs.reshape(2 * tok_count)
    target = chosen * capacity + slot_index
    token_of = jnp.arange(2 * tok_count, dtype=jnp.int32) // 2
    owner_token = jnp.zeros((expert_total * capacity,), jnp.int32).at[target].set(token_of)
    filled = jnp.zeros((expert_total * capacity,), jnp.bool_).at[target].set(True)
    outgoing = jnp.where(
        filled[:, None], jnp.take(normed, owner_token, axis=0), jnp.zeros((), jnp.bfloat16)
    )
    outgoing = outgoing.reshape(n_owner, exp_local * capacity, width)
    arrived = lax.all_to_all(outgoing, "expert", split_axis=0, concat_axis=0, tiled=True)
    arrived = arrived.reshape(1, n_owner, exp_local, capacity, width)
    piece = lax.all_gather(arrived, "rep", axis=0, tiled=True)
    gate_part = jnp.einsum(
        "rsjcd,jdf->rsjcf", piece, expert_gate, preferred_element_type=jnp.float32
    )
    up_part = jnp.einsum("rsjcd,jdf->rsjcf", piece, expert_up, preferred_element_type=jnp.float32)
    hidden = (jax.nn.silu(gate_part) * up_part).astype(jnp.bfloat16)
    piece = hidden
    produced = lax.psum_scatter(
        jnp.einsum(
            "rsjcf,jfd->rsjcd", piece, expert_down, preferred_element_type=jnp.float32
        ).astype(jnp.bfloat16),
        "rep",
        scatter_dimension=0,
        tiled=True,
    )
    results = produced.reshape(n_owner, exp_local * capacity, width)
    returned = lax.all_to_all(results, "expert", split_axis=0, concat_axis=0, tiled=True).reshape(
        expert_total * capacity, width
    )
    picked = jnp.take(returned, target, axis=0).astype(jnp.float32) * gate_value[:, None]
    combined = picked.reshape(tok_count, 2, width).sum(axis=1)
    mixed = (residual + combined).astype(jnp.bfloat16)
    teacher_in = norm_rows(mixed.astype(jnp.float32), teacher_gain).astype(jnp.bfloat16)
    teacher_in = teacher_in.reshape(1, seq_dev, images, width)
    heads_local = teacher_qkv.shape[2]
    head_size = teacher_qkv.shape[3]
    projected = jnp.einsum(
        "rsid,djhe->jrihse",
        lax.all_gather(teacher_in, "rep", axis=0, tiled=True),
        teacher_qkv,
        preferred_element_type=jnp.float32,
    )
    query = norm_rows(projected[0], qk_gain[0][:, None, :])
    keyed = norm_rows(projected[1], qk_gain[1][:, None, :])
    projected = jnp.stack([query, keyed, projected[2]]).astype(jnp.bfloat16)
    pairs_all = n_replica * images * heads_local
    grouped = projected.reshape(3, pairs_all, seq_dev, head_size)
    whole = lax.all_to_all(grouped, "expert", split_axis=1, concat_axis=2, tiled=True)
    pairs_local = whole.shape[1]
    seq_len = whole.shape[2]
    block = min(512, seq_len)
    blocks_count = seq_len // block
    key_rows = whole[1]
    value_rows = whole[2]

    def attend(query_block):
        scores = jnp.einsum(
            "pqe,pke->pqk", query_block, key_rows, preferred_element_type=jnp.float32
        ) * head_size ** (-0.5)
        scores = scores - jnp.max(scores, axis=-1, keepdims=True)
        weights = jnp.exp(scores)
        probs = (weights / jnp.sum(weights, axis=-1, keepdims=True)).astype(jnp.bfloat16)
        return jnp.einsum(
            "pqk,pke->pqe", probs, value_rows, preferred_element_type=jnp.float32
        ).astype(jnp.bfloat16)

    query_blocks = (
        whole[0].reshape(pairs_local, blocks_count, block, head_size).transpose(1, 0, 2, 3)
    )
    attended = (
        lax.map(attend, query_blocks).transpose(1, 0, 2, 3).reshape(pairs_local, seq_len, head_size)
    )
    gathered_heads = lax.all_to_all(attended, "expert", split_axis=1, concat_axis=0, tiled=True)
    gathered_heads = gathered_heads.reshape(n_replica, images, heads_local, seq_dev, head_size)
    piece = gathered_heads
    projected_out = lax.psum_scatter(
        jnp.einsum(
            "rihse,hed->rsid", piece, teacher_out, preferred_element_type=jnp.float32
        ).astype(jnp.bfloat16),
        "rep",
        scatter_dimension=0,
        tiled=True,
    ).astype(jnp.float32)
    features = (
        mixed.reshape(1, seq_dev, images, width).astype(jnp.float32) + projected_out
    ).astype(jnp.bfloat16)
    critic_hidden = jax.nn.gelu(
        jnp.dot(features.reshape(tok_count, width), critic_in, preferred_element_type=jnp.float32),
        approximate=True,
    )
    logits = jnp.dot(
        critic_hidden,
        critic_out,
        precision=lax.Precision.HIGHEST,
        preferred_element_type=jnp.float32,
    )
    return (features, logits.reshape(1, seq_dev, images))


def solution(mesh):
    return jax.shard_map(
        local,
        mesh=mesh,
        in_specs=(
            P("rep", "expert", None, None),
            P("rep", "expert", None, None),
            P("rep", "expert", None, None),
            P(),
            P("expert", None, "rep"),
            P("expert", None, "rep"),
            P("expert", "rep", None),
            P(),
            P(None, None, "rep", None),
            P(None, "rep", None),
            P("rep", None, None),
            P(),
            P(),
        ),
        out_specs=(P("rep", "expert", None, None), P("rep", "expert", None)),
        check_vma=False,
    )
```

profile of v0, /device:TPU:0, one launch (start us, length us, event | category | flops | bytes accessed | tf_op | source)
XLA Modules:
  0.0 1461.5 jit_solution(2136674678946366932)
XLA Ops:
  9.7 4.5 copy_convert_fusion
  14.2 1.2 multiply_reduce_fusion.4
  15.4 4.5 reduce-window.6
  20.9 4.8 scatter_custom_fusion.1
  25.8 7.3 copy.109
  33.2 6.1 reshape.213
  39.6 4.3 scatter_custom_fusion
  44.1 3.9 multiply_convert_fusion.2
  48.0 12.7 gather_fusion
  60.7 3.7 select_select_fusion
  64.4 122.9 %all_to_all.40 = bf16[8,160,2048]{2,1,0:T(8,128)(2,1)S(1)} all-to-all(bf16[8,160,2048]{2,1,0:T(8,128)(2,1)S(1)} %select_select_fusion), channel_id=1, replica_groups=mesh['expert'=8,'rep'=4] {'expert'}, dimensions={0} | all-to-all | bytes 10485760 | tf_op jit(solution)/shard_map/all_to_all | solution.py:54
  187.3 2.8 copy.111
  190.1 129.1 %all-gather.3.cloned.1.call-done = bf16[4,8,2,80,2048]{4,3,1,0,2:T(8,128)(2,1)} async-done(((bf16[1,8,2,80,2048]{4,3,1,0,2:T(8,128)(2,1)}), bf16[4,8,2,80,2048]{4,3,1,0,2:T(8,128)(2,1)}) %all-gather.3.cloned.1.call-update) | async-done | bytes 20971536 | tf_op jit(solution)/shard_map/all_gather | solution.py:56
  319.2 17.9 %fusion.41 = f32[2,4,8,80,352]{4,3,2,1,0:T(8,128)} fusion(bf16[4,8,2,80,2048]{4,3,1,0,2:T(8,128)(2,1)} %all-gather.3.cloned.1.call-done, bf16[2,2048,352]{1,2,0:T(8,128)(2,1)} %param.20), kind=kOutput, calls=%fused_computation.58 | convolution fusion | flops 7381975040 | bytes 31064064 | tf_op jit(solution)/shard_map/rsjcd,jdf->rsjcf/dot_general | solution.py:60
  337.1 28.6 %convert_bitcast_fusion = bf16[4,8,2,80,2048]{4,3,1,0,2:T(8,128)(2,1)} fusion(f32[2,4,8,80,352]{4,3,2,1,0:T(8,128)} %fusion.41, bf16[4,8,2,80,2048]{4,3,1,0,2:T(8,128)(2,1)} %all-gather.3.cloned.1.call-done, bf16[2,352,2048]{2,1,0:T(8,128)(2,1)S(1)} %copy-done, bf16[2,2048,352]{1,2,0:T(8,128)(2,1)} %param.19), kind=kOutput, calls=%fused_computation.21 | convolution fusion | flops 14785249280 | bytes 54919168 | tf_op jit(solution)/shard_map/rsjcf,jfd->rsjcd/dot_general | solution.py:64
  366.9 355.2 %all-reduce.3.cloned.1.call-done = bf16[4,8,2,80,2048]{4,3,1,0,2:T(8,128)(2,1)} async-done(((bf16[4,8,2,80,2048]{4,3,1,0,2:T(8,128)(2,1)}), bf16[4,8,2,80,2048]{4,3,1,0,2:T(8,128)(2,1)}) %all-reduce.3.cloned.1.call-update) | async-done | bytes 20971536
  722.2 3.6 constant_dynamic-slice_fusion
  725.8 2.8 copy.112
  728.6 5.6 all-to-all-start.1
  735.5 114.4 %all-to-all-done.1 = bf16[8,160,2048]{2,1,0:T(8,128)(2,1)} async-done(((bf16[8,160,2048]{2,1,0:T(8,128)(2,1)}), bf16[8,160,2048]{2,1,0:T(8,128)(2,1)}, u32[]{:S(2)}, u32[]{:S(2)}) %all-to-all-start.1) | async-done | bytes 5242912 | tf_op jit(solution)/shard_map/all_to_all | solution.py:72
  849.9 12.0 gather_fusion.1
  861.9 7.6 gather.15
  869.6 20.5 %multiply_reduce_fusion.1 = f32[512,2048]{1,0:T(8,128)} fusion(bf16[512,2,2048]{2,1,0:T(2,128)(2,1)} %gather.15, pred[512,2]{1,0:T(8,128)(4,1)S(1)} %copy.107, f32[512,2]{1,0:T(8,128)S(1)} %bitcast.163), kind=kLoop, calls=%fused_computation.26 | loop fusion | flops 7340032 | bytes 8393728 | tf_op jit(solution)/shard_map/reduce_sum | solution.py:76
  890.0 6.0 reduce_sum.74
  896.0 5.9 fusion.34
  902.0 1.3 copy-done.4
  903.3 1.9 fusion.36
  905.3 56.6 %all-gather.5.cloned.1.call-done = bf16[4,256,2,2048]{3,1,2,0:T(8,128)(2,1)} async-done(((bf16[1,256,2,2048]{3,1,2,0:T(8,128)(2,1)}), bf16[4,256,2,2048]{3,1,2,0:T(8,128)(2,1)}) %all-gather.5.cloned.1.call-update) | async-done | bytes 8388624 | tf_op jit(solution)/shard_map/all_gather | solution.py:84
  961.8 17.9 %fusion.29 = f32[3,4,2,4,256,128]{4,5,3,0,2,1:T(8,128)S(1)} fusion(bf16[2048,3,4,128,1,1]{3,2,1,0,5,4:T(4,128)(2,1)} %bitcast.171, bf16[4,256,2,2048]{3,1,2,0:T(8,128)(2,1)} %all-gather.5.cloned.1.call-done), kind=kOutput, calls=%fused_computation.41 | convolution fusion | flops 12884901888 | bytes 27262976 | tf_op jit(solution)/shard_map/rsid,djhe->jrihse/dot_general | solution.py:82
  979.7 1.2 multiply_reduce_fusion.3
  981.3 2.7 multiply_convert_fusion.1
  983.9 4.1 copy.117
  988.0 4.1 copy.118
  992.1 2.9 copy.119
  994.9 6.4 pad_maximum_fusion
  1001.4 5.5 all-to-all-start.2
  1006.9 138.6 %all-to-all-done.2 = bf16[3,32,256,128]{3,2,0,1:T(8,128)(2,1)} async-done(((bf16[3,32,256,128]{3,2,0,1:T(8,128)(2,1)}), bf16[3,32,256,128]{3,2,0,1:T(8,128)(2,1)}, u32[]{:S(2)}, u32[]{:S(2)}) %all-to-all-start.2) | async-done | bytes 6291488 | tf_op jit(solution)/shard_map/all_to_all | solution.py:93
  1145.5 3.2 copy.120
  1149.2 1.6 copy.121
  1151.0 1.5 copy.123
  1152.5 152.2 %while.10 = (s32[]{:T(128)}, bf16[4,4,512,128]{3,2,0,1:T(8,128)(2,1)}, bf16[4,4,512,128]{3,2,0,1:T(8,128)(2,1)}, bf16[4,2048,128]{2,1,0:T(8,128)(2,1)S(1)}, bf16[4,2048,128]{2,1,0:T(8,128)(2,1)}, /*index=5*/s32[]{:T(128)}) while((s32[]{:T(128)}, bf16[4,4,512,128]{3,2,0,1:T(8,128)(2,1)}, bf16[4,4,512,128]{3,2,0,1:T(8,128)(2,1)}, ...), condition=%wide.region_14.15_spmd, body=%wide.region_11.14_spmd.sunk | while | flops 2185500672 | bytes 72369224 | solution.py:116
  1152.7 9.1 fusion.98
  1161.8 14.2 fusion.99
  1175.9 14.7 %fusion.100 = bf16[4,4,512,128]{3,2,0,1:T(8,128)(2,1)} fusion(bf16[4,4,512,128]{3,2,0,1:T(8,128)(2,1)} %get-tuple-element.121, s32[]{:T(128)} %get-tuple-element.120, bf16[4,2048,128]{2,1,0:T(8,128)(2,1)} %get-tuple-element.130, f32[4,512]{1,0:T(4,128)S(1)} %fusion.99, f32[4,512,2048]{2,1,0:T(8,128)} %fusion.98), kind=kOutput, calls=%fused_computation.13.clone.1 | convolution fusion | flops 1094979584 | bytes 36184576 | tf_op jit(solution)/shard_map/while/body/eval_jaxpr/pqk,pke->pqe/dot_general | solution.py:108
  1190.7 9.1 fusion.98
  1199.8 14.2 fusion.99
  1214.0 14.7 %fusion.100 = bf16[4,4,512,128]{3,2,0,1:T(8,128)(2,1)} fusion(bf16[4,4,512,128]{3,2,0,1:T(8,128)(2,1)} %get-tuple-element.121, s32[]{:T(128)} %get-tuple-element.120, bf16[4,2048,128]{2,1,0:T(8,128)(2,1)} %get-tuple-element.130, f32[4,512]{1,0:T(4,128)S(1)} %fusion.99, f32[4,512,2048]{2,1,0:T(8,128)} %fusion.98), kind=kOutput, calls=%fused_computation.13.clone.1 | convolution fusion | flops 1094979584 | bytes 36184576 | tf_op jit(solution)/shard_map/while/body/eval_jaxpr/pqk,pke->pqe/dot_general | solution.py:108
  1228.7 9.1 fusion.98
  1237.8 14.2 fusion.99
  1252.0 14.7 %fusion.100 = bf16[4,4,512,128]{3,2,0,1:T(8,128)(2,1)} fusion(bf16[4,4,512,128]{3,2,0,1:T(8,128)(2,1)} %get-tuple-element.121, s32[]{:T(128)} %get-tuple-element.120, bf16[4,2048,128]{2,1,0:T(8,128)(2,1)} %get-tuple-element.130, f32[4,512]{1,0:T(4,128)S(1)} %fusion.99, f32[4,512,2048]{2,1,0:T(8,128)} %fusion.98), kind=kOutput, calls=%fused_computation.13.clone.1 | convolution fusion | flops 1094979584 | bytes 36184576 | tf_op jit(solution)/shard_map/while/body/eval_jaxpr/pqk,pke->pqe/dot_general | solution.py:108
  1266.7 9.1 fusion.98
  1275.8 14.2 fusion.99
  1290.0 14.8 %fusion.100 = bf16[4,4,512,128]{3,2,0,1:T(8,128)(2,1)} fusion(bf16[4,4,512,128]{3,2,0,1:T(8,128)(2,1)} %get-tuple-element.121, s32[]{:T(128)} %get-tuple-element.120, bf16[4,2048,128]{2,1,0:T(8,128)(2,1)} %get-tuple-element.130, f32[4,512]{1,0:T(4,128)S(1)} %fusion.99, f32[4,512,2048]{2,1,0:T(8,128)} %fusion.98), kind=kOutput, calls=%fused_computation.13.clone.1 | convolution fusion | flops 1094979584 | bytes 36184576 | tf_op jit(solution)/shard_map/while/body/eval_jaxpr/pqk,pke->pqe/dot_general | solution.py:108
  1304.7 3.4 copy.126
  1308.2 52.0 %all_to_all.41 = bf16[4,2048,128]{2,0,1:T(4,128)(2,1)S(1)} all-to-all(bf16[4,2048,128]{2,0,1:T(4,128)(2,1)S(1)} %copy.126), channel_id=1, replica_groups=mesh['expert'=8,'rep'=4] {'expert'}, dimensions={1} | all-to-all | bytes 4194304 | tf_op jit(solution)/shard_map/all_to_all | solution.py:118
  1360.7 1.1 copy-done.11
  1361.8 6.6 fusion.21
  1368.4 69.7 %reduce-scatter.5.cloned.1.call-done = bf16[1,256,2,2048]{3,1,2,0:T(8,128)(2,1)} async-done(((bf16[4,256,2,2048]{3,1,2,0:T(8,128)(2,1)}), bf16[1,256,2,2048]{3,1,2,0:T(8,128)(2,1)}) %reduce-scatter.5.cloned.1.call-update) | async-done | bytes 2097168 | tf_op jit(solution)/shard_map/reduce_scatter | solution.py:121
  1438.1 2.4 fusion.37
  1440.4 2.2 copy.130
  1442.6 1.3 copy-done.6
  1443.9 2.2 reshape.211
  1446.2 5.3 fusion.78
  1451.5 2.4 fusion.53
  (78 shorter events, 8.9 us)
Async XLA Ops:
  7.2 329.9 %copy-start = (bf16[2,352,2048]{2,1,0:T(8,128)(2,1)S(1)}, bf16[2,352,2048]{2,1,0:T(8,128)(2,1)}, u32[]{:S(2)}) copy-start(bf16[2,352,2048]{2,1,0:T(8,128)(2,1)} %param.21) | copy-start | bytes 8650756
  7.2 312.0 %all-gather.3.cloned.1.call-start = ((), (), s32[]{:S(2)}) async-start(), calls=%async_computation.5 | async-start | bytes 26214400 | tf_op jit(solution)/shard_map/all_gather | solution.py:56
  8.9 5.3 copy-start.2
  33.2 10.9 copy-start.7
  190.1 532.1 %all-reduce.3.cloned.1.call-start = ((), (), s32[]{:S(2)}) async-start(), calls=%async_computation.8 | async-start | bytes 41943040
  365.7 0.7 copy-start.13
  728.6 6.8 copy-start.9
  728.6 121.3 %all-to-all-start.1 = ((bf16[8,160,2048]{2,1,0:T(8,128)(2,1)}), bf16[8,160,2048]{2,1,0:T(8,128)(2,1)}, u32[]{:S(2)}, u32[]{:S(2)}) async-start(bf16[8,160,2048]{2,1,0:T(8,128)(2,1)} %bitcast.153), calls=%async_computation.1 | async-start | bytes 10485760 | tf_op jit(solution)/shard_map/all_to_all | solution.py:72
  734.2 227.6 %all-gather.5.cloned.1.call-start = ((), (), s32[]{:S(2)}) async-start(), calls=%async_computation.6 | async-start | bytes 10485760 | tf_op jit(solution)/shard_map/all_gather | solution.py:84
  890.0 6.0 copy-start.3
  896.0 7.2 copy-start.8
  901.9 1.3 copy-start.4
  902.0 3.3 copy-start.10
  1001.4 144.2 %all-to-all-start.2 = ((bf16[3,32,256,128]{3,2,0,1:T(8,128)(2,1)}), bf16[3,32,256,128]{3,2,0,1:T(8,128)(2,1)}, u32[]{:S(2)}, u32[]{:S(2)}) async-start(bf16[3,32,256,128]{3,2,0,1:T(8,128)(2,1)} %pad_maximum_fusion), calls=%async_computation.2 | async-start | bytes 12582912 | tf_op jit(solution)/shard_map/all_to_all | solution.py:93
  1006.9 431.2 %reduce-scatter.5.cloned.1.call-start = ((), (), s32[]{:S(2)}) async-start(), calls=%async_computation.7 | async-start | bytes 10485760 | tf_op jit(solution)/shard_map/reduce_scatter | solution.py:121
  1360.2 1.6 copy-start.11
  1368.3 69.7 %copy-start.5 = (bf16[1,256,2,2048]{3,1,2,0:T(8,128)(2,1)S(1)}, bf16[1,256,2,2048]{3,1,2,0:T(8,128)(2,1)}, u32[]{:S(2)}) copy-start(bf16[1,256,2,2048]{3,1,2,0:T(8,128)(2,1)} %copy-done.4) | copy-start | bytes 6291460
  1442.6 1.3 copy-start.6
  1446.2 5.3 copy-start.12
  1446.2 8.6 copy-start.1
Sparse Core Ops, SparseCore 0:
  190.2 128.9 all-gather.2
  365.8 356.2 all-reduce.2
  905.4 56.4 all-gather.4
  1368.5 69.5 reduce-scatter.4
where the time goes:
time: 1470 us; the launch traced here: 1460 us
  waiting for transfers between devices  864 us (59%)
  blocking collectives  175 us (12%)
  matrix products  174 us (12%)
  other arithmetic  117 us (8%)
  local copies, waits for them, and re-layouts  106 us (7%)
    unnamed x5, waiting for transfers between devices  355 us
    all_to_all x1, waiting for transfers between devices, local(): lax.all_to_all(grouped, 'expert', split_axis=1, concat_axis=2, tiled=True)  139 us
    all_gather x1, waiting for transfers between devices, local(): piece = lax.all_gather(arrived, 'rep', axis=0, tiled=True)  129 us
    all_to_all x1, blocking collectives, local(): lax.all_to_all(outgoing, 'expert', split_axis=0, concat_axis=0, tiled=True)  123 us
    all_to_all x1, waiting for transfers between devices, local(): lax.all_to_all(results, 'expert', split_axis=0, concat_axis=0, tiled=True)  114 us
    reduce_scatter x1, waiting for transfers between devices, local(): lax.psum_scatter(jnp.einsum('rihse,hed->rsid', piece, teacher_out, prefer...  69.7 us
    dot_general x4, matrix products, attend(): jnp.einsum('pqk,pke->pqe', probs, value_rows, preferred_element_type=jnp....  59 us
    sub x4, other arithmetic, attend(): scores = scores - jnp.max(scores, axis=-1, keepdims=True)  56.7 us
  transfers between devices with their start and end apart: 6, of which 6 were waited for; matrix products, arithmetic and copies ran while one was open for 0% of the time, Pallas kernels for 0%

commit v1 on v0

--- a/solution.py
+++ b/solution.py
@@ -38,6 +38,12 @@
     exp_local = expert_gate.shape[0]
     expert_total = exp_local * n_owner
     capacity = max(2, tok_count * 10 // (4 * expert_total))
+    gate_full = lax.all_gather(expert_gate, "rep", axis=2, tiled=True)
+    up_full = lax.all_gather(expert_up, "rep", axis=2, tiled=True)
+    down_full = lax.all_gather(expert_down, "rep", axis=1, tiled=True)
+    qkv_full = lax.all_gather(teacher_qkv, "rep", axis=2, tiled=True)
+    qk_gain_full = lax.all_gather(qk_gain, "rep", axis=1, tiled=True)
+    out_full = lax.all_gather(teacher_out, "rep", axis=0, tiled=True)
     residual = tokens.reshape(tok_count, width).astype(jnp.float32)
     normed = norm_rows(residual, norm_gain).astype(jnp.bfloat16)
     chosen = expert_ids.reshape(2 * tok_count)
@@ -52,23 +58,24 @@
     )
     outgoing = outgoing.reshape(n_owner, exp_local * capacity, width)
     arrived = lax.all_to_all(outgoing, "expert", split_axis=0, concat_axis=0, tiled=True)
-    arrived = arrived.reshape(1, n_owner, exp_local, capacity, width)
-    piece = lax.all_gather(arrived, "rep", axis=0, tiled=True)
+    arrived = arrived.reshape(n_owner, exp_local, capacity, width)
     gate_part = jnp.einsum(
-        "rsjcd,jdf->rsjcf", piece, expert_gate, preferred_element_type=jnp.float32
+        "sjcd,jdf->sjcf", arrived, gate_full, preferred_element_type=jnp.float32
     )
-    up_part = jnp.einsum("rsjcd,jdf->rsjcf", piece, expert_up, preferred_element_type=jnp.float32)
+    up_part = jnp.einsum("sjcd,jdf->sjcf", arrived, up_full, preferred_element_type=jnp.float32)
     hidden = (jax.nn.silu(gate_part) * up_part).astype(jnp.bfloat16)
-    piece = hidden
-    produced = lax.psum_scatter(
-        jnp.einsum(
-            "rsjcf,jfd->rsjcd", piece, expert_down, preferred_element_type=jnp.float32
-        ).astype(jnp.bfloat16),
-        "rep",
-        scatter_dimension=0,
-        tiled=True,
-    )
-    results = produced.reshape(n_owner, exp_local * capacity, width)
+    ff_total = hidden.shape[-1]
+    ff_part = ff_total // n_replica
+    produced = jnp.zeros(arrived.shape, jnp.float32)
+    for part in range(n_replica):
+        low = part * ff_part
+        produced = produced + jnp.einsum(
+            "sjcf,jfd->sjcd",
+            hidden[..., low:low + ff_part],
+            down_full[:, low:low + ff_part],
+            preferred_element_type=jnp.float32,
+        ).astype(jnp.bfloat16).astype(jnp.float32)
+    results = produced.astype(jnp.bfloat16).reshape(n_owner, exp_local * capacity, width)
     returned = lax.all_to_all(results, "expert", split_axis=0, concat_axis=0, tiled=True).reshape(
         expert_total * capacity, width
     )
@@ -76,19 +83,16 @@
     combined = picked.reshape(tok_count, 2, width).sum(axis=1)
     mixed = (residual + combined).astype(jnp.bfloat16)
     teacher_in = norm_rows(mixed.astype(jnp.float32), teacher_gain).astype(jnp.bfloat16)
-    teacher_in = teacher_in.reshape(1, seq_dev, images, width)
-    heads_local = teacher_qkv.shape[2]
-    head_size = teacher_qkv.shape[3]
+    teacher_in = teacher_in.reshape(seq_dev, images, width)
+    heads_all = qkv_full.shape[2]
+    head_size = qkv_full.shape[3]
     projected = jnp.einsum(
-        "rsid,djhe->jrihse",
-        lax.all_gather(teacher_in, "rep", axis=0, tiled=True),
-        teacher_qkv,
-        preferred_element_type=jnp.float32,
+        "sid,djhe->jihse", teacher_in, qkv_full, preferred_element_type=jnp.float32
     )
-    query = norm_rows(projected[0], qk_gain[0][:, None, :])
-    keyed = norm_rows(projected[1], qk_gain[1][:, None, :])
+    query = norm_rows(projected[0], qk_gain_full[0][:, None, :])
+    keyed = norm_rows(projected[1], qk_gain_full[1][:, None, :])
     projected = jnp.stack([query, keyed, projected[2]]).astype(jnp.bfloat16)
-    pairs_all = n_replica * images * heads_local
+    pairs_all = images * heads_all
     grouped = projected.reshape(3, pairs_all, seq_dev, head_size)
     whole = lax.all_to_all(grouped, "expert", split_axis=1, concat_axis=2, tiled=True)
     pairs_local = whole.shape[1]
@@ -116,18 +120,19 @@
         lax.map(attend, query_blocks).transpose(1, 0, 2, 3).reshape(pairs_local, seq_len, head_size)
     )
     gathered_heads = lax.all_to_all(attended, "expert", split_axis=1, concat_axis=0, tiled=True)
-    gathered_heads = gathered_heads.reshape(n_replica, images, heads_local, seq_dev, head_size)
-    piece = gathered_heads
-    projected_out = lax.psum_scatter(
-        jnp.einsum(
-            "rihse,hed->rsid", piece, teacher_out, preferred_element_type=jnp.float32
-        ).astype(jnp.bfloat16),
-        "rep",
-        scatter_dimension=0,
-        tiled=True,
-    ).astype(jnp.float32)
+    gathered_heads = gathered_heads.reshape(images, heads_all, seq_dev, head_size)
+    heads_part = heads_all // n_replica
+    projected_out = jnp.zeros((seq_dev, images, width), jnp.float32)
+    for part in range(n_replica):
+        low = part * heads_part
+        projected_out = projected_out + jnp.einsum(
+            "ihse,hed->sid",
+            gathered_heads[:, low:low + heads_part],
+            out_full[low:low + heads_part],
+            preferred_element_type=jnp.float32,
+        ).astype(jnp.bfloat16).astype(jnp.float32)
     features = (
-        mixed.reshape(1, seq_dev, images, width).astype(jnp.float32) + projected_out
+        mixed.reshape(seq_dev, images, width).astype(jnp.float32) + projected_out
     ).astype(jnp.bfloat16)
     critic_hidden = jax.nn.gelu(
         jnp.dot(features.reshape(tok_count, width), critic_in, preferred_element_type=jnp.float32),
@@ -139,7 +144,7 @@
         precision=lax.Precision.HIGHEST,
         preferred_element_type=jnp.float32,
     )
-    return (features, logits.reshape(1, seq_dev, images))
+    return (features.reshape(1, seq_dev, images, width), logits.reshape(1, seq_dev, images))
 
 
 def solution(mesh):

time: 1470 us -> 918 us (0.62)
  waiting for transfers between devices: 864 us -> 276 us
  matrix products: 174 us -> 204 us
    unnamed x5, waiting for transfers between devices: 355 us -> 2.61 us
    all_gather x2 -> x5, waiting for transfers between devices: 186 us -> 26.5 us  [the longest x1 26.5 us: local(): down_full = lax.all_gather(expert_down, 'rep', axis=1, tiled=True)]
    reduce_scatter x1 -> x0, waiting for transfers between devices: 69.7 us -> none  [local(): lax.psum_scatter(jnp.einsum('rihse,hed->rsid', piece, teacher_out, prefer...]
    dot_general x4 -> x11, matrix products: 71 us -> 101 us  [the longest x4 28.8 us: local(): jnp.einsum('sjcf,jfd->sjcd', hidden[..., low:low + ff_part], down_full[:,...]
  transfers between devices with their start and end apart: 6 -> 7, of which waited for: 6 -> 3; matrix products, arithmetic and copies ran while one was open for 0% -> 37% of each run, Pallas kernels for 0% -> 0%
where the time goes in v1:
time: 918 us; the launch traced here: 909 us
  waiting for transfers between devices  276 us (30%)
  matrix products  204 us (22%)
  blocking collectives  181 us (20%)
  local copies, waits for them, and re-layouts  113 us (12%)
  other arithmetic  110 us (12%)
  between operations  14.5 us (2%)
  starting transfers between devices  11.1 us (1%)
    all_to_all x1, waiting for transfers between devices, local(): lax.all_to_all(grouped, 'expert', split_axis=1, concat_axis=2, tiled=True)  137 us
    all_to_all x1, blocking collectives, local(): lax.all_to_all(outgoing, 'expert', split_axis=0, concat_axis=0, tiled=True)  123 us
    all_to_all x1, waiting for transfers between devices, local(): lax.all_to_all(results, 'expert', split_axis=0, concat_axis=0, tiled=True)  110 us
    dot_general x4, matrix products, attend(): jnp.einsum('pqk,pke->pqe', probs, value_rows, preferred_element_type=jnp....  58.9 us
    sub x4, other arithmetic, attend(): scores = scores - jnp.max(scores, axis=-1, keepdims=True)  56.5 us
    all_to_all x1, blocking collectives, local(): lax.all_to_all(attended, 'expert', split_axis=1, concat_axis=0, tiled=True)  51.9 us
    dot_general x4, matrix products, attend(): jnp.einsum('pqe,pke->pqk', query_block, key_rows, preferred_element_type=...  36.5 us
    dot_general x4, matrix products, local(): jnp.einsum('sjcf,jfd->sjcd', hidden[..., low:low + ff_part], down_full[:,...  28.8 us
  transfers between devices with their start and end apart: 7, of which 3 were waited for; matrix products, arithmetic and copies ran while one was open for 37% of the time, Pallas kernels for 0%

profile of v1, /device:TPU:0, one launch (start us, length us, event | category | flops | bytes accessed | tf_op | source)
XLA Modules:
  0.0 908.9 jit_solution(2036090906852341895)
XLA Ops:
  9.4 10.8 %copy.124 = bf16[2048,3,4,128]{0,3,2,1:T(8,128)(2,1)} copy(bf16[2048,3,4,128]{3,2,1,0:T(4,128)(2,1)} %param.23) | data formatting | bytes 12582912 | tf_op args[8]
  21.7 4.5 reduce-window.6
  28.1 5.3 copy.115
  33.3 6.1 reshape.216
  41.1 4.6 scatter_custom_fusion.1
  45.8 4.3 scatter_custom_fusion
  50.3 2.6 multiply_convert_fusion.2
  52.9 6.1 gather_fusion
  59.0 3.7 select_select_fusion
  62.8 123.3 %all_to_all.40 = bf16[8,160,2048]{2,1,0:T(8,128)(2,1)} all-to-all(bf16[8,160,2048]{2,1,0:T(8,128)(2,1)S(1)} %select_select_fusion), channel_id=1, replica_groups=mesh['expert'=8,'rep'=4] {'expert'}, dimensions={0} | all-to-all | bytes 10485760 | tf_op jit(solution)/shard_map/all_to_all | solution.py:60
  186.1 14.7 %fusion.23 = f32[2,8,80,1408]{3,2,1,0:T(8,128)} fusion(bf16[2,2048,1408]{1,2,0:T(8,128)(2,1)} %all-gather.8.cloned.1.call-done, bf16[8,2,80,2048]{3,2,1,0:T(8,128)(2,1)} %bitcast.207), kind=kOutput, calls=%fused_computation.23 | convolution fusion | flops 7381975040 | bytes 23986176 | tf_op jit(solution)/shard_map/sjcd,jdf->sjcf/dot_general | solution.py:65
  200.8 16.6 %fusion.27 = bf16[8,2,80,1408]{3,2,0,1:T(8,128)(2,1)} fusion(f32[2,8,80,1408]{3,2,1,0:T(8,128)} %fusion.23, bf16[2,2048,1408]{1,2,0:T(8,128)(2,1)} %all-gather.6.cloned.1.call-done, bf16[8,2,80,2048]{3,2,1,0:T(8,128)(2,1)} %bitcast.208), kind=kOutput, calls=%fused_computation.31 | convolution fusion | flops 7392788480 | bytes 27590656 | tf_op jit(solution)/shard_map/sjcd,jdf->sjcf/dot_general | solution.py:62
  217.4 26.5 %all-gather.10.cloned.1.call-done = bf16[2,1408,2048]{2,1,0:T(8,128)(2,1)} async-done(((bf16[2,352,2048]{2,1,0:T(8,128)(2,1)}), bf16[2,1408,2048]{2,1,0:T(8,128)(2,1)}) %all-gather.10.cloned.1.call-update) | async-done | bytes 11534352 | tf_op jit(solution)/shard_map/all_gather | solution.py:43
  243.9 5.3 fusion.45
  249.2 6.8 fusion.46
  256.0 7.5 fusion.44
  263.5 9.2 %fusion.31 = bf16[8,2,80,2048]{3,2,0,1:T(8,128)(2,1)S(1)} fusion(bf16[2,8,80,2048]{3,2,1,0:T(8,128)(2,1)} %fusion.44, bf16[2,8,80,2048]{3,2,1,0:T(8,128)(2,1)S(1)} %fusion.45, bf16[2,8,80,2048]{3,2,1,0:T(8,128)(2,1)} %fusion.46, bf16[2,1408,2048]{2,1,0:T(8,128)(2,1)} %all-gather.10.cloned.1.call-done, bf16[8,2,80,1408]{3,2,0,1:T(8,128)(2,1)S(1)} %copy-done.13), kind=kOutput, calls=%fused_computation.40 | convolution fusion | flops 1869086720 | bytes 24838144 | tf_op jit(solution)/shard_map/sjcf,jfd->sjcd/dot_general | solution.py:72
  272.7 2.9 copy.119
  275.6 5.8 all-to-all-start.1
  282.5 5.4 all_gather.22
  287.9 109.6 %all-to-all-done.1 = bf16[8,160,2048]{2,1,0:T(8,128)(2,1)} async-done(((bf16[8,160,2048]{2,1,0:T(8,128)(2,1)}), bf16[8,160,2048]{2,1,0:T(8,128)(2,1)}, u32[]{:S(2)}, u32[]{:S(2)}) %all-to-all-start.1) | async-done | bytes 5242912 | tf_op jit(solution)/shard_map/all_to_all | solution.py:79
  397.6 12.3 %gather_fusion.1 = bf16[1024,2048]{1,0:T(8,128)(2,1)} fusion(bf16[1280,2048]{1,0:T(8,128)(2,1)} %bitcast.25, s32[1024]{0:T(1024)S(1)} %broadcast_clamp_fusion), kind=kCustom, calls=%fused_computation.1 | custom fusion | bytes 8392704 | tf_op jit(solution)/shard_map/jit(_take)/gather | solution.py:82
  409.8 7.6 gather.15
  417.5 20.7 %multiply_reduce_fusion.1 = f32[512,2048]{1,0:T(8,128)} fusion(bf16[512,2,2048]{2,1,0:T(2,128)(2,1)} %gather.15, pred[512,2]{1,0:T(8,128)(4,1)S(1)} %copy.113, f32[512,2]{1,0:T(8,128)S(1)} %bitcast.215), kind=kLoop, calls=%fused_computation.28 | loop fusion | flops 7340032 | bytes 8393728 | tf_op jit(solution)/shard_map/reduce_sum | solution.py:83
  438.1 5.8 reduce_sum.77
  444.0 6.0 reduce_sum.76
  450.0 5.6 multiply_reduce_fusion.4
  455.6 26.7 %fusion.36 = f32[3,2,16,256,128]{3,4,2,0,1:T(8,128)} fusion(bf16[2048,3,16,128]{0,3,2,1:T(8,128)(2,1)} %all-gather.12.cloned.1.call-done, f32[2048]{0:T(1024)S(1)} %copy-done.12, f32[256,2]{0,1:T(2,128)S(1)} %add_rsqrt_fusion.2, f32[256,2,2048]{2,1,0:T(2,128)} %reduce_sum.76, bf16[1,256,2,2048]{3,2,1,0:T(2,128)(2,1)S(1)} %copy-done.2), kind=kOutput, calls=%fused_computation.44 | convolution fusion | flops 12892241920 | bytes 44050432 | tf_op jit(solution)/shard_map/sid,djhe->jihse/dot_general | solution.py:89
  482.3 4.8 multiply_reduce_fusion.3
  487.1 3.2 slice.165
  490.6 2.7 multiply_convert_fusion.1
  493.2 4.0 copy.126
  497.3 4.1 copy.127
  501.4 2.8 copy.128
  504.2 6.4 pad_maximum_fusion
  510.6 5.1 all-to-all-start.2
  516.4 137.0 %all-to-all-done.2 = bf16[3,32,256,128]{3,2,0,1:T(8,128)(2,1)} async-done(((bf16[3,32,256,128]{3,2,0,1:T(8,128)(2,1)}), bf16[3,32,256,128]{3,2,0,1:T(8,128)(2,1)}, u32[]{:S(2)}, u32[]{:S(2)}) %all-to-all-start.2) | async-done | bytes 6291488 | tf_op jit(solution)/shard_map/all_to_all | solution.py:97
  653.4 3.2 copy.129
  657.0 1.6 copy.130
  658.8 1.5 copy.132
  660.3 152.0 %while.10 = (s32[]{:T(128)}, bf16[4,4,512,128]{3,2,0,1:T(8,128)(2,1)}, bf16[4,4,512,128]{3,2,0,1:T(8,128)(2,1)}, bf16[4,2048,128]{2,1,0:T(8,128)(2,1)S(1)}, bf16[4,2048,128]{2,1,0:T(8,128)(2,1)}, /*index=5*/s32[]{:T(128)}) while((s32[]{:T(128)}, bf16[4,4,512,128]{3,2,0,1:T(8,128)(2,1)}, bf16[4,4,512,128]{3,2,0,1:T(8,128)(2,1)}, ...), condition=%wide.region_13.14_spmd, body=%wide.region_10.13_spmd.sunk | while | flops 2185500672 | bytes 72369224 | solution.py:120
  660.3 9.1 %fusion.110 = f32[4,512,2048]{2,1,0:T(8,128)} fusion(bf16[4,2048,128]{2,1,0:T(8,128)(2,1)S(1)} %get-tuple-element.127, bf16[4,4,512,128]{3,2,0,1:T(8,128)(2,1)} %get-tuple-element.126, s32[]{:T(128)} %get-tuple-element.118), kind=kOutput, calls=%fused_computation.14.clone.1 | convolution fusion | flops 1073741824 | bytes 19399168 | tf_op jit(solution)/shard_map/while/body/eval_jaxpr/pqe,pke->pqk/dot_general | solution.py:106
  669.4 14.1 %fusion.111 = f32[4,512]{1,0:T(4,128)S(1)} fusion(f32[4,512,2048]{2,1,0:T(8,128)} %fusion.110), kind=kOutput, calls=%fused_computation.135.clone.1 | output fusion | flops 16779264 | bytes 16785408 | tf_op jit(solution)/shard_map/while/body/eval_jaxpr/sub | solution.py:109
  683.6 14.7 %fusion.112 = bf16[4,4,512,128]{3,2,0,1:T(8,128)(2,1)} fusion(bf16[4,4,512,128]{3,2,0,1:T(8,128)(2,1)} %get-tuple-element.119, s32[]{:T(128)} %get-tuple-element.118, bf16[4,2048,128]{2,1,0:T(8,128)(2,1)} %get-tuple-element.128, f32[4,512]{1,0:T(4,128)S(1)} %fusion.111, f32[4,512,2048]{2,1,0:T(8,128)} %fusion.110), kind=kOutput, calls=%fused_computation.13.clone.1 | convolution fusion | flops 1094979584 | bytes 36184576 | tf_op jit(solution)/shard_map/while/body/eval_jaxpr/pqk,pke->pqe/dot_general | solution.py:112
  698.3 9.1 %fusion.110 = f32[4,512,2048]{2,1,0:T(8,128)} fusion(bf16[4,2048,128]{2,1,0:T(8,128)(2,1)S(1)} %get-tuple-element.127, bf16[4,4,512,128]{3,2,0,1:T(8,128)(2,1)} %get-tuple-element.126, s32[]{:T(128)} %get-tuple-element.118), kind=kOutput, calls=%fused_computation.14.clone.1 | convolution fusion | flops 1073741824 | bytes 19399168 | tf_op jit(solution)/shard_map/while/body/eval_jaxpr/pqe,pke->pqk/dot_general | solution.py:106
  707.4 14.1 %fusion.111 = f32[4,512]{1,0:T(4,128)S(1)} fusion(f32[4,512,2048]{2,1,0:T(8,128)} %fusion.110), kind=kOutput, calls=%fused_computation.135.clone.1 | output fusion | flops 16779264 | bytes 16785408 | tf_op jit(solution)/shard_map/while/body/eval_jaxpr/sub | solution.py:109
  721.6 14.7 %fusion.112 = bf16[4,4,512,128]{3,2,0,1:T(8,128)(2,1)} fusion(bf16[4,4,512,128]{3,2,0,1:T(8,128)(2,1)} %get-tuple-element.119, s32[]{:T(128)} %get-tuple-element.118, bf16[4,2048,128]{2,1,0:T(8,128)(2,1)} %get-tuple-element.128, f32[4,512]{1,0:T(4,128)S(1)} %fusion.111, f32[4,512,2048]{2,1,0:T(8,128)} %fusion.110), kind=kOutput, calls=%fused_computation.13.clone.1 | convolution fusion | flops 1094979584 | bytes 36184576 | tf_op jit(solution)/shard_map/while/body/eval_jaxpr/pqk,pke->pqe/dot_general | solution.py:112
  736.3 9.1 %fusion.110 = f32[4,512,2048]{2,1,0:T(8,128)} fusion(bf16[4,2048,128]{2,1,0:T(8,128)(2,1)S(1)} %get-tuple-element.127, bf16[4,4,512,128]{3,2,0,1:T(8,128)(2,1)} %get-tuple-element.126, s32[]{:T(128)} %get-tuple-element.118), kind=kOutput, calls=%fused_computation.14.clone.1 | convolution fusion | flops 1073741824 | bytes 19399168 | tf_op jit(solution)/shard_map/while/body/eval_jaxpr/pqe,pke->pqk/dot_general | solution.py:106
  745.4 14.1 %fusion.111 = f32[4,512]{1,0:T(4,128)S(1)} fusion(f32[4,512,2048]{2,1,0:T(8,128)} %fusion.110), kind=kOutput, calls=%fused_computation.135.clone.1 | output fusion | flops 16779264 | bytes 16785408 | tf_op jit(solution)/shard_map/while/body/eval_jaxpr/sub | solution.py:109
  759.6 14.7 %fusion.112 = bf16[4,4,512,128]{3,2,0,1:T(8,128)(2,1)} fusion(bf16[4,4,512,128]{3,2,0,1:T(8,128)(2,1)} %get-tuple-element.119, s32[]{:T(128)} %get-tuple-element.118, bf16[4,2048,128]{2,1,0:T(8,128)(2,1)} %get-tuple-element.128, f32[4,512]{1,0:T(4,128)S(1)} %fusion.111, f32[4,512,2048]{2,1,0:T(8,128)} %fusion.110), kind=kOutput, calls=%fused_computation.13.clone.1 | convolution fusion | flops 1094979584 | bytes 36184576 | tf_op jit(solution)/shard_map/while/body/eval_jaxpr/pqk,pke->pqe/dot_general | solution.py:112
  774.3 9.1 %fusion.110 = f32[4,512,2048]{2,1,0:T(8,128)} fusion(bf16[4,2048,128]{2,1,0:T(8,128)(2,1)S(1)} %get-tuple-element.127, bf16[4,4,512,128]{3,2,0,1:T(8,128)(2,1)} %get-tuple-element.126, s32[]{:T(128)} %get-tuple-element.118), kind=kOutput, calls=%fused_computation.14.clone.1 | convolution fusion | flops 1073741824 | bytes 19399168 | tf_op jit(solution)/shard_map/while/body/eval_jaxpr/pqe,pke->pqk/dot_general | solution.py:106
  783.4 14.1 %fusion.111 = f32[4,512]{1,0:T(4,128)S(1)} fusion(f32[4,512,2048]{2,1,0:T(8,128)} %fusion.110), kind=kOutput, calls=%fused_computation.135.clone.1 | output fusion | flops 16779264 | bytes 16785408 | tf_op jit(solution)/shard_map/while/body/eval_jaxpr/sub | solution.py:109
  797.6 14.7 %fusion.112 = bf16[4,4,512,128]{3,2,0,1:T(8,128)(2,1)} fusion(bf16[4,4,512,128]{3,2,0,1:T(8,128)(2,1)} %get-tuple-element.119, s32[]{:T(128)} %get-tuple-element.118, bf16[4,2048,128]{2,1,0:T(8,128)(2,1)} %get-tuple-element.128, f32[4,512]{1,0:T(4,128)S(1)} %fusion.111, f32[4,512,2048]{2,1,0:T(8,128)} %fusion.110), kind=kOutput, calls=%fused_computation.13.clone.1 | convolution fusion | flops 1094979584 | bytes 36184576 | tf_op jit(solution)/shard_map/while/body/eval_jaxpr/pqk,pke->pqe/dot_general | solution.py:112
  812.3 3.4 copy.135
  815.8 51.9 %all_to_all.41 = bf16[4,2048,128]{2,0,1:T(4,128)(2,1)S(1)} all-to-all(bf16[4,2048,128]{2,0,1:T(4,128)(2,1)S(1)} %copy.135), channel_id=1, replica_groups=mesh['expert'=8,'rep'=4] {'expert'}, dimensions={1} | all-to-all | bytes 4194304 | tf_op jit(solution)/shard_map/all_to_all | solution.py:122
  868.2 3.6 bitcast_convert_fusion.1
  871.8 3.0 bitcast_convert_fusion.2
  874.9 1.3 bitcast_convert_fusion
  876.5 6.0 fusion.41
  882.5 3.5 copy.138
  886.0 4.3 reshape.213
  890.3 5.2 fusion.93
  895.4 2.4 fusion.62
  898.7 3.5 copy.139
  (88 shorter events, 11.3 us)
Async XLA Ops:
  7.2 888.3 %copy-start = (f32[1024]{0:T(1024)S(1)}, f32[1024]{0:T(1024)}, u32[]{:S(2)}) copy-start(f32[1024]{0:T(1024)} %param.27) | copy-start | bytes 12292
  7.2 178.9 %all-gather.8.cloned.1.call-start = ((), (), s32[]{:S(2)}) async-start(), calls=%async_computation.5 | async-start | bytes 14417920 | tf_op jit(solution)/shard_map/all_gather | solution.py:42
  7.9 192.9 %all-gather.6.cloned.1.call-start = ((), (), s32[]{:S(2)}) async-start(), calls=%async_computation.4 | async-start | bytes 14417920 | tf_op jit(solution)/shard_map/all_gather | solution.py:41
  8.7 235.2 %all-gather.10.cloned.1.call-start = ((), (), s32[]{:S(2)}) async-start(), calls=%async_computation.6 | async-start | bytes 14417920 | tf_op jit(solution)/shard_map/all_gather | solution.py:43
  9.4 446.2 %all-gather.12.cloned.1.call-start = ((), (), s32[]{:S(2)}) async-start(), calls=%async_computation.7 | async-start | bytes 31457280 | tf_op jit(solution)/shard_map/all_gather | solution.py:44
  20.2 0.7 copy-start.8
  20.2 6.9 copy-start.1
  33.3 16.9 %copy-start.9 = (f32[2048]{0:T(1024)S(1)}, f32[2048]{0:T(1024)}, u32[]{:S(2)}) copy-start(f32[2048]{0:T(1024)} %param.18) | copy-start | bytes 24580
  243.9 5.3 copy-start.13
  275.6 6.7 copy-start.10
  275.6 6.9 copy-start.11
  275.6 121.9 %all-to-all-start.1 = ((bf16[8,160,2048]{2,1,0:T(8,128)(2,1)}), bf16[8,160,2048]{2,1,0:T(8,128)(2,1)}, u32[]{:S(2)}, u32[]{:S(2)}) async-start(bf16[8,160,2048]{2,1,0:T(8,128)(2,1)} %bitcast.200), calls=%async_computation.1 | async-start | bytes 10485760 | tf_op jit(solution)/shard_map/all_to_all | solution.py:79
  444.0 6.0 copy-start.2
  450.0 5.7 copy-start.12
  482.3 8.3 copy-start.4
  510.6 142.7 %all-to-all-start.2 = ((bf16[3,32,256,128]{3,2,0,1:T(8,128)(2,1)}), bf16[3,32,256,128]{3,2,0,1:T(8,128)(2,1)}, u32[]{:S(2)}, u32[]{:S(2)}) async-start(bf16[3,32,256,128]{3,2,0,1:T(8,128)(2,1)} %pad_maximum_fusion), calls=%async_computation.2 | async-start | bytes 12582912 | tf_op jit(solution)/shard_map/all_to_all | solution.py:97
  515.8 352.4 %all-gather.14.cloned.1.call-start = ((), (), s32[]{:S(2)}) async-start(), calls=%async_computation.8 | async-start | bytes 10485760 | tf_op jit(solution)/shard_map/all_gather | solution.py:46
  868.1 6.7 copy-start.6
  868.2 6.7 copy-start.7
  871.8 4.4 copy-start.5
  874.9 1.6 copy-start.3
Sparse Core Ops, SparseCore 0:
  9.5 78.8 all-gather.7
  90.0 76.1 all-gather.5
  167.7 76.1 all-gather.9
  245.3 154.8 all-gather.11
  517.8 59.0 all-gather.13

commit v2 on v1

--- a/solution.py
+++ b/solution.py
@@ -1,6 +1,9 @@
+import functools
+
 import jax
 import jax.numpy as jnp
 from jax import lax
+from jax.experimental import pallas as pl
 from jax.sharding import PartitionSpec as P
 
 
@@ -12,6 +15,38 @@
     onehot = (chosen[..., None] == jnp.arange(count, dtype=jnp.int32)).astype(jnp.int32)
     before = jnp.cumsum(onehot, axis=-2) - onehot
     return jnp.sum(before * onehot, axis=-1)
+
+
+def attention_kernel(query_ref, key_ref, value_ref, out_ref, *, scale):
+    scores = lax.dot_general(
+        query_ref[...],
+        key_ref[...],
+        (((1,), (1,)), ((), ())),
+        preferred_element_type=jnp.float32,
+    ) * scale
+    scores = scores - jnp.max(scores, axis=-1, keepdims=True)
+    weights = jnp.exp(scores)
+    probs = (weights / jnp.sum(weights, axis=-1, keepdims=True)).astype(jnp.bfloat16)
+    out_ref[...] = jnp.dot(probs, value_ref[...], preferred_element_type=jnp.float32).astype(
+        out_ref.dtype
+    )
+
+
+def attention(whole, scale, interpret=False):
+    _, pairs, seq_len, head_size = whole.shape
+    block = min(256, seq_len)
+    return pl.pallas_call(
+        functools.partial(attention_kernel, scale=scale),
+        grid=(pairs, seq_len // block),
+        in_specs=[
+            pl.BlockSpec((None, None, block, head_size), lambda p, i: (0, p, i, 0)),
+            pl.BlockSpec((None, None, seq_len, head_size), lambda p, i: (1, p, 0, 0)),
+            pl.BlockSpec((None, None, seq_len, head_size), lambda p, i: (2, p, 0, 0)),
+        ],
+        out_specs=pl.BlockSpec((None, block, head_size), lambda p, i: (p, i, 0)),
+        out_shape=jax.ShapeDtypeStruct((pairs, seq_len, head_size), whole.dtype),
+        interpret=interpret,
+    )(whole, whole, whole)
 
 
 def local(
@@ -97,28 +132,7 @@
     whole = lax.all_to_all(grouped, "expert", split_axis=1, concat_axis=2, tiled=True)
     pairs_local = whole.shape[1]
     seq_len = whole.shape[2]
-    block = min(512, seq_len)
-    blocks_count = seq_len // block
-    key_rows = whole[1]
-    value_rows = whole[2]
-
-    def attend(query_block):
-        scores = jnp.einsum(
-            "pqe,pke->pqk", query_block, key_rows, preferred_element_type=jnp.float32
-        ) * head_size ** (-0.5)
-        scores = scores - jnp.max(scores, axis=-1, keepdims=True)
-        weights = jnp.exp(scores)
-        probs = (weights / jnp.sum(weights, axis=-1, keepdims=True)).astype(jnp.bfloat16)
-        return jnp.einsum(
-            "pqk,pke->pqe", probs, value_rows, preferred_element_type=jnp.float32
-        ).astype(jnp.bfloat16)
-
-    query_blocks = (
-        whole[0].reshape(pairs_local, blocks_count, block, head_size).transpose(1, 0, 2, 3)
-    )
-    attended = (
-        lax.map(attend, query_blocks).transpose(1, 0, 2, 3).reshape(pairs_local, seq_len, head_size)
-    )
+    attended = attention(whole, head_size ** (-0.5))
     gathered_heads = lax.all_to_all(attended, "expert", split_axis=1, concat_axis=0, tiled=True)
     gathered_heads = gathered_heads.reshape(images, heads_all, seq_dev, head_size)
     heads_part = heads_all // n_replica

time: 918 us -> 810 us (0.88)
  matrix products: 204 us -> 107 us
  other arithmetic: 110 us -> 53.4 us
  Pallas kernels: 0 us -> 44.7 us
    dot_general x8 -> x0, matrix products: 95.5 us -> none  [the longest x4 58.9 us: attend(): jnp.einsum('pqk,pke->pqe', probs, value_rows, preferred_element_type=jnp....]
    sub x4 -> x0, other arithmetic: 56.5 us -> none  [attend(): scores = scores - jnp.max(scores, axis=-1, keepdims=True)]
    pallas_call x0 -> x1, Pallas kernels: none -> 44.7 us  [attention(): pl.pallas_call(functools.partial(attention_kernel, scale=scale), grid=(pa...]
  transfers between devices with their start and end apart: 7 -> 7, of which waited for: 3 -> 3; matrix products, arithmetic and copies ran while one was open for 37% -> 23% of each run, Pallas kernels for 0% -> 6%
where the time goes in v2:
time: 810 us; the launch traced here: 802 us
  waiting for transfers between devices  276 us (34%)
  blocking collectives  180 us (22%)
  local copies, waits for them, and re-layouts  115 us (14%)
  matrix products  107 us (13%)
  other arithmetic  53.4 us (7%)
  Pallas kernels  44.7 us (6%)
  between operations  14.4 us (2%)
  starting transfers between devices  10.9 us (1%)
    all_to_all x1, waiting for transfers between devices, local(): lax.all_to_all(grouped, 'expert', split_axis=1, concat_axis=2, tiled=True)  137 us
    all_to_all x1, blocking collectives, local(): lax.all_to_all(outgoing, 'expert', split_axis=0, concat_axis=0, tiled=True)  123 us
    all_to_all x1, waiting for transfers between devices, local(): lax.all_to_all(results, 'expert', split_axis=0, concat_axis=0, tiled=True)  110 us
    all_to_all x1, blocking collectives, local(): lax.all_to_all(attended, 'expert', split_axis=1, concat_axis=0, tiled=True)  51.8 us
    pallas_call x1, Pallas kernels, attention(): pl.pallas_call(functools.partial(attention_kernel, scale=scale), grid=(pa...  44.7 us
    dot_general x4, matrix products, local(): jnp.einsum('sjcf,jfd->sjcd', hidden[..., low:low + ff_part], down_full[:,...  28.8 us
    dot_general x1, matrix products, local(): jnp.einsum('sid,djhe->jihse', teacher_in, qkv_full, preferred_element_typ...  26.9 us
    all_gather x1, waiting for transfers between devices, local(): down_full = lax.all_gather(expert_down, 'rep', axis=1, tiled=True)  26.6 us
  transfers between devices with their start and end apart: 7, of which 3 were waited for; matrix products, arithmetic and copies ran while one was open for 23% of the time, Pallas kernels for 6%

profile of v2, /device:TPU:0, one launch (start us, length us, event | category | flops | bytes accessed | tf_op | source)
XLA Modules:
  0.0 801.7 jit_solution(4989749399852048809)
XLA Ops:
  7.2 0.7 all-gather.8.cloned.1.call-update
  8.0 0.7 all-gather.6.cloned.1.call-update
  8.7 0.7 all-gather.10.cloned.1.call-update
  9.4 10.8 %copy.66 = bf16[2048,3,4,128]{0,3,2,1:T(8,128)(2,1)} copy(bf16[2048,3,4,128]{3,2,1,0:T(4,128)(2,1)} %param.21) | data formatting | bytes 12582912 | tf_op args[8]
  20.2 0.7 copy-done.9
  21.1 0.3 eq.26
  21.4 0.3 reshape.194
  21.7 4.5 reduce-window.6
  26.8 0.3 mul.158
  27.1 0.9 copy_convert_fusion
  28.1 5.3 copy.57
  33.3 6.1 reshape.204
  39.5 1.2 multiply_reduce_fusion.4
  41.1 4.5 scatter_custom_fusion.1
  45.8 4.3 scatter_custom_fusion
  50.2 2.6 multiply_convert_fusion.2
  52.8 6.2 gather_fusion
  59.0 3.7 select_select_fusion
  62.7 123.2 %all_to_all.43 = bf16[8,160,2048]{2,1,0:T(8,128)(2,1)} all-to-all(bf16[8,160,2048]{2,1,0:T(8,128)(2,1)S(1)} %select_select_fusion), channel_id=1, replica_groups=mesh['expert'=8,'rep'=4] {'expert'}, dimensions={0} | all-to-all | bytes 10485760 | tf_op jit(solution)/shard_map/all_to_all | solution.py:95
  185.9 14.8 %fusion.2 = f32[2,8,80,1408]{3,2,1,0:T(8,128)} fusion(bf16[2,2048,1408]{1,2,0:T(8,128)(2,1)} %all-gather.8.cloned.1.call-done, bf16[8,2,80,2048]{3,2,1,0:T(8,128)(2,1)} %bitcast.165), kind=kOutput, calls=%fused_computation.6 | convolution fusion | flops 7381975040 | bytes 23986176 | tf_op jit(solution)/shard_map/sjcd,jdf->sjcf/dot_general | solution.py:100
  200.7 16.5 %fusion.6 = bf16[8,2,80,1408]{3,2,0,1:T(8,128)(2,1)} fusion(f32[2,8,80,1408]{3,2,1,0:T(8,128)} %fusion.2, bf16[2,2048,1408]{1,2,0:T(8,128)(2,1)} %all-gather.6.cloned.1.call-done, bf16[8,2,80,2048]{3,2,1,0:T(8,128)(2,1)} %bitcast.166), kind=kOutput, calls=%fused_computation.14 | convolution fusion | flops 7392788480 | bytes 27590656 | tf_op jit(solution)/shard_map/sjcd,jdf->sjcf/dot_general | solution.py:97
  217.2 26.6 %all-gather.10.cloned.1.call-done = bf16[2,1408,2048]{2,1,0:T(8,128)(2,1)} async-done(((bf16[2,352,2048]{2,1,0:T(8,128)(2,1)}), bf16[2,1408,2048]{2,1,0:T(8,128)(2,1)}) %all-gather.10.cloned.1.call-update) | async-done | bytes 11534352 | tf_op jit(solution)/shard_map/all_gather | solution.py:78
  243.9 5.3 fusion.24
  249.2 6.8 fusion.25
  256.0 7.5 fusion.23
  263.5 9.2 %fusion.10 = bf16[8,2,80,2048]{3,2,0,1:T(8,128)(2,1)S(1)} fusion(bf16[2,8,80,2048]{3,2,1,0:T(8,128)(2,1)} %fusion.23, bf16[2,8,80,2048]{3,2,1,0:T(8,128)(2,1)S(1)} %fusion.24, bf16[2,8,80,2048]{3,2,1,0:T(8,128)(2,1)} %fusion.25, bf16[2,1408,2048]{2,1,0:T(8,128)(2,1)} %all-gather.10.cloned.1.call-done, bf16[8,2,80,1408]{3,2,0,1:T(8,128)(2,1)S(1)} %copy-done.14), kind=kOutput, calls=%fused_computation.23 | convolution fusion | flops 1869086720 | bytes 24838144 | tf_op jit(solution)/shard_map/sjcf,jfd->sjcd/dot_general | solution.py:107
  272.7 2.9 copy.61
  275.6 5.8 all-to-all-start.1
  282.5 5.4 all_gather.22
  288.0 109.6 %all-to-all-done.1 = bf16[8,160,2048]{2,1,0:T(8,128)(2,1)} async-done(((bf16[8,160,2048]{2,1,0:T(8,128)(2,1)}), bf16[8,160,2048]{2,1,0:T(8,128)(2,1)}, u32[]{:S(2)}, u32[]{:S(2)}) %all-to-all-start.1) | async-done | bytes 5242912 | tf_op jit(solution)/shard_map/all_to_all | solution.py:114
  397.6 12.3 %gather_fusion.1 = bf16[1024,2048]{1,0:T(8,128)(2,1)} fusion(bf16[1280,2048]{1,0:T(8,128)(2,1)} %bitcast.23, s32[1024]{0:T(1024)S(1)} %broadcast_clamp_fusion), kind=kCustom, calls=%fused_computation.1 | custom fusion | bytes 8392704 | tf_op jit(solution)/shard_map/jit(_take)/gather | solution.py:117
  409.9 7.7 gather.15
  417.5 20.7 %multiply_reduce_fusion = f32[512,2048]{1,0:T(8,128)} fusion(bf16[512,2,2048]{2,1,0:T(2,128)(2,1)} %gather.15, pred[512,2]{1,0:T(8,128)(4,1)S(1)} %copy.55, f32[512,2]{1,0:T(8,128)S(1)} %bitcast.171), kind=kLoop, calls=%fused_computation.11 | loop fusion | flops 7340032 | bytes 8393728 | tf_op jit(solution)/shard_map/reduce_sum | solution.py:118
  438.2 5.8 reduce_sum.68
  444.1 6.0 reduce_sum.67
  450.1 5.6 multiply_reduce_fusion.3
  455.7 26.9 %fusion.15 = f32[3,2,16,256,128]{3,4,2,0,1:T(8,128)} fusion(bf16[2048,3,16,128]{0,3,2,1:T(8,128)(2,1)} %all-gather.12.cloned.1.call-done, f32[2048]{0:T(1024)S(1)} %copy-done.13, f32[256,2]{0,1:T(2,128)S(1)} %add_rsqrt_fusion.2, f32[256,2,2048]{2,1,0:T(2,128)} %reduce_sum.67, bf16[1,256,2,2048]{3,2,1,0:T(2,128)(2,1)S(1)} %copy-done.2), kind=kOutput, calls=%fused_computation.27 | convolution fusion | flops 12892241920 | bytes 44050432 | tf_op jit(solution)/shard_map/sid,djhe->jihse/dot_general | solution.py:124
  482.6 4.8 multiply_reduce_fusion.2
  487.4 4.6 slice.147
  492.0 2.7 multiply_convert_fusion.1
  494.7 4.1 copy.68
  498.8 4.1 copy.69
  502.8 4.1 copy.70
  506.9 6.4 pad_maximum_fusion
  513.3 4.9 all-to-all-start.2
  518.3 0.5 all-gather.14.cloned.1.call-update
  518.8 137.0 %all-to-all-done.2 = bf16[3,32,256,128]{3,2,0,1:T(8,128)(2,1)} async-done(((bf16[3,32,256,128]{3,2,0,1:T(8,128)(2,1)}), bf16[3,32,256,128]{3,2,0,1:T(8,128)(2,1)}, u32[]{:S(2)}, u32[]{:S(2)}) %all-to-all-start.2) | async-done | bytes 6291488 | tf_op jit(solution)/shard_map/all_to_all | solution.py:132
  655.8 6.3 copy.72
  662.1 44.7 %shard_map.140 = bf16[4,2048,128]{2,1,0:T(8,128)(2,1)} custom-call(bf16[3,4,2048,128]{3,2,1,0:T(8,128)(2,1)} %bitcast.155, bf16[3,4,2048,128]{3,2,1,0:T(8,128)(2,1)} %bitcast.156, bf16[3,4,2048,128]{3,2,1,0:T(8,128)(2,1)} %bitcast.157), custom_call_target="tpu_custom_call" | custom-call | tf_op jit(solution)/shard_map/pallas_call | solution.py:38
  706.8 3.4 copy.73
  710.2 51.8 %all_to_all.44 = bf16[4,2048,128]{2,0,1:T(4,128)(2,1)S(1)} all-to-all(bf16[4,2048,128]{2,0,1:T(4,128)(2,1)S(1)} %copy.73), channel_id=1, replica_groups=mesh['expert'=8,'rep'=4] {'expert'}, dimensions={1} | all-to-all | bytes 4194304 | tf_op jit(solution)/shard_map/all_to_all | solution.py:136
  762.0 1.8 copy.74
  763.8 3.2 bitcast_convert_fusion
  767.0 3.5 bitcast_convert_fusion.1
  770.6 1.3 bitcast_convert_fusion.2
  771.8 0.9 copy-done.6
  772.7 4.4 fusion.20
  777.2 1.3 copy-done.4
  778.5 2.2 copy.75
  780.6 2.4 reshape.201
  783.1 5.2 fusion.64
  788.2 2.4 fusion.37
  790.9 0.7 copy.77
  791.5 3.5 copy.76
  (72 shorter events, 2.8 us)
Async XLA Ops:
  7.2 781.1 %copy-start = (f32[1024]{0:T(1024)S(1)}, f32[1024]{0:T(1024)}, u32[]{:S(2)}) copy-start(f32[1024]{0:T(1024)} %param.25) | copy-start | bytes 12292
  7.2 178.8 %all-gather.8.cloned.1.call-start = ((), (), s32[]{:S(2)}) async-start(), calls=%async_computation.5 | async-start | bytes 14417920 | tf_op jit(solution)/shard_map/all_gather | solution.py:77
  7.9 192.8 %all-gather.6.cloned.1.call-start = ((), (), s32[]{:S(2)}) async-start(), calls=%async_computation.4 | async-start | bytes 14417920 | tf_op jit(solution)/shard_map/all_gather | solution.py:76
  8.7 235.2 %all-gather.10.cloned.1.call-start = ((), (), s32[]{:S(2)}) async-start(), calls=%async_computation.6 | async-start | bytes 14417920 | tf_op jit(solution)/shard_map/all_gather | solution.py:78
  9.4 446.3 %all-gather.12.cloned.1.call-start = ((), (), s32[]{:S(2)}) async-start(), calls=%async_computation.7 | async-start | bytes 31457280 | tf_op jit(solution)/shard_map/all_gather | solution.py:79
  20.2 0.7 copy-start.9
  20.2 6.9 copy-start.1
  33.3 16.9 %copy-start.10 = (f32[2048]{0:T(1024)S(1)}, f32[2048]{0:T(1024)}, u32[]{:S(2)}) copy-start(f32[2048]{0:T(1024)} %param.16) | copy-start | bytes 24580
  243.9 5.3 copy-start.14
  275.6 6.7 copy-start.11
  275.6 6.9 copy-start.12
  275.6 121.9 %all-to-all-start.1 = ((bf16[8,160,2048]{2,1,0:T(8,128)(2,1)}), bf16[8,160,2048]{2,1,0:T(8,128)(2,1)}, u32[]{:S(2)}, u32[]{:S(2)}) async-start(bf16[8,160,2048]{2,1,0:T(8,128)(2,1)} %bitcast.159), calls=%async_computation.1 | async-start | bytes 10485760 | tf_op jit(solution)/shard_map/all_to_all | solution.py:114
  444.1 6.0 copy-start.2
  450.1 5.7 copy-start.13
  482.6 9.4 %copy-start.3 = (f32[3,2,16,256,128]{3,4,2,0,1:T(8,128)S(1)}, f32[3,2,16,256,128]{3,4,2,0,1:T(8,128)}, u32[]{:S(2)}) copy-start(f32[3,2,16,256,128]{3,4,2,0,1:T(8,128)} %fusion.15) | copy-start | bytes 37748740
  513.3 142.5 %all-to-all-start.2 = ((bf16[3,32,256,128]{3,2,0,1:T(8,128)(2,1)}), bf16[3,32,256,128]{3,2,0,1:T(8,128)(2,1)}, u32[]{:S(2)}, u32[]{:S(2)}) async-start(bf16[3,32,256,128]{3,2,0,1:T(8,128)(2,1)} %pad_maximum_fusion), calls=%async_computation.2 | async-start | bytes 12582912 | tf_op jit(solution)/shard_map/all_to_all | solution.py:132
  518.2 245.6 %all-gather.14.cloned.1.call-start = ((), (), s32[]{:S(2)}) async-start(), calls=%async_computation.8 | async-start | bytes 10485760 | tf_op jit(solution)/shard_map/all_gather | solution.py:81
  763.8 3.2 copy-start.7
  763.8 6.7 copy-start.8
  770.5 2.2 copy-start.6
  777.2 1.3 copy-start.4
  788.2 3.3 copy-start.5
Sparse Core Ops, SparseCore 0:
  9.5 78.8 all-gather.7
  90.0 76.1 all-gather.5
  167.7 76.1 all-gather.9
  245.3 154.8 all-gather.11
  520.3 58.9 all-gather.13

commit v3 on v2

--- a/solution.py
+++ b/solution.py
@@ -85,12 +85,12 @@
     slot_index = slot_numbers(chosen, expert_total)
     gate_value = gate_probs.reshape(2 * tok_count)
     target = chosen * capacity + slot_index
-    token_of = jnp.arange(2 * tok_count, dtype=jnp.int32) // 2
-    owner_token = jnp.zeros((expert_total * capacity,), jnp.int32).at[target].set(token_of)
-    filled = jnp.zeros((expert_total * capacity,), jnp.bool_).at[target].set(True)
-    outgoing = jnp.where(
-        filled[:, None], jnp.take(normed, owner_token, axis=0), jnp.zeros((), jnp.bfloat16)
-    )
+    rows_all = jnp.arange(expert_total * capacity, dtype=jnp.int32)
+    assign_rows = (target[:, None] == rows_all[None, :]).astype(jnp.bfloat16)
+    token_rows = assign_rows.reshape(tok_count, 2, expert_total * capacity).sum(axis=1)
+    outgoing = jnp.einsum(
+        "tr,td->rd", token_rows, normed, preferred_element_type=jnp.float32
+    ).astype(jnp.bfloat16)
     outgoing = outgoing.reshape(n_owner, exp_local * capacity, width)
     arrived = lax.all_to_all(outgoing, "expert", split_axis=0, concat_axis=0, tiled=True)
     arrived = arrived.reshape(n_owner, exp_local, capacity, width)
@@ -114,7 +114,7 @@
     returned = lax.all_to_all(results, "expert", split_axis=0, concat_axis=0, tiled=True).reshape(
         expert_total * capacity, width
     )
-    picked = jnp.take(returned, target, axis=0).astype(jnp.float32) * gate_value[:, None]
+    picked = jnp.dot(assign_rows, returned, preferred_element_type=jnp.float32) * gate_value[:, None]
     combined = picked.reshape(tok_count, 2, width).sum(axis=1)
     mixed = (residual + combined).astype(jnp.bfloat16)
     teacher_in = norm_rows(mixed.astype(jnp.float32), teacher_gain).astype(jnp.bfloat16)

time: 810 us -> 810 us (level)
  matrix products: 107 us -> 133 us
  local copies, waits for them, and re-layouts: 115 us -> 90.1 us
  waiting for transfers between devices: 276 us -> 292 us
  other arithmetic: 53.4 us -> 40.3 us
    gather x3 -> x0, local copies, waits for them, and re-layouts: 26.1 us -> none  [the longest x2 20 us: local(): jnp.take(returned, target, axis=0).astype(jnp.float32) * gate_value[:, None]]
    dot_general x0 -> x2, matrix products: none -> 16.1 us  [the longest x1 10.5 us: local(): jnp.dot(assign_rows, returned, preferred_element_type=jnp.float32)]
    all_gather x1, waiting for transfers between devices: 26.6 us -> 41.7 us  [local(): down_full = lax.all_gather(expert_down, 'rep', axis=1, tiled=True)]
    reshape x0 -> x1, local copies, waits for them, and re-layouts: none -> 10.6 us  [local(): combined = picked.reshape(tok_count, 2, width).sum(axis=1)]
    dot_general x4, matrix products: 28.8 us -> 37.9 us  [local(): jnp.einsum('sjcf,jfd->sjcd', hidden[..., low:low + ff_part], down_full[:,...]
    scatter x2 -> x0, local copies, waits for them, and re-layouts: 8.87 us -> none  [the longest x1 4.53 us: local(): jnp.zeros((expert_total * capacity,), jnp.int32).at[target].set(token_of)]
    unnamed x35 -> x34, local copies, waits for them, and re-layouts: 18 us -> 18.2 us
  transfers between devices with their start and end apart: 7 -> 7, of which waited for: 3 -> 3; matrix products, arithmetic and copies ran while one was open for 23% -> 22% of each run, Pallas kernels for 6% -> 6%
where the time goes in v3:
time: 810 us; the launch traced here: 805 us
  waiting for transfers between devices  292 us (36%)
  blocking collectives  180 us (22%)
  matrix products  133 us (16%)
  local copies, waits for them, and re-layouts  90.1 us (11%)
  Pallas kernels  44.7 us (6%)
  other arithmetic  40.3 us (5%)
  between operations  14.3 us (2%)
  starting transfers between devices  10.7 us (1%)
    all_to_all x1, waiting for transfers between devices, local(): lax.all_to_all(grouped, 'expert', split_axis=1, concat_axis=2, tiled=True)  137 us
    all_to_all x1, blocking collectives, local(): lax.all_to_all(outgoing, 'expert', split_axis=0, concat_axis=0, tiled=True)  123 us
    all_to_all x1, waiting for transfers between devices, local(): lax.all_to_all(results, 'expert', split_axis=0, concat_axis=0, tiled=True)  110 us
    all_to_all x1, blocking collectives, local(): lax.all_to_all(attended, 'expert', split_axis=1, concat_axis=0, tiled=True)  51.8 us
    pallas_call x1, Pallas kernels, attention(): pl.pallas_call(functools.partial(attention_kernel, scale=scale), grid=(pa...  44.7 us
    all_gather x1, waiting for transfers between devices, local(): down_full = lax.all_gather(expert_down, 'rep', axis=1, tiled=True)  41.7 us
    dot_general x4, matrix products, local(): jnp.einsum('sjcf,jfd->sjcd', hidden[..., low:low + ff_part], down_full[:,...  37.9 us
    dot_general x1, matrix products, local(): jnp.einsum('sid,djhe->jihse', teacher_in, qkv_full, preferred_element_typ...  26.9 us
  transfers between devices with their start and end apart: 7, of which 3 were waited for; matrix products, arithmetic and copies ran while one was open for 22% of the time, Pallas kernels for 6%

profile of v3, /device:TPU:0, one launch (start us, length us, event | category | flops | bytes accessed | tf_op | source)
XLA Modules:
  0.0 804.6 jit_solution(11016933049074407967)
XLA Ops:
  7.2 0.7 all-gather.8.cloned.1.call-update
  8.0 0.7 all-gather.6.cloned.1.call-update
  8.7 0.7 all-gather.10.cloned.1.call-update
  9.4 10.8 %copy.89 = bf16[2048,3,4,128]{0,3,2,1:T(8,128)(2,1)} copy(bf16[2048,3,4,128]{3,2,1,0:T(4,128)(2,1)} %param.21) | data formatting | bytes 12582912 | tf_op args[8]
  20.2 0.7 copy-done.8
  21.1 0.3 eq.46
  21.4 0.3 reshape.153
  21.7 4.5 reduce-window.6
  26.7 0.2 reduce_sum.73
  27.2 0.2 mul.154
  27.4 0.9 copy_convert_fusion
  28.3 5.3 copy.81
  33.6 6.1 reshape.165
  39.7 1.2 multiply_reduce_fusion.3
  41.2 0.5 fusion.29
  41.7 5.6 convolution_convert_fusion
  47.3 123.1 %all_to_all.43 = bf16[8,160,2048]{2,1,0:T(8,128)(2,1)} all-to-all(bf16[8,160,2048]{2,1,0:T(8,128)(2,1)S(1)} %bitcast.165), channel_id=1, replica_groups=mesh['expert'=8,'rep'=4] {'expert'}, dimensions={0} | all-to-all | bytes 10485760 | tf_op jit(solution)/shard_map/all_to_all | solution.py:95
  170.4 15.3 %fusion.2 = f32[2,8,80,1408]{3,2,1,0:T(8,128)} fusion(bf16[2,2048,1408]{1,2,0:T(8,128)(2,1)} %all-gather.8.cloned.1.call-done, bf16[8,2,80,2048]{3,2,1,0:T(8,128)(2,1)} %bitcast.163), kind=kOutput, calls=%fused_computation.2 | convolution fusion | flops 7381975040 | bytes 23986176 | tf_op jit(solution)/shard_map/sjcd,jdf->sjcf/dot_general | solution.py:100
  185.7 16.5 %fusion.6 = bf16[8,2,80,1408]{3,2,0,1:T(8,128)(2,1)} fusion(f32[2,8,80,1408]{3,2,1,0:T(8,128)} %fusion.2, bf16[2,2048,1408]{1,2,0:T(8,128)(2,1)} %all-gather.6.cloned.1.call-done, bf16[8,2,80,2048]{3,2,1,0:T(8,128)(2,1)} %bitcast.164), kind=kOutput, calls=%fused_computation.9 | convolution fusion | flops 7392788480 | bytes 27590656 | tf_op jit(solution)/shard_map/sjcd,jdf->sjcf/dot_general | solution.py:97
  202.2 41.7 %all-gather.10.cloned.1.call-done = bf16[2,1408,2048]{2,1,0:T(8,128)(2,1)} async-done(((bf16[2,352,2048]{2,1,0:T(8,128)(2,1)}), bf16[2,1408,2048]{2,1,0:T(8,128)(2,1)}) %all-gather.10.cloned.1.call-update) | async-done | bytes 11534352 | tf_op jit(solution)/shard_map/all_gather | solution.py:78
  243.9 5.3 fusion.27
  249.2 6.8 fusion.28
  256.0 17.3 %fusion.26 = bf16[2,8,80,2048]{3,2,1,0:T(8,128)(2,1)} fusion(bf16[2,1408,2048]{2,1,0:T(8,128)(2,1)} %all-gather.10.cloned.1.call-done, bf16[8,2,80,1408]{3,2,0,1:T(8,128)(2,1)S(1)} %copy-done.13), kind=kOutput, calls=%fused_computation.49 | convolution fusion | flops 1845493760 | bytes 9109504 | tf_op jit(solution)/shard_map/sjcf,jfd->sjcd/dot_general | solution.py:107
  273.3 8.4 %fusion.10 = bf16[8,2,80,2048]{3,2,0,1:T(8,128)(2,1)S(1)} fusion(bf16[2,8,80,2048]{3,2,1,0:T(8,128)(2,1)} %fusion.26, bf16[2,8,80,2048]{3,2,1,0:T(8,128)(2,1)S(1)} %fusion.27, bf16[2,8,80,2048]{3,2,1,0:T(8,128)(2,1)} %fusion.28, bf16[2,1408,2048]{2,1,0:T(8,128)(2,1)} %all-gather.10.cloned.1.call-done, bf16[8,2,80,1408]{3,2,0,1:T(8,128)(2,1)} %fusion.6), kind=kOutput, calls=%fused_computation.18 | convolution fusion | flops 1869086720 | bytes 24838144 | tf_op jit(solution)/shard_map/sjcf,jfd->sjcd/dot_general | solution.py:107
  281.8 3.0 copy.85
  284.8 5.6 all-to-all-start.1
  290.4 0.2 copy.86
  290.6 0.3 mul.162
  290.9 5.4 all_gather.22
  296.4 110.2 %all-to-all-done.1 = bf16[8,160,2048]{2,1,0:T(8,128)(2,1)} async-done(((bf16[8,160,2048]{2,1,0:T(8,128)(2,1)}), bf16[8,160,2048]{2,1,0:T(8,128)(2,1)}, u32[]{:S(2)}, u32[]{:S(2)}) %all-to-all-start.1) | async-done | bytes 5242912 | tf_op jit(solution)/shard_map/all_to_all | solution.py:114
  406.6 10.5 %fusion.17 = f32[1024,2048]{1,0:T(8,128)} fusion(bf16[1280,2048]{1,0:T(8,128)(2,1)} %bitcast.21, f32[1024]{0:T(1024)S(1)} %mul.162, s32[1024]{0:T(1024)S(1)} %multiply_add_fusion), kind=kOutput, calls=%fused_computation.25 | convolution fusion | flops 5372116992 | bytes 13639680 | tf_op jit(solution)/shard_map/dot_general | solution.py:117
  417.1 10.6 %reshape.159 = f32[512,2,2048]{2,1,0:T(2,128)} reshape(f32[1024,2048]{1,0:T(8,128)} %fusion.17) | data formatting | bytes 16777216 | tf_op jit(solution)/shard_map/reshape | solution.py:118
  427.6 13.4 %reduce_sum.76 = f32[512,2048]{1,0:T(8,128)} reduce(f32[512,2,2048]{2,1,0:T(2,128)} %reshape.159, f32[]{:T(128)} %constant.10.clone.1), dimensions={1}, to_apply=%region_5.6 | reduce | flops 1048576 | bytes 12582916 | tf_op jit(solution)/shard_map/reduce_sum | solution.py:118
  441.1 5.8 reduce_sum.77
  446.9 5.8 reduce_sum.78
  452.8 5.6 multiply_reduce_fusion.2
  458.4 26.9 %fusion.18 = f32[3,2,16,256,128]{3,4,2,0,1:T(8,128)} fusion(bf16[2048,3,16,128]{0,3,2,1:T(8,128)(2,1)} %all-gather.12.cloned.1.call-done, f32[2048]{0:T(1024)S(1)} %copy-done.12, f32[256,2]{0,1:T(2,128)S(1)} %add_rsqrt_fusion.2, f32[256,2,2048]{2,1,0:T(2,128)} %reduce_sum.77, bf16[1,256,2,2048]{3,2,1,0:T(2,128)(2,1)S(1)} %copy-done.1), kind=kOutput, calls=%fused_computation.26 | convolution fusion | flops 12892241920 | bytes 44050432 | tf_op jit(solution)/shard_map/sid,djhe->jihse/dot_general | solution.py:124
  485.3 4.8 multiply_reduce_fusion.1
  490.1 4.6 slice.143
  494.7 2.7 multiply_convert_fusion.1
  497.4 4.1 copy.91
  501.5 4.1 copy.92
  505.5 4.1 copy.93
  509.6 6.4 pad_maximum_fusion
  516.0 4.9 all-to-all-start.2
  521.0 0.5 all-gather.14.cloned.1.call-update
  521.5 137.1 %all-to-all-done.2 = bf16[3,32,256,128]{3,2,0,1:T(8,128)(2,1)} async-done(((bf16[3,32,256,128]{3,2,0,1:T(8,128)(2,1)}), bf16[3,32,256,128]{3,2,0,1:T(8,128)(2,1)}, u32[]{:S(2)}, u32[]{:S(2)}) %all-to-all-start.2) | async-done | bytes 6291488 | tf_op jit(solution)/shard_map/all_to_all | solution.py:132
  658.7 6.3 copy.95
  664.9 44.7 %shard_map.140 = bf16[4,2048,128]{2,1,0:T(8,128)(2,1)} custom-call(bf16[3,4,2048,128]{3,2,1,0:T(8,128)(2,1)} %bitcast.154, bf16[3,4,2048,128]{3,2,1,0:T(8,128)(2,1)} %bitcast.155, bf16[3,4,2048,128]{3,2,1,0:T(8,128)(2,1)} %bitcast.156), custom_call_target="tpu_custom_call" | custom-call | tf_op jit(solution)/shard_map/pallas_call | solution.py:38
  709.6 3.4 copy.96
  713.0 51.8 %all_to_all.44 = bf16[4,2048,128]{2,0,1:T(4,128)(2,1)S(1)} all-to-all(bf16[4,2048,128]{2,0,1:T(4,128)(2,1)S(1)} %copy.96), channel_id=1, replica_groups=mesh['expert'=8,'rep'=4] {'expert'}, dimensions={1} | all-to-all | bytes 4194304 | tf_op jit(solution)/shard_map/all_to_all | solution.py:136
  764.8 1.8 copy.97
  766.7 3.2 bitcast_convert_fusion
  769.8 3.5 bitcast_convert_fusion.1
  773.4 1.3 bitcast_convert_fusion.2
  774.6 0.9 copy-done.5
  775.6 4.4 fusion.23
  780.0 1.3 copy-done.3
  781.3 2.2 copy.98
  783.5 2.4 reshape.162
  785.9 5.2 fusion.64
  791.1 2.4 fusion.44
  793.7 0.7 copy.100
  794.3 3.5 copy.99
  (57 shorter events, 1.7 us)
Async XLA Ops:
  7.2 783.9 %copy-start = (f32[1024]{0:T(1024)S(1)}, f32[1024]{0:T(1024)}, u32[]{:S(2)}) copy-start(f32[1024]{0:T(1024)} %param.25) | copy-start | bytes 12292
  7.2 163.3 %all-gather.8.cloned.1.call-start = ((), (), s32[]{:S(2)}) async-start(), calls=%async_computation.5 | async-start | bytes 14417920 | tf_op jit(solution)/shard_map/all_gather | solution.py:77
  7.9 177.8 %all-gather.6.cloned.1.call-start = ((), (), s32[]{:S(2)}) async-start(), calls=%async_computation.4 | async-start | bytes 14417920 | tf_op jit(solution)/shard_map/all_gather | solution.py:76
  8.7 235.2 %all-gather.10.cloned.1.call-start = ((), (), s32[]{:S(2)}) async-start(), calls=%async_computation.6 | async-start | bytes 14417920 | tf_op jit(solution)/shard_map/all_gather | solution.py:78
  9.4 449.0 %all-gather.12.cloned.1.call-start = ((), (), s32[]{:S(2)}) async-start(), calls=%async_computation.7 | async-start | bytes 31457280 | tf_op jit(solution)/shard_map/all_gather | solution.py:79
  20.2 0.7 copy-start.8
  20.2 7.2 copy-start.1
  33.6 8.1 %copy-start.11 = (f32[2048]{0:T(1024)S(1)}, f32[2048]{0:T(1024)}, u32[]{:S(2)}) copy-start(f32[2048]{0:T(1024)} %param.16) | copy-start | bytes 24580
  243.9 5.3 copy-start.13
  284.8 5.6 copy-start.9
  284.8 6.1 copy-start.10
  284.8 121.7 %all-to-all-start.1 = ((bf16[8,160,2048]{2,1,0:T(8,128)(2,1)}), bf16[8,160,2048]{2,1,0:T(8,128)(2,1)}, u32[]{:S(2)}, u32[]{:S(2)}) async-start(bf16[8,160,2048]{2,1,0:T(8,128)(2,1)} %bitcast.157), calls=%async_computation.1 | async-start | bytes 10485760 | tf_op jit(solution)/shard_map/all_to_all | solution.py:114
  452.8 5.7 copy-start.12
  485.3 9.4 %copy-start.2 = (f32[3,2,16,256,128]{3,4,2,0,1:T(8,128)S(1)}, f32[3,2,16,256,128]{3,4,2,0,1:T(8,128)}, u32[]{:S(2)}) copy-start(f32[3,2,16,256,128]{3,4,2,0,1:T(8,128)} %fusion.18) | copy-start | bytes 37748740
  516.0 142.6 %all-to-all-start.2 = ((bf16[3,32,256,128]{3,2,0,1:T(8,128)(2,1)}), bf16[3,32,256,128]{3,2,0,1:T(8,128)(2,1)}, u32[]{:S(2)}, u32[]{:S(2)}) async-start(bf16[3,32,256,128]{3,2,0,1:T(8,128)(2,1)} %pad_maximum_fusion), calls=%async_computation.2 | async-start | bytes 12582912 | tf_op jit(solution)/shard_map/all_to_all | solution.py:132
  520.9 245.7 %all-gather.14.cloned.1.call-start = ((), (), s32[]{:S(2)}) async-start(), calls=%async_computation.8 | async-start | bytes 10485760 | tf_op jit(solution)/shard_map/all_gather | solution.py:81
  766.7 3.2 copy-start.6
  766.7 6.7 copy-start.7
  773.4 2.2 copy-start.5
  780.0 1.3 copy-start.3
  791.1 3.3 copy-start.4
Sparse Core Ops, SparseCore 0:
  9.5 78.8 all-gather.7
  90.0 76.1 all-gather.5
  167.7 76.1 all-gather.9
  245.3 154.8 all-gather.11
  523.0 58.6 all-gather.13

commit v4 on v3

--- a/solution.py
+++ b/solution.py
@@ -49,6 +49,26 @@
     )(whole, whole, whole)
 
 
+def rep_parts(parts, count):
+    if count == 1:
+        return [parts]
+
+    def send(values, shift):
+        return tuple(
+            lax.ppermute(v, "rep", [(i, shift(i)) for i in range(count)]) for v in values
+        )
+
+    if count == 4:
+        far = send(parts, lambda i: i ^ 2)
+        near = send(parts, lambda i: i ^ 1)
+        far_near = send(far, lambda i: i ^ 1)
+        return [parts, near, far, far_near]
+    received = [parts]
+    for _ in range(count - 1):
+        received.append(send(received[-1], lambda i: (i + 1) % count))
+    return received
+
+
 def local(
     tokens,
     expert_ids,
@@ -73,9 +93,7 @@
     exp_local = expert_gate.shape[0]
     expert_total = exp_local * n_owner
     capacity = max(2, tok_count * 10 // (4 * expert_total))
-    gate_full = lax.all_gather(expert_gate, "rep", axis=2, tiled=True)
-    up_full = lax.all_gather(expert_up, "rep", axis=2, tiled=True)
-    down_full = lax.all_gather(expert_down, "rep", axis=1, tiled=True)
+    weight_parts = rep_parts((expert_gate, expert_up, expert_down), n_replica)
     qkv_full = lax.all_gather(teacher_qkv, "rep", axis=2, tiled=True)
     qk_gain_full = lax.all_gather(qk_gain, "rep", axis=1, tiled=True)
     out_full = lax.all_gather(teacher_out, "rep", axis=0, tiled=True)
@@ -94,21 +112,15 @@
     outgoing = outgoing.reshape(n_owner, exp_local * capacity, width)
     arrived = lax.all_to_all(outgoing, "expert", split_axis=0, concat_axis=0, tiled=True)
     arrived = arrived.reshape(n_owner, exp_local, capacity, width)
-    gate_part = jnp.einsum(
-        "sjcd,jdf->sjcf", arrived, gate_full, preferred_element_type=jnp.float32
-    )
-    up_part = jnp.einsum("sjcd,jdf->sjcf", arrived, up_full, preferred_element_type=jnp.float32)
-    hidden = (jax.nn.silu(gate_part) * up_part).astype(jnp.bfloat16)
-    ff_total = hidden.shape[-1]
-    ff_part = ff_total // n_replica
     produced = jnp.zeros(arrived.shape, jnp.float32)
-    for part in range(n_replica):
-        low = part * ff_part
+    for gate_w, up_w, down_w in weight_parts:
+        gate_part = jnp.einsum(
+            "sjcd,jdf->sjcf", arrived, gate_w, preferred_element_type=jnp.float32
+        )
+        up_part = jnp.einsum("sjcd,jdf->sjcf", arrived, up_w, preferred_element_type=jnp.float32)
+        hidden = (jax.nn.silu(gate_part) * up_part).astype(jnp.bfloat16)
         produced = produced + jnp.einsum(
-            "sjcf,jfd->sjcd",
-            hidden[..., low:low + ff_part],
-            down_full[:, low:low + ff_part],
-            preferred_element_type=jnp.float32,
+            "sjcf,jfd->sjcd", hidden, down_w, preferred_element_type=jnp.float32
         ).astype(jnp.bfloat16).astype(jnp.float32)
     results = produced.astype(jnp.bfloat16).reshape(n_owner, exp_local * capacity, width)
     returned = lax.all_to_all(results, "expert", split_axis=0, concat_axis=0, tiled=True).reshape(

time: 810 us -> 961 us (1.19)
  waiting for transfers between devices: 292 us -> 531 us
  blocking collectives: 180 us -> 57 us
  matrix products: 133 us -> 147 us
  starting transfers between devices: 10.7 us -> 22.7 us
    ppermute x0 -> x9, waiting for transfers between devices: none -> 284 us  [send(): lax.ppermute(v, 'rep', [(i, shift(i)) for i in range(count)])]
    all_to_all x1 -> x0, blocking collectives: 123 us -> none  [local(): lax.all_to_all(outgoing, 'expert', split_axis=0, concat_axis=0, tiled=True)]
    all_gather x3 -> x0, waiting for transfers between devices: 41.7 us -> none  [the longest x1 41.7 us: local(): down_full = lax.all_gather(expert_down, 'rep', axis=1, tiled=True)]
    dot_general x6 -> x8, matrix products: 69.7 us -> 82.7 us  [the longest x4 52.1 us: local(): jnp.einsum('sjcf,jfd->sjcd', hidden, down_w, preferred_element_type=jnp.f...]
  transfers between devices with their start and end apart: 7 -> 14, of which waited for: 3 -> 5; matrix products, arithmetic and copies ran while one was open for 22% -> 19% of each run, Pallas kernels for 6% -> 5%
where the time goes in v4:
time: 961 us; the launch traced here: 952 us
  waiting for transfers between devices  531 us (55%)
  matrix products  147 us (15%)
  local copies, waits for them, and re-layouts  93.8 us (10%)
  blocking collectives  57 us (6%)
  Pallas kernels  44.7 us (5%)
  other arithmetic  40.2 us (4%)
  starting transfers between devices  22.7 us (2%)
  between operations  14.6 us (2%)
    ppermute x9, waiting for transfers between devices, send(): lax.ppermute(v, 'rep', [(i, shift(i)) for i in range(count)])  284 us
    all_to_all x1, waiting for transfers between devices, local(): lax.all_to_all(grouped, 'expert', split_axis=1, concat_axis=2, tiled=True)  137 us
    all_to_all x1, waiting for transfers between devices, local(): lax.all_to_all(results, 'expert', split_axis=0, concat_axis=0, tiled=True)  110 us
    dot_general x4, matrix products, local(): jnp.einsum('sjcf,jfd->sjcd', hidden, down_w, preferred_element_type=jnp.f...  52.1 us
    all_to_all x1, blocking collectives, local(): lax.all_to_all(attended, 'expert', split_axis=1, concat_axis=0, tiled=True)  51.8 us
    pallas_call x1, Pallas kernels, attention(): pl.pallas_call(functools.partial(attention_kernel, scale=scale), grid=(pa...  44.7 us
    dot_general x4, matrix products, local(): jnp.einsum('sjcd,jdf->sjcf', arrived, gate_w, preferred_element_type=jnp....  30.6 us
    dot_general x1, matrix products, local(): jnp.einsum('sid,djhe->jihse', teacher_in, qkv_full, preferred_element_typ...  26.7 us
  transfers between devices with their start and end apart: 14, of which 5 were waited for; matrix products, arithmetic and copies ran while one was open for 19% of the time, Pallas kernels for 5%

profile of v4, /device:TPU:0, one launch (start us, length us, event | category | flops | bytes accessed | tf_op | source)
XLA Modules:
  0.0 951.8 jit_solution(16172603343947775145)
XLA Ops:
  7.2 10.6 %copy.103 = bf16[2048,3,4,128]{0,3,2,1:T(8,128)(2,1)} copy(bf16[2048,3,4,128]{3,2,1,0:T(4,128)(2,1)} %param.21) | data formatting | bytes 12582912 | tf_op args[8]
  17.9 0.7 copy-done.8
  19.4 4.5 reduce-window.6
  25.0 0.9 copy_convert_fusion
  26.0 6.0 copy.89
  31.9 6.5 reshape.165
  38.5 1.2 multiply_reduce_fusion.3
  40.0 0.5 fusion.37
  40.5 7.5 convolution_convert_fusion
  48.0 7.5 all-to-all-start
  55.5 1.6 collective-permute-start.3
  57.1 0.5 collective-permute-start.4
  57.6 1.5 collective-permute-start.5
  59.1 0.5 collective-permute-start.1
  59.6 123.4 %collective-permute-done.3 = bf16[2,2048,352]{1,2,0:T(8,128)(2,1)} collective-permute-done((bf16[2,2048,352]{1,2,0:T(8,128)(2,1)}, bf16[2,2048,352]{1,2,0:T(8,128)(2,1)}, u32[]{:S(2)}, u32[]{:S(2)}) %collective-permute-start.3) | collective-permute-done | bytes 2883616 | tf_op jit(solution)/shard_map/ppermute | solution.py:58
  183.0 7.5 fusion.35
  190.6 7.5 fusion.23
  198.1 99.1 %collective-permute-done.4 = bf16[2,2048,352]{1,2,0:T(8,128)(2,1)} collective-permute-done((bf16[2,2048,352]{1,2,0:T(8,128)(2,1)}, bf16[2,2048,352]{1,2,0:T(8,128)(2,1)}, u32[]{:S(2)}, u32[]{:S(2)}) %collective-permute-start.4) | collective-permute-done | bytes 2883616 | tf_op jit(solution)/shard_map/ppermute | solution.py:58
  297.1 61.4 %collective-permute-done.5 = bf16[2,352,2048]{2,1,0:T(8,128)(2,1)} collective-permute-done((bf16[2,352,2048]{2,1,0:T(8,128)(2,1)}, bf16[2,352,2048]{2,1,0:T(8,128)(2,1)}, u32[]{:S(2)}, u32[]{:S(2)}) %collective-permute-start.5) | collective-permute-done | bytes 2883616 | tf_op jit(solution)/shard_map/ppermute | solution.py:58
  358.5 0.5 collective-permute-start.8
  359.0 7.5 fusion.29
  366.6 12.7 %fusion.31 = bf16[2,8,80,2048]{3,2,1,0:T(8,128)(2,1)} fusion(bf16[2,352,2048]{2,1,0:T(8,128)(2,1)} %param.19, f32[2,8,80,352]{3,2,1,0:T(8,128)} %fusion.35, bf16[2,2048,352]{1,2,0:T(8,128)(2,1)} %param.18, bf16[8,2,80,2048]{3,2,1,0:T(8,128)(2,1)} %bitcast.4), kind=kOutput, calls=%fused_computation.51 | convolution fusion | flops 3693690880 | bytes 18055168 | tf_op jit(solution)/shard_map/sjcf,jfd->sjcd/dot_general | solution.py:122
  379.3 8.0 fusion.17
  387.3 12.7 %fusion.19 = bf16[2,8,80,2048]{3,2,1,0:T(8,128)(2,1)} fusion(bf16[2,352,2048]{2,1,0:T(8,128)(2,1)} %collective-permute-done.5, f32[2,8,80,352]{3,2,1,0:T(8,128)} %fusion.23, bf16[2,2048,352]{1,2,0:T(8,128)(2,1)} %collective-permute-done.4, bf16[8,2,80,2048]{3,2,1,0:T(8,128)(2,1)} %bitcast.4), kind=kOutput, calls=%fused_computation.39 | convolution fusion | flops 3693690880 | bytes 18055168 | tf_op jit(solution)/shard_map/sjcf,jfd->sjcd/dot_general | solution.py:122
  400.0 12.8 %fusion.25 = bf16[2,8,80,2048]{3,2,1,0:T(8,128)(2,1)} fusion(bf16[2,352,2048]{2,1,0:T(8,128)(2,1)} %collective-permute-done.2, f32[2,8,80,352]{3,2,1,0:T(8,128)} %fusion.29, bf16[2,2048,352]{1,2,0:T(8,128)(2,1)} %collective-permute-done.1, bf16[8,2,80,2048]{3,2,1,0:T(8,128)(2,1)} %bitcast.4), kind=kOutput, calls=%fused_computation.45 | convolution fusion | flops 3693690880 | bytes 18055168 | tf_op jit(solution)/shard_map/sjcf,jfd->sjcd/dot_general | solution.py:122
  412.7 13.9 %fusion.2 = bf16[8,2,80,2048]{3,2,0,1:T(8,128)(2,1)} fusion(bf16[2,8,80,2048]{3,2,1,0:T(8,128)(2,1)} %fusion.19, bf16[2,8,80,2048]{3,2,1,0:T(8,128)(2,1)} %fusion.25, bf16[2,8,80,2048]{3,2,1,0:T(8,128)(2,1)} %fusion.31, bf16[2,352,2048]{2,1,0:T(8,128)(2,1)} %collective-permute-done.8, f32[2,8,80,352]{3,2,1,0:T(8,128)} %fusion.17, ...), kind=kOutput, calls=%fused_computation.7 | convolution fusion | flops 3717283840 | bytes 33783808 | tf_op jit(solution)/shard_map/sjcf,jfd->sjcd/dot_general | solution.py:122
  426.7 5.6 copy.99
  432.3 5.6 all-to-all-start.1
  438.5 5.2 all_gather.10
  443.7 110.2 %all-to-all-done.1 = bf16[8,160,2048]{2,1,0:T(8,128)(2,1)} async-done(((bf16[8,160,2048]{2,1,0:T(8,128)(2,1)}), bf16[8,160,2048]{2,1,0:T(8,128)(2,1)}, u32[]{:S(2)}, u32[]{:S(2)}) %all-to-all-start.1) | async-done | bytes 5242912 | tf_op jit(solution)/shard_map/all_to_all | solution.py:126
  553.9 10.5 %fusion.5 = f32[1024,2048]{1,0:T(8,128)} fusion(bf16[1280,2048]{1,0:T(8,128)(2,1)} %bitcast.39, f32[1024]{0:T(1024)S(1)} %mul.186, s32[1024]{0:T(1024)S(1)} %multiply_add_fusion), kind=kOutput, calls=%fused_computation.12 | convolution fusion | flops 5372116992 | bytes 13639680 | tf_op jit(solution)/shard_map/dot_general | solution.py:129
  564.4 10.6 %reshape.159 = f32[512,2,2048]{2,1,0:T(2,128)} reshape(f32[1024,2048]{1,0:T(8,128)} %fusion.5) | data formatting | bytes 16777216 | tf_op jit(solution)/shard_map/reshape | solution.py:130
  575.0 13.4 %reduce_sum.76 = f32[512,2048]{1,0:T(8,128)} reduce(f32[512,2,2048]{2,1,0:T(2,128)} %reshape.159, f32[]{:T(128)} %constant.28.clone.1), dimensions={1}, to_apply=%region_5.6 | reduce | flops 1048576 | bytes 12582916 | tf_op jit(solution)/shard_map/reduce_sum | solution.py:130
  588.4 5.9 reduce_sum.77
  594.3 5.9 reduce_sum.78
  600.1 5.6 multiply_reduce_fusion.2
  605.8 26.7 %fusion.6 = f32[3,2,16,256,128]{3,4,2,0,1:T(8,128)} fusion(bf16[2048,3,16,128]{0,3,2,1:T(8,128)(2,1)} %all-gather.3.cloned.1.call-done, f32[2048]{0:T(1024)S(1)} %copy-done.12, f32[256,2]{0,1:T(2,128)S(1)} %add_rsqrt_fusion.2, f32[256,2,2048]{2,1,0:T(2,128)} %reduce_sum.77, bf16[1,256,2,2048]{3,2,1,0:T(2,128)(2,1)S(1)} %copy-done.1), kind=kOutput, calls=%fused_computation.13 | convolution fusion | flops 12892241920 | bytes 44050432 | tf_op jit(solution)/shard_map/sid,djhe->jihse/dot_general | solution.py:136
  632.5 4.8 multiply_reduce_fusion.1
  637.4 4.6 slice.87
  641.9 2.6 multiply_convert_fusion.1
  644.5 4.1 copy.105
  648.7 4.1 copy.106
  652.7 4.1 copy.107
  656.8 6.4 pad_maximum_fusion
  663.2 4.9 all-to-all-start.2
  668.2 0.7 all-gather.5.cloned.1.call-update
  668.9 136.7 %all-to-all-done.2 = bf16[3,32,256,128]{3,2,0,1:T(8,128)(2,1)} async-done(((bf16[3,32,256,128]{3,2,0,1:T(8,128)(2,1)}), bf16[3,32,256,128]{3,2,0,1:T(8,128)(2,1)}, u32[]{:S(2)}, u32[]{:S(2)}) %all-to-all-start.2) | async-done | bytes 6291488 | tf_op jit(solution)/shard_map/all_to_all | solution.py:144
  805.6 6.2 copy.109
  811.8 44.7 %shard_map.140 = bf16[4,2048,128]{2,1,0:T(8,128)(2,1)} custom-call(bf16[3,4,2048,128]{3,2,1,0:T(8,128)(2,1)} %bitcast.265, bf16[3,4,2048,128]{3,2,1,0:T(8,128)(2,1)} %bitcast.266, bf16[3,4,2048,128]{3,2,1,0:T(8,128)(2,1)} %bitcast.267), custom_call_target="tpu_custom_call" | custom-call | tf_op jit(solution)/shard_map/pallas_call | solution.py:38
  856.5 3.4 copy.110
  859.9 51.8 %all_to_all.43 = bf16[4,2048,128]{2,0,1:T(4,128)(2,1)S(1)} all-to-all(bf16[4,2048,128]{2,0,1:T(4,128)(2,1)S(1)} %copy.110), channel_id=1, replica_groups=mesh['expert'=8,'rep'=4] {'expert'}, dimensions={1} | all-to-all | bytes 4194304 | tf_op jit(solution)/shard_map/all_to_all | solution.py:148
  911.7 1.8 copy.111
  913.6 3.2 bitcast_convert_fusion
  916.8 3.5 bitcast_convert_fusion.1
  920.3 1.3 bitcast_convert_fusion.2
  921.6 0.9 copy-done.5
  922.5 4.4 fusion.11
  926.9 1.3 copy-done.3
  928.2 2.2 copy.112
  930.4 2.4 reshape.162
  932.8 5.2 fusion.120
  938.0 2.4 fusion.52
  940.6 0.7 copy.114
  941.2 3.5 copy.113
  (67 shorter events, 3.1 us)
Async XLA Ops:
  7.2 930.8 %copy-start = (f32[1024]{0:T(1024)S(1)}, f32[1024]{0:T(1024)}, u32[]{:S(2)}) copy-start(f32[1024]{0:T(1024)} %param.25) | copy-start | bytes 12292
  7.2 598.6 %all-gather.3.cloned.1.call-start = ((), (), s32[]{:S(2)}) async-start(), calls=%async_computation.4 | async-start | bytes 31457280 | tf_op jit(solution)/shard_map/all_gather | solution.py:97
  17.9 0.7 copy-start.8
  17.9 7.2 copy-start.1
  38.5 2.0 copy-start.11
  48.0 135.0 %all-to-all-start = ((bf16[8,160,2048]{2,1,0:T(8,128)(2,1)}), bf16[8,160,2048]{2,1,0:T(8,128)(2,1)}, u32[]{:S(2)}, u32[]{:S(2)}) async-start(bf16[8,160,2048]{2,1,0:T(8,128)(2,1)} %bitcast.274), calls=%async_computation | async-start | bytes 10485760 | tf_op jit(solution)/shard_map/all_to_all | solution.py:113
  55.5 127.5 %collective-permute-start.3 = (bf16[2,2048,352]{1,2,0:T(8,128)(2,1)}, bf16[2,2048,352]{1,2,0:T(8,128)(2,1)}, u32[]{:S(2)}, u32[]{:S(2)}) collective-permute-start(bf16[2,2048,352]{1,2,0:T(8,128)(2,1)} %param.17), channel_id=1, source_target_pairs={{0,2},{1,3},{2,0},{3,1},{4,6},{5,7},{6,4},{7,5},{8,10},{9,11},{10,... | collective-permute-start | bytes 8650760 | tf_op jit(solution)/shard_map/ppermute | solution.py:58
  57.1 240.1 %collective-permute-start.4 = (bf16[2,2048,352]{1,2,0:T(8,128)(2,1)}, bf16[2,2048,352]{1,2,0:T(8,128)(2,1)}, u32[]{:S(2)}, u32[]{:S(2)}) collective-permute-start(bf16[2,2048,352]{1,2,0:T(8,128)(2,1)} %param.18), channel_id=1, source_target_pairs={{0,2},{1,3},{2,0},{3,1},{4,6},{5,7},{6,4},{7,5},{8,10},{9,11},{10,... | collective-permute-start | bytes 8650760 | tf_op jit(solution)/shard_map/ppermute | solution.py:58
  57.6 300.9 %collective-permute-start.5 = (bf16[2,352,2048]{2,1,0:T(8,128)(2,1)}, bf16[2,352,2048]{2,1,0:T(8,128)(2,1)}, u32[]{:S(2)}, u32[]{:S(2)}) collective-permute-start(bf16[2,352,2048]{2,1,0:T(8,128)(2,1)} %param.19), channel_id=1, source_target_pairs={{0,2},{1,3},{2,0},{3,1},{4,6},{5,7},{6,4},{7,5},{8,10},{9,11},{10,... | collective-permute-start | bytes 8650760 | tf_op jit(solution)/shard_map/ppermute | solution.py:58
  59.1 299.4 %collective-permute-start = (bf16[2,2048,352]{1,2,0:T(8,128)(2,1)}, bf16[2,2048,352]{1,2,0:T(8,128)(2,1)}, u32[]{:S(2)}, u32[]{:S(2)}) collective-permute-start(bf16[2,2048,352]{1,2,0:T(8,128)(2,1)} %param.17), channel_id=1, source_target_pairs={{0,1},{1,0},{2,3},{3,2},{4,5},{5,4},{6,7},{7,6},{8,9},{9,8},{10,11... | collective-permute-start | bytes 8650760 | tf_op jit(solution)/shard_map/ppermute | solution.py:58
  59.1 340.9 %collective-permute-start.1 = (bf16[2,2048,352]{1,2,0:T(8,128)(2,1)}, bf16[2,2048,352]{1,2,0:T(8,128)(2,1)}, u32[]{:S(2)}, u32[]{:S(2)}) collective-permute-start(bf16[2,2048,352]{1,2,0:T(8,128)(2,1)} %param.18), channel_id=1, source_target_pairs={{0,1},{1,0},{2,3},{3,2},{4,5},{5,4},{6,7},{7,6},{8,9},{9,8},{10,11... | collective-permute-start | bytes 8650760 | tf_op jit(solution)/shard_map/ppermute | solution.py:58
  183.0 196.3 %collective-permute-start.6 = (bf16[2,2048,352]{1,2,0:T(8,128)(2,1)}, bf16[2,2048,352]{1,2,0:T(8,128)(2,1)}, u32[]{:S(2)}, u32[]{:S(2)}) collective-permute-start(bf16[2,2048,352]{1,2,0:T(8,128)(2,1)} %collective-permute-done.3), channel_id=1, source_target_pairs={{0,1},{1,0},{2,3},{3,2},{4,5},{5,4},{6,7},{7,6},{8,9},{9,8},{10,11... | collective-permute-start | bytes 8650760 | tf_op jit(solution)/shard_map/ppermute | solution.py:58
  297.1 102.8 %collective-permute-start.2 = (bf16[2,352,2048]{2,1,0:T(8,128)(2,1)}, bf16[2,352,2048]{2,1,0:T(8,128)(2,1)}, u32[]{:S(2)}, u32[]{:S(2)}) collective-permute-start(bf16[2,352,2048]{2,1,0:T(8,128)(2,1)} %param.19), channel_id=1, source_target_pairs={{0,1},{1,0},{2,3},{3,2},{4,5},{5,4},{6,7},{7,6},{8,9},{9,8},{10,11... | collective-permute-start | bytes 8650760 | tf_op jit(solution)/shard_map/ppermute | solution.py:58
  358.5 54.2 %collective-permute-start.7 = (bf16[2,2048,352]{1,2,0:T(8,128)(2,1)}, bf16[2,2048,352]{1,2,0:T(8,128)(2,1)}, u32[]{:S(2)}, u32[]{:S(2)}) collective-permute-start(bf16[2,2048,352]{1,2,0:T(8,128)(2,1)} %collective-permute-done.4), channel_id=1, source_target_pairs={{0,1},{1,0},{2,3},{3,2},{4,5},{5,4},{6,7},{7,6},{8,9},{9,8},{10,11... | collective-permute-start | bytes 8650760 | tf_op jit(solution)/shard_map/ppermute | solution.py:58
  358.5 54.2 %collective-permute-start.8 = (bf16[2,352,2048]{2,1,0:T(8,128)(2,1)}, bf16[2,352,2048]{2,1,0:T(8,128)(2,1)}, u32[]{:S(2)}, u32[]{:S(2)}) collective-permute-start(bf16[2,352,2048]{2,1,0:T(8,128)(2,1)} %collective-permute-done.5), channel_id=1, source_target_pairs={{0,1},{1,0},{2,3},{3,2},{4,5},{5,4},{6,7},{7,6},{8,9},{9,8},{10,11... | collective-permute-start | bytes 8650760 | tf_op jit(solution)/shard_map/ppermute | solution.py:58
  432.3 5.7 copy-start.9
  432.3 6.2 copy-start.10
  432.3 121.6 %all-to-all-start.1 = ((bf16[8,160,2048]{2,1,0:T(8,128)(2,1)}), bf16[8,160,2048]{2,1,0:T(8,128)(2,1)}, u32[]{:S(2)}, u32[]{:S(2)}) async-start(bf16[8,160,2048]{2,1,0:T(8,128)(2,1)} %bitcast.268), calls=%async_computation.1 | async-start | bytes 10485760 | tf_op jit(solution)/shard_map/all_to_all | solution.py:126
  600.1 5.7 copy-start.12
  632.5 9.4 copy-start.2
  663.2 142.4 %all-to-all-start.2 = ((bf16[3,32,256,128]{3,2,0,1:T(8,128)(2,1)}), bf16[3,32,256,128]{3,2,0,1:T(8,128)(2,1)}, u32[]{:S(2)}, u32[]{:S(2)}) async-start(bf16[3,32,256,128]{3,2,0,1:T(8,128)(2,1)} %pad_maximum_fusion), calls=%async_computation.2 | async-start | bytes 12582912 | tf_op jit(solution)/shard_map/all_to_all | solution.py:144
  668.1 245.5 %all-gather.5.cloned.1.call-start = ((), (), s32[]{:S(2)}) async-start(), calls=%async_computation.5 | async-start | bytes 10485760 | tf_op jit(solution)/shard_map/all_gather | solution.py:99
  913.6 3.2 copy-start.6
  913.6 6.7 copy-start.7
  920.3 2.2 copy-start.5
  926.9 1.3 copy-start.3
  938.0 3.3 copy-start.4
Sparse Core Ops, SparseCore 0:
  18.0 272.3 all-gather.2
  670.5 58.6 all-gather.4

commit v5 on v3

--- a/solution.py
+++ b/solution.py
@@ -119,6 +119,28 @@
     mixed = (residual + combined).astype(jnp.bfloat16)
     teacher_in = norm_rows(mixed.astype(jnp.float32), teacher_gain).astype(jnp.bfloat16)
     teacher_in = teacher_in.reshape(seq_dev, images, width)
+    mixed = mixed.reshape(seq_dev, images, width)
+    heads_all = qkv_full.shape[2]
+    head_size = qkv_full.shape[3]
+    chunks = images if (heads_all % n_owner == 0) else 1
+    per_chunk = images // chunks
+    features_parts = []
+    logits_parts = []
+    for chunk in range(chunks):
+        sel = slice(chunk * per_chunk, (chunk + 1) * per_chunk)
+        features, logits = teach(
+            teacher_in[:, sel], mixed[:, sel], qkv_full, qk_gain_full, out_full, critic_in, critic_out,
+            n_replica,
+        )
+        features_parts.append(features)
+        logits_parts.append(logits)
+    features = jnp.concatenate(features_parts, axis=1)
+    logits = jnp.concatenate(logits_parts, axis=1)
+    return (features.reshape(1, seq_dev, images, width), logits.reshape(1, seq_dev, images))
+
+
+def teach(teacher_in, mixed, qkv_full, qk_gain_full, out_full, critic_in, critic_out, n_replica):
+    seq_dev, images, width = teacher_in.shape
     heads_all = qkv_full.shape[2]
     head_size = qkv_full.shape[3]
     projected = jnp.einsum(
@@ -130,8 +152,6 @@
     pairs_all = images * heads_all
     grouped = projected.reshape(3, pairs_all, seq_dev, head_size)
     whole = lax.all_to_all(grouped, "expert", split_axis=1, concat_axis=2, tiled=True)
-    pairs_local = whole.shape[1]
-    seq_len = whole.shape[2]
     attended = attention(whole, head_size ** (-0.5))
     gathered_heads = lax.all_to_all(attended, "expert", split_axis=1, concat_axis=0, tiled=True)
     gathered_heads = gathered_heads.reshape(images, heads_all, seq_dev, head_size)
@@ -145,11 +165,11 @@
             out_full[low:low + heads_part],
             preferred_element_type=jnp.float32,
         ).astype(jnp.bfloat16).astype(jnp.float32)
-    features = (
-        mixed.reshape(seq_dev, images, width).astype(jnp.float32) + projected_out
-    ).astype(jnp.bfloat16)
+    features = (mixed.astype(jnp.float32) + projected_out).astype(jnp.bfloat16)
     critic_hidden = jax.nn.gelu(
-        jnp.dot(features.reshape(tok_count, width), critic_in, preferred_element_type=jnp.float32),
+        jnp.dot(
+            features.reshape(seq_dev * images, width), critic_in, preferred_element_type=jnp.float32
+        ),
         approximate=True,
     )
     logits = jnp.dot(
@@ -158,7 +178,7 @@
         precision=lax.Precision.HIGHEST,
         preferred_element_type=jnp.float32,
     )
-    return (features.reshape(1, seq_dev, images, width), logits.reshape(1, seq_dev, images))
+    return features, logits.reshape(seq_dev, images)
 
 
 def solution(mesh):

time: 810 us -> 746 us (0.921)
  blocking collectives: 180 us -> 129 us
  starting transfers between devices: 10.7 us -> 23.9 us
  matrix products: 133 us -> 121 us
  local copies, waits for them, and re-layouts: 90.1 us -> 78.7 us
    all_to_all x1 -> x0, blocking collectives: 51.8 us -> none  [local(): lax.all_to_all(attended, 'expert', split_axis=1, concat_axis=0, tiled=True)]
    dot_general x7 -> x12, matrix products: 46.8 us -> 14.7 us  [the longest x8 9.93 us: teach(): jnp.einsum('ihse,hed->sid', gathered_heads[:, low:low + heads_part], out_...]
    unnamed x0 -> x2, matrix products: none -> 27.8 us
    all_to_all x1 -> x4, starting transfers between devices: 4.92 us -> 18 us  [the longest x2 9.61 us: teach(): lax.all_to_all(attended, 'expert', split_axis=1, concat_axis=0, tiled=True)]
    all_to_all x1 -> x4, waiting for transfers between devices: 137 us -> 130 us  [the longest x2 105 us: teach(): lax.all_to_all(grouped, 'expert', split_axis=1, concat_axis=2, tiled=True)]
    pallas_call x1 -> x2, Pallas kernels: 44.7 us -> 46.5 us  [attention(): pl.pallas_call(functools.partial(attention_kernel, scale=scale), grid=(pa...]
    unnamed x34 -> x33, local copies, waits for them, and re-layouts: 18.2 us -> 18.6 us
  transfers between devices with their start and end apart: 7 -> 10, of which waited for: 3 -> 5; matrix products, arithmetic and copies ran while one was open for 22% -> 25% of each run, Pallas kernels for 6% -> 6%
where the time goes in v5:
time: 746 us; the launch traced here: 736 us
  waiting for transfers between devices  285 us (38%)
  blocking collectives  129 us (17%)
  matrix products  121 us (16%)
  local copies, waits for them, and re-layouts  78.7 us (11%)
  Pallas kernels  46.5 us (6%)
  other arithmetic  38 us (5%)
  starting transfers between devices  23.9 us (3%)
  between operations  14.7 us (2%)
    all_to_all x1, blocking collectives, local(): lax.all_to_all(outgoing, 'expert', split_axis=0, concat_axis=0, tiled=True)  123 us
    all_to_all x1, waiting for transfers between devices, local(): lax.all_to_all(results, 'expert', split_axis=0, concat_axis=0, tiled=True)  110 us
    all_to_all x2, waiting for transfers between devices, teach(): lax.all_to_all(grouped, 'expert', split_axis=1, concat_axis=2, tiled=True)  105 us
    pallas_call x2, Pallas kernels, attention(): pl.pallas_call(functools.partial(attention_kernel, scale=scale), grid=(pa...  46.5 us
    all_gather x1, waiting for transfers between devices, local(): down_full = lax.all_gather(expert_down, 'rep', axis=1, tiled=True)  41.7 us
    dot_general x4, matrix products, local(): jnp.einsum('sjcf,jfd->sjcd', hidden[..., low:low + ff_part], down_full[:,...  30.8 us
    unnamed x2, matrix products  27.8 us
    all_to_all x2, waiting for transfers between devices, teach(): lax.all_to_all(attended, 'expert', split_axis=1, concat_axis=0, tiled=True)  25.3 us
  transfers between devices with their start and end apart: 10, of which 5 were waited for; matrix products, arithmetic and copies ran while one was open for 25% of the time, Pallas kernels for 6%

profile of v5, /device:TPU:0, one launch (start us, length us, event | category | flops | bytes accessed | tf_op | source)
XLA Modules:
  0.0 736.4 jit_solution(1941580373928219050)
XLA Ops:
  8.0 0.7 all-gather.6.cloned.1.call-update
  8.7 0.7 all-gather.10.cloned.1.call-update
  9.4 10.8 %copy.94 = bf16[2048,3,4,128]{0,3,2,1:T(8,128)(2,1)} copy(bf16[2048,3,4,128]{3,2,1,0:T(4,128)(2,1)} %param.21) | data formatting | bytes 12582912 | tf_op args[8]
  21.8 4.5 reduce-window.6
  27.4 0.9 copy_convert_fusion
  28.4 5.3 copy.86
  33.7 6.1 reshape.393
  39.7 1.2 multiply_reduce_fusion.1
  41.8 5.6 convolution_convert_fusion
  47.3 123.1 %all_to_all.76 = bf16[8,160,2048]{2,1,0:T(8,128)(2,1)} all-to-all(bf16[8,160,2048]{2,1,0:T(8,128)(2,1)S(1)} %bitcast.303), channel_id=1, replica_groups=mesh['expert'=8,'rep'=4] {'expert'}, dimensions={0} | all-to-all | bytes 10485760 | tf_op jit(solution)/shard_map/all_to_all | solution.py:95
  170.5 15.2 %fusion = f32[2,8,80,1408]{3,2,1,0:T(8,128)} fusion(bf16[2,2048,1408]{1,2,0:T(8,128)(2,1)} %all-gather.8.cloned.1.call-done, bf16[8,2,80,2048]{3,2,1,0:T(8,128)(2,1)} %bitcast.301), kind=kOutput, calls=%fused_computation | convolution fusion | flops 7381975040 | bytes 23986176 | tf_op jit(solution)/shard_map/sjcd,jdf->sjcf/dot_general | solution.py:100
  185.7 16.5 %fusion.4 = bf16[8,2,80,1408]{3,2,0,1:T(8,128)(2,1)} fusion(f32[2,8,80,1408]{3,2,1,0:T(8,128)} %fusion, bf16[2,2048,1408]{1,2,0:T(8,128)(2,1)} %all-gather.6.cloned.1.call-done, bf16[8,2,80,2048]{3,2,1,0:T(8,128)(2,1)} %bitcast.302), kind=kOutput, calls=%fused_computation.7 | convolution fusion | flops 7392788480 | bytes 27590656 | tf_op jit(solution)/shard_map/sjcd,jdf->sjcf/dot_general | solution.py:97
  202.2 41.7 %all-gather.10.cloned.1.call-done = bf16[2,1408,2048]{2,1,0:T(8,128)(2,1)} async-done(((bf16[2,352,2048]{2,1,0:T(8,128)(2,1)}), bf16[2,1408,2048]{2,1,0:T(8,128)(2,1)}) %all-gather.10.cloned.1.call-update) | async-done | bytes 11534352 | tf_op jit(solution)/shard_map/all_gather | solution.py:78
  243.9 5.3 fusion.19
  249.2 6.8 fusion.20
  256.0 7.8 %fusion.18 = bf16[2,8,80,2048]{3,2,1,0:T(8,128)(2,1)} fusion(bf16[2,1408,2048]{2,1,0:T(8,128)(2,1)} %all-gather.10.cloned.1.call-done, bf16[8,2,80,1408]{3,2,0,1:T(8,128)(2,1)S(1)} %copy-done.13), kind=kOutput, calls=%fused_computation.33 | convolution fusion | flops 1845493760 | bytes 9109504 | tf_op jit(solution)/shard_map/sjcf,jfd->sjcd/dot_general | solution.py:107
  263.8 10.9 %fusion.8 = bf16[8,2,80,2048]{3,2,0,1:T(8,128)(2,1)S(1)} fusion(bf16[2,8,80,2048]{3,2,1,0:T(8,128)(2,1)} %fusion.18, bf16[2,8,80,2048]{3,2,1,0:T(8,128)(2,1)S(1)} %fusion.19, bf16[2,8,80,2048]{3,2,1,0:T(8,128)(2,1)} %fusion.20, bf16[2,1408,2048]{2,1,0:T(8,128)(2,1)} %all-gather.10.cloned.1.call-done, bf16[8,2,80,1408]{3,2,0,1:T(8,128)(2,1)} %fusion.4), kind=kOutput, calls=%fused_computation.13 | convolution fusion | flops 1869086720 | bytes 24838144 | tf_op jit(solution)/shard_map/sjcf,jfd->sjcd/dot_general | solution.py:107
  274.7 3.1 copy.90
  277.7 5.7 all-to-all-start.1
  284.0 5.4 all_gather.22
  289.4 110.2 %all-to-all-done.1 = bf16[8,160,2048]{2,1,0:T(8,128)(2,1)} async-done(((bf16[8,160,2048]{2,1,0:T(8,128)(2,1)}), bf16[8,160,2048]{2,1,0:T(8,128)(2,1)}, u32[]{:S(2)}, u32[]{:S(2)}) %all-to-all-start.1) | async-done | bytes 5242912 | tf_op jit(solution)/shard_map/all_to_all | solution.py:114
  399.6 10.5 %fusion.15 = f32[1024,2048]{1,0:T(8,128)} fusion(bf16[1280,2048]{1,0:T(8,128)(2,1)} %bitcast.21, f32[1024]{0:T(1024)S(1)} %mul.253, s32[1024]{0:T(1024)S(1)} %multiply_add_fusion), kind=kOutput, calls=%fused_computation.20 | convolution fusion | flops 5372116992 | bytes 13639680 | tf_op jit(solution)/shard_map/dot_general | solution.py:117
  410.1 10.6 %reshape.373 = f32[512,2,2048]{2,1,0:T(2,128)} reshape(f32[1024,2048]{1,0:T(8,128)} %fusion.15) | data formatting | bytes 16777216 | tf_op jit(solution)/shard_map/reshape | solution.py:118
  420.7 13.4 %reduce_sum.94 = f32[512,2048]{1,0:T(8,128)} reduce(f32[512,2,2048]{2,1,0:T(2,128)} %reshape.373, f32[]{:T(128)} %constant.27.clone.1), dimensions={1}, to_apply=%region_5.6 | reduce | flops 1048576 | bytes 12582916 | tf_op jit(solution)/shard_map/reduce_sum | solution.py:118
  434.1 5.8 reduce_sum.96
  439.9 6.0 reduce_sum.95
  446.0 5.8 multiply_reduce_fusion
  451.8 5.4 multiply_convert_fusion
  457.2 15.6 %fusion.82 = f32[256,6144]{0,1:S(1)} fusion(bf16[2048,6144]{0,1:T(8,128)(2,1)} %bitcast.318, bf16[256,2,2048]{2,0,1:T(8,128)(2,1)} %get-tuple-element.14), kind=kOutput, calls=%fused_computation.125 | convolution fusion | flops 6442450944 | bytes 32505856
  472.8 12.2 %fusion.81 = f32[256,6144]{0,1:S(1)} fusion(bf16[2048,6144]{0,1:T(8,128)(2,1)} %bitcast.319, bf16[256,2,2048]{2,0,1:T(8,128)(2,1)S(1)} %copy-done.6), kind=kOutput, calls=%fused_computation.123 | convolution fusion | flops 6442450944 | bytes 32505856
  486.1 1.6 copy-done.4
  487.7 2.3 fusion.77
  490.3 2.0 copy.98
  492.3 3.9 all-to-all-start.2
  496.8 1.7 fusion.80
  498.5 1.9 pad_maximum_fusion.1
  500.4 2.1 copy.102
  502.5 64.6 %all-to-all-done.2 = bf16[3,16,256,128]{2,3,0,1:T(8,128)(2,1)S(1)} async-done(((bf16[3,16,256,128]{2,3,0,1:T(8,128)(2,1)}), bf16[3,16,256,128]{2,3,0,1:T(8,128)(2,1)S(1)}, u32[]{:S(2)}, u32[]{:S(2)}) %all-to-all-start.2) | async-done | bytes 3145760 | tf_op jit(solution)/shard_map/all_to_all | solution.py:154
  567.1 4.5 all-to-all-start.4
  571.6 2.8 copy.99
  574.4 23.2 %shard_map.140 = bf16[2,2048,128]{2,1,0:T(8,128)(2,1)} custom-call(bf16[3,2,2048,128]{3,2,1,0:T(8,128)(2,1)} %bitcast.287, bf16[3,2,2048,128]{3,2,1,0:T(8,128)(2,1)} %bitcast.288, bf16[3,2,2048,128]{3,2,1,0:T(8,128)(2,1)} %bitcast.289), custom_call_target="tpu_custom_call" | custom-call | tf_op jit(solution)/shard_map/pallas_call | solution.py:38
  597.6 3.6 copy.100
  601.2 40.5 %all-to-all-done.4 = bf16[3,16,256,128]{2,3,0,1:T(8,128)(2,1)} async-done(((bf16[3,16,256,128]{2,3,0,1:T(8,128)(2,1)}), bf16[3,16,256,128]{2,3,0,1:T(8,128)(2,1)}, u32[]{:S(2)}, u32[]{:S(2)}) %all-to-all-start.4) | async-done | bytes 3145760 | tf_op jit(solution)/shard_map/all_to_all | solution.py:154
  641.8 3.6 all-to-all-start.3
  645.4 4.7 copy.103
  650.1 23.2 %shard_map.141 = bf16[2,2048,128]{2,1,0:T(8,128)(2,1)} custom-call(bf16[3,2,2048,128]{3,2,1,0:T(8,128)(2,1)} %bitcast.290, bf16[3,2,2048,128]{3,2,1,0:T(8,128)(2,1)} %bitcast.291, bf16[3,2,2048,128]{3,2,1,0:T(8,128)(2,1)} %bitcast.292), custom_call_target="tpu_custom_call" | custom-call | tf_op jit(solution)/shard_map/pallas_call | solution.py:38
  673.3 3.6 copy.104
  677.0 6.0 all-to-all-start.5
  683.2 25.3 %all-to-all-done.5 = bf16[2,2048,128]{2,0,1:T(2,128)(2,1)S(1)} async-done(((bf16[2,2048,128]{2,0,1:T(2,128)(2,1)}), bf16[2,2048,128]{2,0,1:T(2,128)(2,1)S(1)}, u32[]{:S(2)}, u32[]{:S(2)}) %all-to-all-start.5) | async-done | bytes 1048608 | tf_op jit(solution)/shard_map/all_to_all | solution.py:156
  708.8 2.5 fusion.50
  711.2 2.9 fusion.49
  714.1 0.8 fusion.47
  714.9 0.8 copy-done.5
  715.7 0.8 fusion.45
  716.5 0.7 copy-done.11
  717.3 1.5 fusion.67
  718.7 0.7 fusion.40
  719.5 0.8 fusion.39
  720.3 0.7 fusion.37
  721.0 0.8 fusion.35
  721.8 1.5 fusion.74
  723.5 0.9 convolution_bitcast_fusion.9
  724.4 0.9 convolution_bitcast_fusion.8
  725.3 3.5 copy.106
  (75 shorter events, 8.0 us)
Async XLA Ops:
  7.2 716.3 %copy-start = (f32[1024]{0:T(1024)S(1)}, f32[1024]{0:T(1024)}, u32[]{:S(2)}) copy-start(f32[1024]{0:T(1024)} %param.25) | copy-start | bytes 12292
  7.2 163.3 %all-gather.8.cloned.1.call-start = ((), (), s32[]{:S(2)}) async-start(), calls=%async_computation.7 | async-start | bytes 14417920 | tf_op jit(solution)/shard_map/all_gather | solution.py:77
  7.9 177.8 %all-gather.6.cloned.1.call-start = ((), (), s32[]{:S(2)}) async-start(), calls=%async_computation.6 | async-start | bytes 14417920 | tf_op jit(solution)/shard_map/all_gather | solution.py:76
  8.7 235.2 %all-gather.10.cloned.1.call-start = ((), (), s32[]{:S(2)}) async-start(), calls=%async_computation.8 | async-start | bytes 14417920 | tf_op jit(solution)/shard_map/all_gather | solution.py:78
  9.4 447.8 %all-gather.12.cloned.1.call-start = ((), (), s32[]{:S(2)}) async-start(), calls=%async_computation.9 | async-start | bytes 31457280 | tf_op jit(solution)/shard_map/all_gather | solution.py:79
  20.2 0.7 copy-start.7
  20.3 7.2 copy-start.2
  39.7 2.0 copy-start.12
  243.9 5.3 copy-start.13
  277.7 5.7 copy-start.9
  277.7 6.3 copy-start.10
  277.7 121.9 %all-to-all-start.1 = ((bf16[8,160,2048]{2,1,0:T(8,128)(2,1)}), bf16[8,160,2048]{2,1,0:T(8,128)(2,1)}, u32[]{:S(2)}, u32[]{:S(2)}) async-start(bf16[8,160,2048]{2,1,0:T(8,128)(2,1)} %bitcast.293), calls=%async_computation.1 | async-start | bytes 10485760 | tf_op jit(solution)/shard_map/all_to_all | solution.py:114
  446.0 5.8 copy-start.3
  446.0 5.8 copy-start.8
  457.2 15.7 %copy-start.6 = (bf16[256,2,2048]{2,0,1:T(8,128)(2,1)S(1)}, bf16[256,2,2048]{2,0,1:T(8,128)(2,1)}, u32[]{:S(2)}) copy-start(bf16[256,2,2048]{2,0,1:T(8,128)(2,1)} %get-tuple-element.14) | copy-start | bytes 6291460
  485.0 2.7 copy-start.4
  492.3 74.8 %all-to-all-start.2 = ((bf16[3,16,256,128]{2,3,0,1:T(8,128)(2,1)}), bf16[3,16,256,128]{2,3,0,1:T(8,128)(2,1)S(1)}, u32[]{:S(2)}, u32[]{:S(2)}) async-start(bf16[3,16,256,128]{2,3,0,1:T(8,128)(2,1)} %copy.98), calls=%async_computation.2 | async-start | bytes 6291456 | tf_op jit(solution)/shard_map/all_to_all | solution.py:154
  496.2 212.5 %all-gather.14.cloned.1.call-start = ((), (), s32[]{:S(2)}) async-start(), calls=%async_computation.10 | async-start | bytes 10485760 | tf_op jit(solution)/shard_map/all_gather | solution.py:81
  567.1 74.7 %all-to-all-start.4 = ((bf16[3,16,256,128]{2,3,0,1:T(8,128)(2,1)}), bf16[3,16,256,128]{2,3,0,1:T(8,128)(2,1)}, u32[]{:S(2)}, u32[]{:S(2)}) async-start(bf16[3,16,256,128]{2,3,0,1:T(8,128)(2,1)} %copy.102), calls=%async_computation.4 | async-start | bytes 6291456 | tf_op jit(solution)/shard_map/all_to_all | solution.py:154
  641.8 35.2 %all-to-all-start.3 = ((bf16[2,2048,128]{2,0,1:T(2,128)(2,1)}), bf16[2,2048,128]{2,0,1:T(2,128)(2,1)S(1)}, u32[]{:S(2)}, u32[]{:S(2)}) async-start(bf16[2,2048,128]{2,0,1:T(2,128)(2,1)} %copy.100), calls=%async_computation.3 | async-start | bytes 2097152 | tf_op jit(solution)/shard_map/all_to_all | solution.py:156
  677.0 31.5 %all-to-all-start.5 = ((bf16[2,2048,128]{2,0,1:T(2,128)(2,1)}), bf16[2,2048,128]{2,0,1:T(2,128)(2,1)S(1)}, u32[]{:S(2)}, u32[]{:S(2)}) async-start(bf16[2,2048,128]{2,0,1:T(2,128)(2,1)} %copy.104), calls=%async_computation.5 | async-start | bytes 2097152 | tf_op jit(solution)/shard_map/all_to_all | solution.py:156
  708.7 5.4 copy-start.1
  714.1 1.6 copy-start.5
  714.9 2.3 copy-start.11
Sparse Core Ops, SparseCore 0:
  9.5 78.8 all-gather.7
  90.0 76.1 all-gather.5
  167.7 76.1 all-gather.9
  245.3 154.8 all-gather.11
  498.3 59.1 all-gather.13

commit v6 on v5

--- a/solution.py
+++ b/solution.py
@@ -47,6 +47,18 @@
         out_shape=jax.ShapeDtypeStruct((pairs, seq_len, head_size), whole.dtype),
         interpret=interpret,
     )(whole, whole, whole)
+
+
+def gather_rep(values, axis, count):
+    if count % 2 != 0 or count < 4:
+        return lax.all_gather(values, "rep", axis=axis, tiled=True)
+    half = count // 2
+    across = [[i, i + half] for i in range(half)]
+    within = [[2 * i, 2 * i + 1] for i in range(half)] if half == 2 else None
+    if within is None:
+        return lax.all_gather(values, "rep", axis=axis, tiled=True)
+    first = lax.all_gather(values, "rep", axis=axis, tiled=True, axis_index_groups=across)
+    return lax.all_gather(first, "rep", axis=axis, tiled=True, axis_index_groups=within)
 
 
 def local(
@@ -73,9 +85,9 @@
     exp_local = expert_gate.shape[0]
     expert_total = exp_local * n_owner
     capacity = max(2, tok_count * 10 // (4 * expert_total))
-    gate_full = lax.all_gather(expert_gate, "rep", axis=2, tiled=True)
-    up_full = lax.all_gather(expert_up, "rep", axis=2, tiled=True)
-    down_full = lax.all_gather(expert_down, "rep", axis=1, tiled=True)
+    gate_full = gather_rep(expert_gate, 2, n_replica)
+    up_full = gather_rep(expert_up, 2, n_replica)
+    down_full = gather_rep(expert_down, 1, n_replica)
     qkv_full = lax.all_gather(teacher_qkv, "rep", axis=2, tiled=True)
     qk_gain_full = lax.all_gather(qk_gain, "rep", axis=1, tiled=True)
     out_full = lax.all_gather(teacher_out, "rep", axis=0, tiled=True)
@@ -114,8 +126,14 @@
     returned = lax.all_to_all(results, "expert", split_axis=0, concat_axis=0, tiled=True).reshape(
         expert_total * capacity, width
     )
-    picked = jnp.dot(assign_rows, returned, preferred_element_type=jnp.float32) * gate_value[:, None]
-    combined = picked.reshape(tok_count, 2, width).sum(axis=1)
+    picked = jnp.einsum(
+        "tkr,rd->ktd",
+        assign_rows.reshape(tok_count, 2, expert_total * capacity),
+        returned,
+        preferred_element_type=jnp.float32,
+    )
+    gate_pair = gate_value.reshape(tok_count, 2)
+    combined = picked[0] * gate_pair[:, 0:1] + picked[1] * gate_pair[:, 1:2]
     mixed = (residual + combined).astype(jnp.bfloat16)
     teacher_in = norm_rows(mixed.astype(jnp.float32), teacher_gain).astype(jnp.bfloat16)
     teacher_in = teacher_in.reshape(seq_dev, images, width)

time: 746 us -> 917 us (1.23)
  waiting for transfers between devices: 285 us -> 471 us
  matrix products: 121 us -> 111 us
    all_gather x3 -> x6, waiting for transfers between devices: 41.7 us -> 229 us  [the longest x3 229 us: gather_rep(): lax.all_gather(values, 'rep', axis=axis, tiled=True, axis_index_groups=ac...]
    squeeze x0 -> x4, local copies, waits for them, and re-layouts: none -> 23.4 us  [local(): combined = picked[0] * gate_pair[:, 0:1] + picked[1] * gate_pair[:, 1:2]]
    reduce_sum x1 -> x0, other arithmetic: 13.4 us -> none  [local(): combined = picked.reshape(tok_count, 2, width).sum(axis=1)]
    reduce_sum x2 -> x0, local copies, waits for them, and re-layouts: 11.8 us -> none  [local(): combined = picked.reshape(tok_count, 2, width).sum(axis=1)]
    reshape x2 -> x0, local copies, waits for them, and re-layouts: 10.9 us -> none  [the longest x1 10.6 us: local(): combined = picked.reshape(tok_count, 2, width).sum(axis=1)]
    unnamed x33 -> x35, local copies, waits for them, and re-layouts: 18.6 us -> 18.7 us
  transfers between devices with their start and end apart: 10 -> 13, of which waited for: 5 -> 7; matrix products, arithmetic and copies ran while one was open for 25% -> 19% of each run, Pallas kernels for 6% -> 5%
where the time goes in v6:
time: 917 us; the launch traced here: 908 us
  waiting for transfers between devices  471 us (51%)
  blocking collectives  126 us (14%)
  matrix products  111 us (12%)
  local copies, waits for them, and re-layouts  83.9 us (9%)
  Pallas kernels  46.5 us (5%)
  other arithmetic  31.3 us (3%)
  starting transfers between devices  23.1 us (3%)
  between operations  14.8 us (2%)
    all_gather x3, waiting for transfers between devices, gather_rep(): lax.all_gather(values, 'rep', axis=axis, tiled=True, axis_index_groups=ac...  229 us
    all_to_all x1, blocking collectives, local(): lax.all_to_all(outgoing, 'expert', split_axis=0, concat_axis=0, tiled=True)  121 us
    all_to_all x1, waiting for transfers between devices, local(): lax.all_to_all(results, 'expert', split_axis=0, concat_axis=0, tiled=True)  109 us
    all_to_all x2, waiting for transfers between devices, teach(): lax.all_to_all(grouped, 'expert', split_axis=1, concat_axis=2, tiled=True)  105 us
    pallas_call x2, Pallas kernels, attention(): pl.pallas_call(functools.partial(attention_kernel, scale=scale), grid=(pa...  46.5 us
    dot_general x4, matrix products, local(): jnp.einsum('sjcf,jfd->sjcd', hidden[..., low:low + ff_part], down_full[:,...  26.9 us
    all_to_all x2, waiting for transfers between devices, teach(): lax.all_to_all(attended, 'expert', split_axis=1, concat_axis=0, tiled=True)  25.3 us
    unnamed x2, matrix products  24.4 us
  transfers between devices with their start and end apart: 13, of which 7 were waited for; matrix products, arithmetic and copies ran while one was open for 19% of the time, Pallas kernels for 5%

profile of v6, /device:TPU:0, one launch (start us, length us, event | category | flops | bytes accessed | tf_op | source)
XLA Modules:
  0.0 908.1 jit_solution(641557920160901939)
XLA Ops:
  9.4 77.3 %all-gather.13.cloned.1.call-done = bf16[2,2048,704]{1,2,0:T(8,128)(2,1)} async-done(((bf16[2,2048,352]{1,2,0:T(8,128)(2,1)}), bf16[2,2048,704]{1,2,0:T(8,128)(2,1)}) %all-gather.13.cloned.1.call-update) | async-done | bytes 5767184 | tf_op jit(solution)/shard_map/all_gather | solution.py:60
  86.8 76.0 %all-gather.9.cloned.1.call-done = bf16[2,2048,704]{1,2,0:T(8,128)(2,1)} async-done(((bf16[2,2048,352]{1,2,0:T(8,128)(2,1)}), bf16[2,2048,704]{1,2,0:T(8,128)(2,1)}) %all-gather.9.cloned.1.call-update) | async-done | bytes 5767184 | tf_op jit(solution)/shard_map/all_gather | solution.py:60
  162.8 76.0 %all-gather.17.cloned.1.call-done = bf16[2,704,2048]{2,1,0:T(8,128)(2,1)} async-done(((bf16[2,352,2048]{2,1,0:T(8,128)(2,1)}), bf16[2,704,2048]{2,1,0:T(8,128)(2,1)}) %all-gather.17.cloned.1.call-update) | async-done | bytes 5767184 | tf_op jit(solution)/shard_map/all_gather | solution.py:60
  238.9 11.0 %copy.117 = bf16[2048,3,4,128]{0,3,2,1:T(8,128)(2,1)} copy(bf16[2048,3,4,128]{3,2,1,0:T(4,128)(2,1)} %param.21) | data formatting | bytes 12582912 | tf_op args[8]
  251.4 4.5 reduce-window.6
  257.0 0.9 copy_convert_fusion
  258.0 5.3 copy.103
  263.2 6.1 reshape.465
  269.4 1.2 multiply_reduce_fusion.1
  271.4 6.6 convolution_convert_fusion
  278.0 121.1 %all_to_all.76 = bf16[8,160,2048]{2,1,0:T(8,128)(2,1)} all-to-all(bf16[8,160,2048]{2,1,0:T(8,128)(2,1)S(1)} %bitcast.316), channel_id=1, replica_groups=mesh['expert'=8,'rep'=4] {'expert'}, dimensions={0} | all-to-all | bytes 10485760 | tf_op jit(solution)/shard_map/all_to_all | solution.py:107
  399.1 14.8 %fusion = f32[2,8,80,1408]{3,2,1,0:T(8,128)} fusion(bf16[2,2048,1408]{1,2,0:T(8,128)(2,1)} %all-gather.15.cloned.1.call-done, bf16[8,2,80,2048]{3,2,1,0:T(8,128)(2,1)} %bitcast.314), kind=kOutput, calls=%fused_computation | convolution fusion | flops 7381975040 | bytes 23986176 | tf_op jit(solution)/shard_map/sjcd,jdf->sjcf/dot_general | solution.py:112
  413.9 16.4 %fusion.4 = bf16[8,2,80,1408]{3,2,0,1:T(8,128)(2,1)} fusion(f32[2,8,80,1408]{3,2,1,0:T(8,128)} %fusion, bf16[2,2048,1408]{1,2,0:T(8,128)(2,1)} %all-gather.11.cloned.1.call-done, bf16[8,2,80,2048]{3,2,1,0:T(8,128)(2,1)} %bitcast.315), kind=kOutput, calls=%fused_computation.7 | convolution fusion | flops 7392788480 | bytes 27590656 | tf_op jit(solution)/shard_map/sjcd,jdf->sjcf/dot_general | solution.py:109
  430.3 5.3 fusion.26
  435.6 6.4 fusion.27
  442.0 6.7 fusion.25
  448.7 8.4 fusion.8
  457.1 2.9 copy.107
  460.0 4.9 all-to-all-start.1
  465.7 5.2 all_gather.34
  471.0 108.7 %all-to-all-done.1 = bf16[8,160,2048]{2,1,0:T(8,128)(2,1)} async-done(((bf16[8,160,2048]{2,1,0:T(8,128)(2,1)}), bf16[8,160,2048]{2,1,0:T(8,128)(2,1)}, u32[]{:S(2)}, u32[]{:S(2)}) %all-to-all-start.1) | async-done | bytes 5242912 | tf_op jit(solution)/shard_map/all_to_all | solution.py:126
  579.7 7.6 fusion.17
  587.3 3.8 fusion.107
  591.1 5.9 squeeze.16
  597.0 5.8 squeeze.14
  602.8 5.8 squeeze.17
  608.7 5.9 squeeze.15
  614.6 9.3 %multiply_reduce_fusion = f32[256,2]{0,1:T(2,128)S(1)} fusion(f32[256,2]{0,1:T(2,128)S(1)} %copy.111, f32[1,256,2,2048]{3,2,1,0:T(2,128)} %squeeze.17, f32[256,2]{0,1:T(2,128)S(1)} %copy.109, f32[1,256,2,2048]{3,2,1,0:T(2,128)} %squeeze.16, bf16[1,256,2,2048]{3,2,1,0:T(2,128)(2,1)S(1)} %copy-done.2), kind=kLoop, calls=%fused_computation.33 | loop fusion | flops 9436672 | bytes 10491904 | tf_op jit(solution)/shard_map/reduce_sum | solution.py:11
  623.9 8.2 multiply_convert_fusion
  632.1 12.4 %fusion.89 = f32[256,6144]{0,1:S(1)} fusion(bf16[2048,6144]{0,1:T(8,128)(2,1)} %bitcast.331, bf16[256,2,2048]{2,0,1:T(8,128)(2,1)} %get-tuple-element.16), kind=kOutput, calls=%fused_computation.132 | convolution fusion | flops 6442450944 | bytes 32505856
  644.5 12.0 %fusion.88 = f32[256,6144]{0,1:S(1)} fusion(bf16[2048,6144]{0,1:T(8,128)(2,1)} %bitcast.332, bf16[256,2,2048]{2,0,1:T(8,128)(2,1)S(1)} %copy-done.7), kind=kOutput, calls=%fused_computation.130 | convolution fusion | flops 6442450944 | bytes 32505856
  657.5 1.7 copy-done.5
  659.2 2.7 fusion.84
  662.2 2.0 copy.121
  664.2 3.6 all-to-all-start.2
  668.6 1.7 fusion.87
  670.3 1.9 pad_maximum_fusion.1
  672.2 2.1 copy.125
  674.3 64.4 %all-to-all-done.2 = bf16[3,16,256,128]{2,3,0,1:T(8,128)(2,1)S(1)} async-done(((bf16[3,16,256,128]{2,3,0,1:T(8,128)(2,1)}), bf16[3,16,256,128]{2,3,0,1:T(8,128)(2,1)S(1)}, u32[]{:S(2)}, u32[]{:S(2)}) %all-to-all-start.2) | async-done | bytes 3145760 | tf_op jit(solution)/shard_map/all_to_all | solution.py:172
  738.7 4.5 all-to-all-start.4
  743.2 2.8 copy.122
  746.0 23.2 %shard_map.140 = bf16[2,2048,128]{2,1,0:T(8,128)(2,1)} custom-call(bf16[3,2,2048,128]{3,2,1,0:T(8,128)(2,1)} %bitcast.300, bf16[3,2,2048,128]{3,2,1,0:T(8,128)(2,1)} %bitcast.301, bf16[3,2,2048,128]{3,2,1,0:T(8,128)(2,1)} %bitcast.302), custom_call_target="tpu_custom_call" | custom-call | tf_op jit(solution)/shard_map/pallas_call | solution.py:38
  769.2 3.6 copy.123
  772.8 40.5 %all-to-all-done.4 = bf16[3,16,256,128]{2,3,0,1:T(8,128)(2,1)} async-done(((bf16[3,16,256,128]{2,3,0,1:T(8,128)(2,1)}), bf16[3,16,256,128]{2,3,0,1:T(8,128)(2,1)}, u32[]{:S(2)}, u32[]{:S(2)}) %all-to-all-start.4) | async-done | bytes 3145760 | tf_op jit(solution)/shard_map/all_to_all | solution.py:172
  813.3 3.6 all-to-all-start.3
  817.0 4.7 copy.126
  821.6 23.2 %shard_map.141 = bf16[2,2048,128]{2,1,0:T(8,128)(2,1)} custom-call(bf16[3,2,2048,128]{3,2,1,0:T(8,128)(2,1)} %bitcast.303, bf16[3,2,2048,128]{3,2,1,0:T(8,128)(2,1)} %bitcast.304, bf16[3,2,2048,128]{3,2,1,0:T(8,128)(2,1)} %bitcast.305), custom_call_target="tpu_custom_call" | custom-call | tf_op jit(solution)/shard_map/pallas_call | solution.py:38
  844.9 3.6 copy.127
  848.5 6.2 all-to-all-start.5
  854.9 25.3 %all-to-all-done.5 = bf16[2,2048,128]{2,0,1:T(2,128)(2,1)S(1)} async-done(((bf16[2,2048,128]{2,0,1:T(2,128)(2,1)}), bf16[2,2048,128]{2,0,1:T(2,128)(2,1)S(1)}, u32[]{:S(2)}, u32[]{:S(2)}) %all-to-all-start.5) | async-done | bytes 1048608 | tf_op jit(solution)/shard_map/all_to_all | solution.py:174
  880.4 2.5 fusion.57
  882.9 2.9 fusion.56
  885.9 0.8 fusion.54
  886.6 0.8 copy-done.6
  887.4 0.8 fusion.52
  888.2 0.7 copy-done.12
  889.0 1.5 fusion.74
  891.2 0.7 fusion.46
  891.9 0.8 fusion.44
  892.7 0.8 fusion.42
  893.5 1.5 fusion.81
  895.2 0.9 convolution_bitcast_fusion.9
  896.1 0.9 convolution_bitcast_fusion.8
  897.0 3.5 copy.129
  (91 shorter events, 10.7 us)
Async XLA Ops:
  7.2 888.0 %copy-start = (f32[1024]{0:T(1024)S(1)}, f32[1024]{0:T(1024)}, u32[]{:S(2)}) copy-start(f32[1024]{0:T(1024)} %param.25) | copy-start | bytes 12292
  7.2 79.6 %all-gather.13.cloned.1.call-start = ((), (), s32[]{:S(2)}) async-start(), calls=%async_computation.8 | async-start | bytes 8650752 | tf_op jit(solution)/shard_map/all_gather | solution.py:60
  7.9 154.8 %all-gather.9.cloned.1.call-start = ((), (), s32[]{:S(2)}) async-start(), calls=%async_computation.6 | async-start | bytes 8650752 | tf_op jit(solution)/shard_map/all_gather | solution.py:60
  8.7 230.1 %all-gather.17.cloned.1.call-start = ((), (), s32[]{:S(2)}) async-start(), calls=%async_computation.10 | async-start | bytes 8650752 | tf_op jit(solution)/shard_map/all_gather | solution.py:60
  9.4 389.7 %all-gather.15.cloned.1.call-start = ((), (), s32[]{:S(2)}) async-start(), calls=%async_computation.9 | async-start | bytes 17301504 | tf_op jit(solution)/shard_map/all_gather | solution.py:61
  86.8 327.1 %all-gather.11.cloned.1.call-start = ((), (), s32[]{:S(2)}) async-start(), calls=%async_computation.7 | async-start | bytes 17301504 | tf_op jit(solution)/shard_map/all_gather | solution.py:61
  162.8 267.5 %all-gather.19.cloned.1.call-start = ((), (), s32[]{:S(2)}) async-start(), calls=%async_computation.11 | async-start | bytes 17301504 | tf_op jit(solution)/shard_map/all_gather | solution.py:61
  238.8 393.3 %all-gather.21.cloned.1.call-start = ((), (), s32[]{:S(2)}) async-start(), calls=%async_computation.12 | async-start | bytes 31457280 | tf_op jit(solution)/shard_map/all_gather | solution.py:91
  249.8 0.7 copy-start.8
  249.8 7.2 copy-start.2
  263.2 8.2 copy-start.13
  430.2 5.3 copy-start.14
  460.0 4.9 copy-start.10
  460.0 5.7 copy-start.11
  460.0 119.6 %all-to-all-start.1 = ((bf16[8,160,2048]{2,1,0:T(8,128)(2,1)}), bf16[8,160,2048]{2,1,0:T(8,128)(2,1)}, u32[]{:S(2)}, u32[]{:S(2)}) async-start(bf16[8,160,2048]{2,1,0:T(8,128)(2,1)} %bitcast.306), calls=%async_computation.1 | async-start | bytes 10485760 | tf_op jit(solution)/shard_map/all_to_all | solution.py:126
  614.6 9.3 %copy-start.3 = (f32[256,2,2048]{2,1,0:T(2,128)S(1)}, f32[256,2,2048]{2,1,0:T(2,128)}, u32[]{:S(2)}) copy-start(f32[256,2,2048]{2,1,0:T(2,128)} %squeeze.14) | copy-start | bytes 12582916
  614.6 9.4 %copy-start.4 = (f32[256,2,2048]{2,1,0:T(2,128)S(1)}, f32[256,2,2048]{2,1,0:T(2,128)}, u32[]{:S(2)}) copy-start(f32[256,2,2048]{2,1,0:T(2,128)} %squeeze.15) | copy-start | bytes 12582916
  614.6 9.4 %copy-start.9 = (f32[2048]{0:T(1024)S(1)}, f32[2048]{0:T(1024)}, u32[]{:S(2)}) copy-start(f32[2048]{0:T(1024)} %param.20) | copy-start | bytes 24580
  632.1 12.4 %copy-start.7 = (bf16[256,2,2048]{2,0,1:T(8,128)(2,1)S(1)}, bf16[256,2,2048]{2,0,1:T(8,128)(2,1)}, u32[]{:S(2)}) copy-start(bf16[256,2,2048]{2,0,1:T(8,128)(2,1)} %get-tuple-element.16) | copy-start | bytes 6291460
  656.5 2.7 copy-start.5
  664.2 74.5 %all-to-all-start.2 = ((bf16[3,16,256,128]{2,3,0,1:T(8,128)(2,1)}), bf16[3,16,256,128]{2,3,0,1:T(8,128)(2,1)S(1)}, u32[]{:S(2)}, u32[]{:S(2)}) async-start(bf16[3,16,256,128]{2,3,0,1:T(8,128)(2,1)} %copy.121), calls=%async_computation.2 | async-start | bytes 6291456 | tf_op jit(solution)/shard_map/all_to_all | solution.py:172
  667.8 212.6 %all-gather.23.cloned.1.call-start = ((), (), s32[]{:S(2)}) async-start(), calls=%async_computation.13 | async-start | bytes 10485760 | tf_op jit(solution)/shard_map/all_gather | solution.py:93
  738.7 74.7 %all-to-all-start.4 = ((bf16[3,16,256,128]{2,3,0,1:T(8,128)(2,1)}), bf16[3,16,256,128]{2,3,0,1:T(8,128)(2,1)}, u32[]{:S(2)}, u32[]{:S(2)}) async-start(bf16[3,16,256,128]{2,3,0,1:T(8,128)(2,1)} %copy.125), calls=%async_computation.4 | async-start | bytes 6291456 | tf_op jit(solution)/shard_map/all_to_all | solution.py:172
  813.3 35.2 %all-to-all-start.3 = ((bf16[2,2048,128]{2,0,1:T(2,128)(2,1)}), bf16[2,2048,128]{2,0,1:T(2,128)(2,1)S(1)}, u32[]{:S(2)}, u32[]{:S(2)}) async-start(bf16[2,2048,128]{2,0,1:T(2,128)(2,1)} %copy.123), calls=%async_computation.3 | async-start | bytes 2097152 | tf_op jit(solution)/shard_map/all_to_all | solution.py:174
  848.5 31.7 %all-to-all-start.5 = ((bf16[2,2048,128]{2,0,1:T(2,128)(2,1)}), bf16[2,2048,128]{2,0,1:T(2,128)(2,1)S(1)}, u32[]{:S(2)}, u32[]{:S(2)}) async-start(bf16[2,2048,128]{2,0,1:T(2,128)(2,1)} %copy.127), calls=%async_computation.5 | async-start | bytes 2097152 | tf_op jit(solution)/shard_map/all_to_all | solution.py:174
  880.4 5.4 copy-start.1
  885.8 1.6 copy-start.6
  886.6 2.3 copy-start.12
Sparse Core Ops, SparseCore 0:
  9.5 77.1 all-gather.12
  88.3 74.4 all-gather.8
  164.3 74.4 all-gather.16
  240.2 23.0 all-gather.14
  264.7 24.1 all-gather.10
  290.3 24.1 all-gather.18
  316.1 156.0 all-gather.20
  670.2 58.6 all-gather.22

commit v7 on v5

--- a/solution.py
+++ b/solution.py
@@ -86,8 +86,10 @@
     gate_value = gate_probs.reshape(2 * tok_count)
     target = chosen * capacity + slot_index
     rows_all = jnp.arange(expert_total * capacity, dtype=jnp.int32)
-    assign_rows = (target[:, None] == rows_all[None, :]).astype(jnp.bfloat16)
-    token_rows = assign_rows.reshape(tok_count, 2, expert_total * capacity).sum(axis=1)
+    target_pair = target.reshape(tok_count, 2)
+    first_rows = (target_pair[:, 0:1] == rows_all[None, :]).astype(jnp.bfloat16)
+    second_rows = (target_pair[:, 1:2] == rows_all[None, :]).astype(jnp.bfloat16)
+    token_rows = first_rows + second_rows
     outgoing = jnp.einsum(
         "tr,td->rd", token_rows, normed, preferred_element_type=jnp.float32
     ).astype(jnp.bfloat16)
@@ -114,8 +116,10 @@
     returned = lax.all_to_all(results, "expert", split_axis=0, concat_axis=0, tiled=True).reshape(
         expert_total * capacity, width
     )
-    picked = jnp.dot(assign_rows, returned, preferred_element_type=jnp.float32) * gate_value[:, None]
-    combined = picked.reshape(tok_count, 2, width).sum(axis=1)
+    gate_pair = gate_value.reshape(tok_count, 2)
+    combined = jnp.dot(first_rows, returned, preferred_element_type=jnp.float32) * gate_pair[
+        :, 0:1
+    ] + jnp.dot(second_rows, returned, preferred_element_type=jnp.float32) * gate_pair[:, 1:2]
     mixed = (residual + combined).astype(jnp.bfloat16)
     teacher_in = norm_rows(mixed.astype(jnp.float32), teacher_gain).astype(jnp.bfloat16)
     teacher_in = teacher_in.reshape(seq_dev, images, width)

time: 746 us -> 710 us (0.952)
  other arithmetic: 38 us -> 14.9 us
  local copies, waits for them, and re-layouts: 78.7 us -> 67.4 us
    reduce_sum x2 -> x0, other arithmetic: 14 us -> none  [the longest x1 13.4 us: local(): combined = picked.reshape(tok_count, 2, width).sum(axis=1)]
    reduce_sum x2 -> x0, local copies, waits for them, and re-layouts: 11.8 us -> none  [local(): combined = picked.reshape(tok_count, 2, width).sum(axis=1)]
    slice x2 -> x6, local copies, waits for them, and re-layouts: 0.21 us -> 8.82 us  [the longest x1 4.43 us: local(): mixed[:, sel]]
    convert_element_type x2 -> x1, local copies, waits for them, and re-layouts: 11.4 us -> 2.78 us  [local(): residual = tokens.reshape(tok_count, width).astype(jnp.float32)]
    all_to_all x2, waiting for transfers between devices: 25.3 us -> 17.8 us  [teach(): lax.all_to_all(attended, 'expert', split_axis=1, concat_axis=0, tiled=True)]
    unnamed x33 -> x37, local copies, waits for them, and re-layouts: 18.6 us -> 22.6 us
  transfers between devices with their start and end apart: 10 -> 10, of which waited for: 5 -> 5; matrix products, arithmetic and copies ran while one was open for 25% -> 21% of each run, Pallas kernels for 6% -> 7%
where the time goes in v7:
time: 710 us; the launch traced here: 703 us
  waiting for transfers between devices  285 us (40%)
  blocking collectives  128 us (18%)
  matrix products  122 us (17%)
  local copies, waits for them, and re-layouts  67.4 us (9%)
  Pallas kernels  46.5 us (7%)
  starting transfers between devices  23.8 us (3%)
  other arithmetic  14.9 us (2%)
  between operations  14.5 us (2%)
    all_to_all x1, blocking collectives, local(): lax.all_to_all(outgoing, 'expert', split_axis=0, concat_axis=0, tiled=True)  123 us
    all_to_all x1, waiting for transfers between devices, local(): lax.all_to_all(results, 'expert', split_axis=0, concat_axis=0, tiled=True)  110 us
    all_to_all x2, waiting for transfers between devices, teach(): lax.all_to_all(grouped, 'expert', split_axis=1, concat_axis=2, tiled=True)  105 us
    all_gather x1, waiting for transfers between devices, local(): down_full = lax.all_gather(expert_down, 'rep', axis=1, tiled=True)  48.9 us
    pallas_call x2, Pallas kernels, attention(): pl.pallas_call(functools.partial(attention_kernel, scale=scale), grid=(pa...  46.5 us
    dot_general x4, matrix products, local(): jnp.einsum('sjcf,jfd->sjcd', hidden[..., low:low + ff_part], down_full[:,...  30.8 us
    unnamed x2, matrix products  25.1 us
    unnamed x37, local copies, waits for them, and re-layouts  22.6 us
  transfers between devices with their start and end apart: 10, of which 5 were waited for; matrix products, arithmetic and copies ran while one was open for 21% of the time, Pallas kernels for 7%

profile of v7, /device:TPU:0, one launch (start us, length us, event | category | flops | bytes accessed | tf_op | source)
XLA Modules:
  0.0 702.6 jit_solution(8442155839644124252)
XLA Ops:
  9.4 10.8 %copy.63 = bf16[2048,3,4,128]{0,3,2,1:T(8,128)(2,1)} copy(bf16[2048,3,4,128]{3,2,1,0:T(4,128)(2,1)} %param.21) | data formatting | bytes 12582912 | tf_op args[8]
  21.8 4.5 reduce-window.6
  27.5 2.8 reshape.354
  30.2 2.2 multiply_reduce_fusion
  32.7 5.5 convolution_convert_fusion
  38.2 122.9 %all_to_all.76 = bf16[8,160,2048]{2,1,0:T(8,128)(2,1)} all-to-all(bf16[8,160,2048]{2,1,0:T(8,128)(2,1)S(1)} %bitcast.306), channel_id=1, replica_groups=mesh['expert'=8,'rep'=4] {'expert'}, dimensions={0} | all-to-all | bytes 10485760 | tf_op jit(solution)/shard_map/all_to_all | solution.py:97
  161.2 14.7 %fusion = f32[2,8,80,1408]{3,2,1,0:T(8,128)} fusion(bf16[2,2048,1408]{1,2,0:T(8,128)(2,1)} %all-gather.8.cloned.1.call-done, bf16[8,2,80,2048]{3,2,1,0:T(8,128)(2,1)} %bitcast.304), kind=kOutput, calls=%fused_computation | convolution fusion | flops 7381975040 | bytes 23986176 | tf_op jit(solution)/shard_map/sjcd,jdf->sjcf/dot_general | solution.py:102
  175.8 19.1 %fusion.4 = bf16[8,2,80,1408]{3,2,0,1:T(8,128)(2,1)} fusion(f32[2,8,80,1408]{3,2,1,0:T(8,128)} %fusion, bf16[2,2048,1408]{1,2,0:T(8,128)(2,1)} %all-gather.6.cloned.1.call-done, bf16[8,2,80,2048]{3,2,1,0:T(8,128)(2,1)} %bitcast.305), kind=kOutput, calls=%fused_computation.7 | convolution fusion | flops 7392788480 | bytes 27590656 | tf_op jit(solution)/shard_map/sjcd,jdf->sjcf/dot_general | solution.py:99
  195.0 48.9 %all-gather.10.cloned.1.call-done = bf16[2,1408,2048]{2,1,0:T(8,128)(2,1)} async-done(((bf16[2,352,2048]{2,1,0:T(8,128)(2,1)}), bf16[2,1408,2048]{2,1,0:T(8,128)(2,1)}) %all-gather.10.cloned.1.call-update) | async-done | bytes 11534352 | tf_op jit(solution)/shard_map/all_gather | solution.py:78
  243.9 5.3 fusion.17
  249.2 6.8 fusion.18
  256.0 7.8 %fusion.16 = bf16[2,8,80,2048]{3,2,1,0:T(8,128)(2,1)} fusion(bf16[2,1408,2048]{2,1,0:T(8,128)(2,1)} %all-gather.10.cloned.1.call-done, bf16[8,2,80,1408]{3,2,0,1:T(8,128)(2,1)S(1)} %copy-done.15), kind=kOutput, calls=%fused_computation.28 | convolution fusion | flops 1845493760 | bytes 9109504 | tf_op jit(solution)/shard_map/sjcf,jfd->sjcd/dot_general | solution.py:109
  263.8 10.9 %fusion.8 = bf16[8,2,80,2048]{3,2,0,1:T(8,128)(2,1)S(1)} fusion(bf16[2,8,80,2048]{3,2,1,0:T(8,128)(2,1)} %fusion.16, bf16[2,8,80,2048]{3,2,1,0:T(8,128)(2,1)S(1)} %fusion.17, bf16[2,8,80,2048]{3,2,1,0:T(8,128)(2,1)} %fusion.18, bf16[2,1408,2048]{2,1,0:T(8,128)(2,1)} %all-gather.10.cloned.1.call-done, bf16[8,2,80,1408]{3,2,0,1:T(8,128)(2,1)} %fusion.4), kind=kOutput, calls=%fused_computation.15 | convolution fusion | flops 1869086720 | bytes 24838144 | tf_op jit(solution)/shard_map/sjcf,jfd->sjcd/dot_general | solution.py:109
  274.7 2.9 copy.59
  277.6 5.7 all-to-all-start.1
  283.7 5.4 all_gather.22
  289.1 110.3 %all-to-all-done.1 = bf16[8,160,2048]{2,1,0:T(8,128)(2,1)} async-done(((bf16[8,160,2048]{2,1,0:T(8,128)(2,1)}), bf16[8,160,2048]{2,1,0:T(8,128)(2,1)}, u32[]{:S(2)}, u32[]{:S(2)}) %all-to-all-start.1) | async-done | bytes 5242912 | tf_op jit(solution)/shard_map/all_to_all | solution.py:116
  399.4 5.1 fusion.20
  404.5 6.4 fusion.13
  411.0 1.4 copy-done.4
  412.4 1.9 fusion.15
  414.2 3.2 reshape.335
  417.4 4.2 fusion.106
  421.6 12.7 %fusion.88 = f32[256,6144]{0,1:S(1)} fusion(bf16[2048,6144]{0,1:T(8,128)(2,1)} %bitcast.326, bf16[256,1,2048]{2,1,0:T(2,128)(2,1)} %get-tuple-element.18), kind=kOutput, calls=%fused_computation.127 | convolution fusion | flops 6442450944 | bytes 32505856
  434.7 1.2 copy-done.8
  435.9 12.4 %fusion.87 = f32[256,6144]{0,1:S(1)} fusion(bf16[2048,6144]{0,1:T(8,128)(2,1)} %bitcast.327, bf16[256,1,2048]{2,1,0:T(2,128)(2,1)S(1)} %copy-done.8), kind=kOutput, calls=%fused_computation.125 | convolution fusion | flops 6442450944 | bytes 32505856
  448.9 2.1 copy-done.2
  451.0 2.3 fusion.83
  453.6 2.0 copy.67
  455.6 3.8 all-to-all-start.2
  459.9 1.7 fusion.86
  461.7 1.9 pad_maximum_fusion.1
  463.5 2.1 copy.73
  465.6 64.7 %all-to-all-done.2 = bf16[3,16,256,128]{2,3,0,1:T(8,128)(2,1)S(1)} async-done(((bf16[3,16,256,128]{2,3,0,1:T(8,128)(2,1)}), bf16[3,16,256,128]{2,3,0,1:T(8,128)(2,1)S(1)}, u32[]{:S(2)}, u32[]{:S(2)}) %all-to-all-start.2) | async-done | bytes 3145760 | tf_op jit(solution)/shard_map/all_to_all | solution.py:158
  530.3 4.5 all-to-all-start.4
  534.8 2.8 copy.68
  537.6 23.2 %shard_map.140 = bf16[2,2048,128]{2,1,0:T(8,128)(2,1)} custom-call(bf16[3,2,2048,128]{3,2,1,0:T(8,128)(2,1)} %bitcast.290, bf16[3,2,2048,128]{3,2,1,0:T(8,128)(2,1)} %bitcast.291, bf16[3,2,2048,128]{3,2,1,0:T(8,128)(2,1)} %bitcast.292), custom_call_target="tpu_custom_call" | custom-call | tf_op jit(solution)/shard_map/pallas_call | solution.py:38
  560.9 3.6 copy.69
  564.5 40.5 %all-to-all-done.4 = bf16[3,16,256,128]{2,3,0,1:T(8,128)(2,1)} async-done(((bf16[3,16,256,128]{2,3,0,1:T(8,128)(2,1)}), bf16[3,16,256,128]{2,3,0,1:T(8,128)(2,1)}, u32[]{:S(2)}, u32[]{:S(2)}) %all-to-all-start.4) | async-done | bytes 3145760 | tf_op jit(solution)/shard_map/all_to_all | solution.py:158
  605.0 3.6 all-to-all-start.3
  608.6 4.7 copy.74
  613.3 23.2 %shard_map.141 = bf16[2,2048,128]{2,1,0:T(8,128)(2,1)} custom-call(bf16[3,2,2048,128]{3,2,1,0:T(8,128)(2,1)} %bitcast.293, bf16[3,2,2048,128]{3,2,1,0:T(8,128)(2,1)} %bitcast.294, bf16[3,2,2048,128]{3,2,1,0:T(8,128)(2,1)} %bitcast.295), custom_call_target="tpu_custom_call" | custom-call | tf_op jit(solution)/shard_map/pallas_call | solution.py:38
  636.6 3.6 copy.75
  640.2 6.0 all-to-all-start.5
  646.2 3.2 reshape.334
  649.4 4.4 fusion.105
  654.0 17.8 %all-to-all-done.5 = bf16[2,2048,128]{2,0,1:T(2,128)(2,1)} async-done(((bf16[2,2048,128]{2,0,1:T(2,128)(2,1)}), bf16[2,2048,128]{2,0,1:T(2,128)(2,1)}, u32[]{:S(2)}, u32[]{:S(2)}) %all-to-all-start.5) | async-done | bytes 1048608 | tf_op jit(solution)/shard_map/all_to_all | solution.py:160
  671.8 1.4 copy.76
  673.3 2.5 fusion.49
  675.8 2.9 fusion.48
  678.7 0.8 fusion.46
  679.5 0.8 copy-done.6
  680.3 1.2 fusion.44
  681.5 1.0 copy-done.13
  682.5 1.5 fusion.73
  684.0 0.7 fusion.39
  684.7 0.7 fusion.38
  685.5 0.8 fusion.36
  686.3 0.8 copy-done.5
  687.1 1.2 fusion.34
  688.2 1.5 fusion.80
  689.9 0.9 convolution_bitcast_fusion.9
  690.8 0.9 convolution_bitcast_fusion.8
  691.8 3.5 copy.77
  (76 shorter events, 8.3 us)
Async XLA Ops:
  7.2 682.8 %copy-start = (f32[1024]{0:T(1024)S(1)}, f32[1024]{0:T(1024)}, u32[]{:S(2)}) copy-start(f32[1024]{0:T(1024)} %param.25) | copy-start | bytes 12292
  7.2 154.0 %all-gather.8.cloned.1.call-start = ((), (), s32[]{:S(2)}) async-start(), calls=%async_computation.7 | async-start | bytes 14417920 | tf_op jit(solution)/shard_map/all_gather | solution.py:77
  7.9 167.9 %all-gather.6.cloned.1.call-start = ((), (), s32[]{:S(2)}) async-start(), calls=%async_computation.6 | async-start | bytes 14417920 | tf_op jit(solution)/shard_map/all_gather | solution.py:76
  8.7 235.2 %all-gather.10.cloned.1.call-start = ((), (), s32[]{:S(2)}) async-start(), calls=%async_computation.8 | async-start | bytes 14417920 | tf_op jit(solution)/shard_map/all_gather | solution.py:78
  9.4 412.2 %all-gather.12.cloned.1.call-start = ((), (), s32[]{:S(2)}) async-start(), calls=%async_computation.9 | async-start | bytes 31457280 | tf_op jit(solution)/shard_map/all_gather | solution.py:79
  20.3 0.7 copy-start.9
  20.3 7.2 %copy-start.3 = (bf16[1,256,2,2048]{3,2,1,0:T(2,128)(2,1)S(1)}, bf16[1,256,2,2048]{3,2,1,0:T(2,128)(2,1)}, u32[]{:S(2)}) copy-start(bf16[1,256,2,2048]{3,2,1,0:T(2,128)(2,1)} %param.13) | copy-start | bytes 6291460
  27.4 5.2 copy-start.14
  243.9 5.3 copy-start.15
  277.6 5.7 copy-start.11
  277.6 6.1 copy-start.12
  277.6 121.8 %all-to-all-start.1 = ((bf16[8,160,2048]{2,1,0:T(8,128)(2,1)}), bf16[8,160,2048]{2,1,0:T(8,128)(2,1)}, u32[]{:S(2)}, u32[]{:S(2)}) async-start(bf16[8,160,2048]{2,1,0:T(8,128)(2,1)} %bitcast.296), calls=%async_computation.1 | async-start | bytes 10485760 | tf_op jit(solution)/shard_map/all_to_all | solution.py:116
  399.4 5.1 copy-start.7
  404.5 7.9 %copy-start.10 = (f32[2048]{0:T(1024)S(1)}, f32[2048]{0:T(1024)}, u32[]{:S(2)}) copy-start(f32[2048]{0:T(1024)} %param.20) | copy-start | bytes 24580
  411.0 1.4 copy-start.4
  434.3 1.6 copy-start.8
  448.2 2.7 copy-start.2
  455.6 74.8 %all-to-all-start.2 = ((bf16[3,16,256,128]{2,3,0,1:T(8,128)(2,1)}), bf16[3,16,256,128]{2,3,0,1:T(8,128)(2,1)S(1)}, u32[]{:S(2)}, u32[]{:S(2)}) async-start(bf16[3,16,256,128]{2,3,0,1:T(8,128)(2,1)} %copy.67), calls=%async_computation.2 | async-start | bytes 6291456 | tf_op jit(solution)/shard_map/all_to_all | solution.py:158
  459.3 213.9 %all-gather.14.cloned.1.call-start = ((), (), s32[]{:S(2)}) async-start(), calls=%async_computation.10 | async-start | bytes 10485760 | tf_op jit(solution)/shard_map/all_gather | solution.py:81
  530.3 74.7 %all-to-all-start.4 = ((bf16[3,16,256,128]{2,3,0,1:T(8,128)(2,1)}), bf16[3,16,256,128]{2,3,0,1:T(8,128)(2,1)}, u32[]{:S(2)}, u32[]{:S(2)}) async-start(bf16[3,16,256,128]{2,3,0,1:T(8,128)(2,1)} %copy.73), calls=%async_computation.4 | async-start | bytes 6291456 | tf_op jit(solution)/shard_map/all_to_all | solution.py:158
  605.0 35.2 %all-to-all-start.3 = ((bf16[2,2048,128]{2,0,1:T(2,128)(2,1)}), bf16[2,2048,128]{2,0,1:T(2,128)(2,1)S(1)}, u32[]{:S(2)}, u32[]{:S(2)}) async-start(bf16[2,2048,128]{2,0,1:T(2,128)(2,1)} %copy.69), calls=%async_computation.3 | async-start | bytes 2097152 | tf_op jit(solution)/shard_map/all_to_all | solution.py:160
  640.2 31.7 %all-to-all-start.5 = ((bf16[2,2048,128]{2,0,1:T(2,128)(2,1)}), bf16[2,2048,128]{2,0,1:T(2,128)(2,1)}, u32[]{:S(2)}, u32[]{:S(2)}) async-start(bf16[2,2048,128]{2,0,1:T(2,128)(2,1)} %copy.75), calls=%async_computation.5 | async-start | bytes 2097152 | tf_op jit(solution)/shard_map/all_to_all | solution.py:160
  673.3 5.4 copy-start.1
  678.7 1.6 copy-start.6
  680.3 2.2 copy-start.13
  685.5 1.6 copy-start.5
Sparse Core Ops, SparseCore 0:
  9.5 78.8 all-gather.7
  90.0 76.1 all-gather.5
  167.7 76.1 all-gather.9
  245.3 154.8 all-gather.11
  461.4 59.3 all-gather.13

commit v8 on v7

--- a/solution.py
+++ b/solution.py
@@ -73,9 +73,14 @@
     exp_local = expert_gate.shape[0]
     expert_total = exp_local * n_owner
     capacity = max(2, tok_count * 10 // (4 * expert_total))
-    gate_full = lax.all_gather(expert_gate, "rep", axis=2, tiled=True)
-    up_full = lax.all_gather(expert_up, "rep", axis=2, tiled=True)
-    down_full = lax.all_gather(expert_down, "rep", axis=1, tiled=True)
+    expert_weights = [
+        (
+            lax.all_gather(expert_gate[j], "rep", axis=1, tiled=True),
+            lax.all_gather(expert_up[j], "rep", axis=1, tiled=True),
+            lax.all_gather(expert_down[j], "rep", axis=0, tiled=True),
+        )
+        for j in range(exp_local)
+    ]
     qkv_full = lax.all_gather(teacher_qkv, "rep", axis=2, tiled=True)
     qk_gain_full = lax.all_gather(qk_gain, "rep", axis=1, tiled=True)
     out_full = lax.all_gather(teacher_out, "rep", axis=0, tiled=True)
@@ -96,26 +101,29 @@
     outgoing = outgoing.reshape(n_owner, exp_local * capacity, width)
     arrived = lax.all_to_all(outgoing, "expert", split_axis=0, concat_axis=0, tiled=True)
     arrived = arrived.reshape(n_owner, exp_local, capacity, width)
-    gate_part = jnp.einsum(
-        "sjcd,jdf->sjcf", arrived, gate_full, preferred_element_type=jnp.float32
-    )
-    up_part = jnp.einsum("sjcd,jdf->sjcf", arrived, up_full, preferred_element_type=jnp.float32)
-    hidden = (jax.nn.silu(gate_part) * up_part).astype(jnp.bfloat16)
-    ff_total = hidden.shape[-1]
-    ff_part = ff_total // n_replica
-    produced = jnp.zeros(arrived.shape, jnp.float32)
-    for part in range(n_replica):
-        low = part * ff_part
-        produced = produced + jnp.einsum(
-            "sjcf,jfd->sjcd",
-            hidden[..., low:low + ff_part],
-            down_full[:, low:low + ff_part],
-            preferred_element_type=jnp.float32,
-        ).astype(jnp.bfloat16).astype(jnp.float32)
-    results = produced.astype(jnp.bfloat16).reshape(n_owner, exp_local * capacity, width)
-    returned = lax.all_to_all(results, "expert", split_axis=0, concat_axis=0, tiled=True).reshape(
-        expert_total * capacity, width
-    )
+    returned_parts = []
+    for j, (gate_w, up_w, down_w) in enumerate(expert_weights):
+        rows = arrived[:, j]
+        gate_part = jnp.einsum("scd,df->scf", rows, gate_w, preferred_element_type=jnp.float32)
+        up_part = jnp.einsum("scd,df->scf", rows, up_w, preferred_element_type=jnp.float32)
+        hidden = (jax.nn.silu(gate_part) * up_part).astype(jnp.bfloat16)
+        ff_total = hidden.shape[-1]
+        ff_part = ff_total // n_replica
+        produced = jnp.zeros(rows.shape, jnp.float32)
+        for part in range(n_replica):
+            low = part * ff_part
+            produced = produced + jnp.einsum(
+                "scf,fd->scd",
+                hidden[..., low:low + ff_part],
+                down_w[low:low + ff_part],
+                preferred_element_type=jnp.float32,
+            ).astype(jnp.bfloat16).astype(jnp.float32)
+        returned_parts.append(
+            lax.all_to_all(
+                produced.astype(jnp.bfloat16), "expert", split_axis=0, concat_axis=0, tiled=True
+            )
+        )
+    returned = jnp.stack(returned_parts, axis=1).reshape(expert_total * capacity, width)
     gate_pair = gate_value.reshape(tok_count, 2)
     combined = jnp.dot(first_rows, returned, preferred_element_type=jnp.float32) * gate_pair[
         :, 0:1

time: 710 us -> 730 us (1.028)
  waiting for transfers between devices: 285 us -> 411 us
  blocking collectives: 128 us -> 5.39 us
  starting transfers between devices: 23.8 us -> 37.4 us
  local copies, waits for them, and re-layouts: 67.4 us -> 75.1 us
    all_to_all x1 -> x0, blocking collectives: 123 us -> none  [local(): lax.all_to_all(outgoing, 'expert', split_axis=0, concat_axis=0, tiled=True)]
    all_to_all x1 -> x3, waiting for transfers between devices: 110 us -> 170 us  [the longest x1 116 us: local(): lax.all_to_all(outgoing, 'expert', split_axis=0, concat_axis=0, tiled=True)]
    all_gather x1, waiting for transfers between devices: 0.01 us -> 58 us  [local(): qkv_full = lax.all_gather(teacher_qkv, 'rep', axis=2, tiled=True)]
    all_to_all x1 -> x3, starting transfers between devices: 5.73 us -> 17.5 us  [the longest x2 9.93 us: local(): lax.all_to_all(produced.astype(jnp.bfloat16), 'expert', split_axis=0, con...]
    slice x2 -> x5, local copies, waits for them, and re-layouts: 0.21 us -> 9.72 us  [the longest x1 3.99 us: local(): expert_gate[j]]
    all_gather x3 -> x6, waiting for transfers between devices: 48.9 us -> 56.8 us  [the longest x2 34.8 us: local(): lax.all_gather(expert_down[j], 'rep', axis=0, tiled=True)]
    dot_general x6 -> x12, matrix products: 64.6 us -> 60.6 us  [the longest x8 22.8 us: local(): jnp.einsum('scf,fd->scd', hidden[..., low:low + ff_part], down_w[low:low...]
    unnamed x37 -> x47, local copies, waits for them, and re-layouts: 22.6 us -> 22.8 us
  transfers between devices with their start and end apart: 10 -> 15, of which waited for: 5 -> 9; matrix products, arithmetic and copies ran while one was open for 21% -> 20% of each run, Pallas kernels for 7% -> 6%
where the time goes in v8:
time: 730 us; the launch traced here: 722 us
  waiting for transfers between devices  411 us (56%)
  matrix products  116 us (16%)
  local copies, waits for them, and re-layouts  75.1 us (10%)
  Pallas kernels  46.5 us (6%)
  starting transfers between devices  37.4 us (5%)
  other arithmetic  16 us (2%)
  between operations  15 us (2%)
    all_to_all x1, waiting for transfers between devices, local(): lax.all_to_all(outgoing, 'expert', split_axis=0, concat_axis=0, tiled=True)  116 us
    all_to_all x2, waiting for transfers between devices, teach(): lax.all_to_all(grouped, 'expert', split_axis=1, concat_axis=2, tiled=True)  106 us
    all_gather x1, waiting for transfers between devices, local(): qkv_full = lax.all_gather(teacher_qkv, 'rep', axis=2, tiled=True)  58 us
    all_to_all x2, waiting for transfers between devices, local(): lax.all_to_all(produced.astype(jnp.bfloat16), 'expert', split_axis=0, con...  54.2 us
    pallas_call x2, Pallas kernels, attention(): pl.pallas_call(functools.partial(attention_kernel, scale=scale), grid=(pa...  46.5 us
    all_gather x2, waiting for transfers between devices, local(): lax.all_gather(expert_down[j], 'rep', axis=0, tiled=True)  34.8 us
    unnamed x2, matrix products  24.9 us
    unnamed x47, local copies, waits for them, and re-layouts  22.8 us
  transfers between devices with their start and end apart: 15, of which 9 were waited for; matrix products, arithmetic and copies ran while one was open for 20% of the time, Pallas kernels for 6%

profile of v8, /device:TPU:0, one launch (start us, length us, event | category | flops | bytes accessed | tf_op | source)
XLA Modules:
  0.0 722.5 jit_solution(7915490743591865532)
XLA Ops:
  7.2 4.0 fusion.113
  11.3 1.8 fusion.114
  13.2 3.7 fusion.115
  18.7 10.8 %copy.75 = bf16[2048,3,4,128]{0,3,2,1:T(8,128)(2,1)} copy(bf16[2048,3,4,128]{3,2,1,0:T(4,128)(2,1)} %param.21) | data formatting | bytes 12582912 | tf_op args[8]
  31.1 4.5 reduce-window.6
  36.7 2.7 reshape.350
  39.4 2.2 multiply_reduce_fusion
  41.9 7.7 %convolution_convert_fusion = bf16[1280,2048]{1,0:T(8,128)(2,1)} fusion(f32[512,2048]{1,0:T(8,128)} %reshape.350, f32[2048]{0:T(1024)S(1)} %copy-done.19, f32[512]{0:T(512)S(1)} %rsqrt.52, s32[512]{0:T(512)S(1)} %bitcast.342, s32[512]{0:T(512)S(1)} %bitcast.344), kind=kOutput, calls=%fused_computation | convolution fusion | flops 2695364608 | bytes 9451520 | tf_op jit(solution)/shard_map/tr,td->rd/dot_general | solution.py:98
  49.6 7.6 %all-to-all-start = ((bf16[8,160,2048]{2,1,0:T(8,128)(2,1)}), bf16[8,160,2048]{2,1,0:T(8,128)(2,1)}, u32[]{:S(2)}, u32[]{:S(2)}) async-start(bf16[8,160,2048]{2,1,0:T(8,128)(2,1)} %bitcast.328), calls=%async_computation | async-start | bytes 10485760 | tf_op jit(solution)/shard_map/all_to_all | solution.py:102
  57.5 115.5 %all-to-all-done = bf16[8,160,2048]{2,1,0:T(8,128)(2,1)} async-done(((bf16[8,160,2048]{2,1,0:T(8,128)(2,1)}), bf16[8,160,2048]{2,1,0:T(8,128)(2,1)}, u32[]{:S(2)}, u32[]{:S(2)}) %all-to-all-start) | async-done | bytes 5242912 | tf_op jit(solution)/shard_map/all_to_all | solution.py:102
  173.0 9.5 %fusion.6 = f32[8,80,1408]{2,1,0:T(8,128)} fusion(bf16[1,2048,1408]{1,2,0:T(8,128)(2,1)} %all-gather.19.cloned.1.call-done, bf16[8,2,80,2048]{3,2,1,0:T(8,128)(2,1)} %bitcast.5), kind=kOutput, calls=%fused_computation.7 | convolution fusion | flops 3690987520 | bytes 11993088 | tf_op jit(solution)/shard_map/scd,df->scf/dot_general | solution.py:107
  182.5 8.9 %fusion.20 = bf16[8,80,1408]{2,1,0:T(8,128)(2,1)S(1)} fusion(bf16[1,2048,1408]{1,2,0:T(8,128)(2,1)} %all-gather.21.cloned.1.call-done, f32[8,80,1408]{2,1,0:T(8,128)} %fusion.6, bf16[8,2,80,2048]{3,2,1,0:T(8,128)(2,1)} %bitcast.5), kind=kOutput, calls=%fused_computation.23 | convolution fusion | flops 3696394240 | bytes 13795328 | tf_op jit(solution)/shard_map/scd,df->scf/dot_general | solution.py:108
  191.5 3.1 convolution_convert_fusion.5
  194.6 2.9 convolution_convert_fusion.6
  197.6 1.6 convolution_convert_fusion.7
  199.1 3.4 add_convert_fusion.1
  202.5 4.1 all-to-all-start.1
  206.6 9.5 %fusion.2 = f32[8,80,1408]{2,1,0:T(8,128)} fusion(bf16[1,2048,1408]{1,2,0:T(8,128)(2,1)} %all-gather.25.cloned.1.call-done, bf16[8,2,80,2048]{3,2,1,0:T(8,128)(2,1)} %bitcast.5), kind=kOutput, calls=%fused_computation.3 | convolution fusion | flops 3690987520 | bytes 11993088 | tf_op jit(solution)/shard_map/scd,df->scf/dot_general | solution.py:107
  216.1 21.6 %all-gather.27.cloned.1.call-done = bf16[1,2048,1408]{1,2,0:T(8,128)(2,1)} async-done(((bf16[1,2048,352]{1,2,0:T(8,128)(2,1)}), bf16[1,2048,1408]{1,2,0:T(8,128)(2,1)}) %all-gather.27.cloned.1.call-update) | async-done | bytes 5767184 | tf_op jit(solution)/shard_map/all_gather | solution.py:79
  237.7 10.0 %fusion.17 = bf16[8,80,1408]{2,1,0:T(8,128)(2,1)} fusion(bf16[1,2048,1408]{1,2,0:T(8,128)(2,1)} %all-gather.27.cloned.1.call-done, f32[8,80,1408]{2,1,0:T(8,128)} %fusion.2, bf16[8,2,80,2048]{3,2,1,0:T(8,128)(2,1)} %bitcast.5), kind=kOutput, calls=%fused_computation.22 | convolution fusion | flops 3696394240 | bytes 13795328 | tf_op jit(solution)/shard_map/scd,df->scf/dot_general | solution.py:108
  247.7 34.8 %all-gather.29.cloned.1.call-done = bf16[1,1408,2048]{2,1,0:T(8,128)(2,1)} async-done(((bf16[1,352,2048]{2,1,0:T(8,128)(2,1)}), bf16[1,1408,2048]{2,1,0:T(8,128)(2,1)}) %all-gather.29.cloned.1.call-update) | async-done | bytes 5767184 | tf_op jit(solution)/shard_map/all_gather | solution.py:80
  282.5 3.3 convolution_convert_fusion.3
  285.8 3.3 convolution_convert_fusion.2
  289.1 1.6 convolution_convert_fusion.1
  290.7 3.6 add_convert_fusion
  294.3 5.9 all-to-all-start.2
  300.6 5.4 all_gather.34
  306.0 54.2 %all-to-all-done.2 = bf16[8,80,2048]{2,1,0:T(8,128)(2,1)} async-done(((bf16[8,80,2048]{2,1,0:T(8,128)(2,1)}), bf16[8,80,2048]{2,1,0:T(8,128)(2,1)}, u32[]{:S(2)}, u32[]{:S(2)}) %all-to-all-start.2) | async-done | bytes 2621472 | tf_op jit(solution)/shard_map/all_to_all | solution.py:122
  360.2 2.2 pad_maximum_fusion
  363.2 3.0 fusion.24
  366.3 4.2 fusion.8
  370.5 1.3 copy-done.4
  371.8 1.9 fusion.10
  373.7 3.2 reshape.331
  376.8 4.2 fusion.117
  381.0 58.0 %all-gather.15.cloned.1.call-done = bf16[2048,3,16,128]{0,3,2,1:T(8,128)(2,1)} async-done(((bf16[2048,3,4,128]{0,3,2,1:T(8,128)(2,1)}), bf16[2048,3,16,128]{0,3,2,1:T(8,128)(2,1)}) %all-gather.15.cloned.1.call-update) | async-done | bytes 25165840 | tf_op jit(solution)/shard_map/all_gather | solution.py:84
  439.0 12.7 %fusion.92 = f32[256,6144]{0,1:S(1)} fusion(bf16[2048,6144]{0,1:T(8,128)(2,1)} %bitcast.348, bf16[256,1,2048]{2,1,0:T(2,128)(2,1)} %get-tuple-element.24), kind=kOutput, calls=%fused_computation.138 | convolution fusion | flops 6442450944 | bytes 32505856
  453.3 12.2 %fusion.91 = f32[256,6144]{0,1:S(1)} fusion(bf16[2048,6144]{0,1:T(8,128)(2,1)} %bitcast.349, bf16[256,1,2048]{2,1,0:T(2,128)(2,1)S(1)} %copy-done.11), kind=kOutput, calls=%fused_computation.136 | convolution fusion | flops 6442450944 | bytes 32505856
  466.1 2.1 copy-done.2
  468.2 2.7 fusion.87
  471.2 2.0 copy.79
  473.2 5.5 all-to-all-start.3
  479.5 1.9 fusion.90
  482.0 2.0 copy.85
  484.0 65.8 %all-to-all-done.3 = bf16[3,16,256,128]{2,3,0,1:T(8,128)(2,1)S(1)} async-done(((bf16[3,16,256,128]{2,3,0,1:T(8,128)(2,1)}), bf16[3,16,256,128]{2,3,0,1:T(8,128)(2,1)S(1)}, u32[]{:S(2)}, u32[]{:S(2)}) %all-to-all-start.3) | async-done | bytes 3145760 | tf_op jit(solution)/shard_map/all_to_all | solution.py:166
  549.9 4.5 all-to-all-start.5
  554.4 2.8 copy.80
  557.2 23.2 %shard_map.140 = bf16[2,2048,128]{2,1,0:T(8,128)(2,1)} custom-call(bf16[3,2,2048,128]{3,2,1,0:T(8,128)(2,1)} %bitcast.312, bf16[3,2,2048,128]{3,2,1,0:T(8,128)(2,1)} %bitcast.313, bf16[3,2,2048,128]{3,2,1,0:T(8,128)(2,1)} %bitcast.314), custom_call_target="tpu_custom_call" | custom-call | tf_op jit(solution)/shard_map/pallas_call | solution.py:38
  580.4 3.6 copy.81
  584.1 40.6 %all-to-all-done.5 = bf16[3,16,256,128]{2,3,0,1:T(8,128)(2,1)} async-done(((bf16[3,16,256,128]{2,3,0,1:T(8,128)(2,1)}), bf16[3,16,256,128]{2,3,0,1:T(8,128)(2,1)}, u32[]{:S(2)}, u32[]{:S(2)}) %all-to-all-start.5) | async-done | bytes 3145760 | tf_op jit(solution)/shard_map/all_to_all | solution.py:166
  624.7 3.6 all-to-all-start.4
  628.3 4.7 copy.86
  633.0 23.2 %shard_map.141 = bf16[2,2048,128]{2,1,0:T(8,128)(2,1)} custom-call(bf16[3,2,2048,128]{3,2,1,0:T(8,128)(2,1)} %bitcast.315, bf16[3,2,2048,128]{3,2,1,0:T(8,128)(2,1)} %bitcast.316, bf16[3,2,2048,128]{3,2,1,0:T(8,128)(2,1)} %bitcast.317), custom_call_target="tpu_custom_call" | custom-call | tf_op jit(solution)/shard_map/pallas_call | solution.py:38
  656.2 3.6 copy.87
  659.8 6.0 all-to-all-start.6
  665.8 3.2 reshape.330
  669.0 4.3 fusion.116
  673.5 17.9 %all-to-all-done.6 = bf16[2,2048,128]{2,0,1:T(2,128)(2,1)} async-done(((bf16[2,2048,128]{2,0,1:T(2,128)(2,1)}), bf16[2,2048,128]{2,0,1:T(2,128)(2,1)}, u32[]{:S(2)}, u32[]{:S(2)}) %all-to-all-start.6) | async-done | bytes 1048608 | tf_op jit(solution)/shard_map/all_to_all | solution.py:168
  691.5 1.4 copy.88
  692.9 2.5 fusion.53
  695.4 2.9 fusion.52
  702.1 1.5 fusion.77
  707.8 1.5 fusion.84
  711.4 3.5 copy.89
  (108 shorter events, 21.0 us)
Async XLA Ops:
  7.2 702.4 %copy-start = (f32[1024]{0:T(1024)S(1)}, f32[1024]{0:T(1024)}, u32[]{:S(2)}) copy-start(f32[1024]{0:T(1024)} %param.25) | copy-start | bytes 12292
  7.2 4.1 copy-start.10
  7.2 50.3 %all-gather.19.cloned.1.call-start = ((), (), s32[]{:S(2)}) async-start(), calls=%async_computation.9 | async-start | bytes 7208960 | tf_op jit(solution)/shard_map/all_gather | solution.py:78
  11.3 171.3 %all-gather.21.cloned.1.call-start = ((), (), s32[]{:S(2)}) async-start(), calls=%async_computation.10 | async-start | bytes 7208960 | tf_op jit(solution)/shard_map/all_gather | solution.py:79
  13.1 178.3 %all-gather.23.cloned.1.call-start = ((), (), s32[]{:S(2)}) async-start(), calls=%async_computation.11 | async-start | bytes 7208960 | tf_op jit(solution)/shard_map/all_gather | solution.py:80
  16.9 189.7 %all-gather.25.cloned.1.call-start = ((), (), s32[]{:S(2)}) async-start(), calls=%async_computation.12 | async-start | bytes 7208960 | tf_op jit(solution)/shard_map/all_gather | solution.py:78
  17.5 220.2 %all-gather.27.cloned.1.call-start = ((), (), s32[]{:S(2)}) async-start(), calls=%async_computation.13 | async-start | bytes 7208960 | tf_op jit(solution)/shard_map/all_gather | solution.py:79
  18.1 264.4 %all-gather.29.cloned.1.call-start = ((), (), s32[]{:S(2)}) async-start(), calls=%async_computation.14 | async-start | bytes 7208960 | tf_op jit(solution)/shard_map/all_gather | solution.py:80
  18.7 420.3 %all-gather.15.cloned.1.call-start = ((), (), s32[]{:S(2)}) async-start(), calls=%async_computation.7 | async-start | bytes 31457280 | tf_op jit(solution)/shard_map/all_gather | solution.py:84
  29.6 0.7 copy-start.12
  30.3 6.5 copy-start.3
  39.4 2.4 copy-start.19
  49.6 123.4 %all-to-all-start = ((bf16[8,160,2048]{2,1,0:T(8,128)(2,1)}), bf16[8,160,2048]{2,1,0:T(8,128)(2,1)}, u32[]{:S(2)}, u32[]{:S(2)}) async-start(bf16[8,160,2048]{2,1,0:T(8,128)(2,1)} %bitcast.328), calls=%async_computation | async-start | bytes 10485760 | tf_op jit(solution)/shard_map/all_to_all | solution.py:102
  191.4 6.1 copy-start.16
  202.5 91.8 %all-to-all-start.1 = ((bf16[8,80,2048]{2,1,0:T(8,128)(2,1)}), bf16[8,80,2048]{2,1,0:T(8,128)(2,1)S(1)}, u32[]{:S(2)}, u32[]{:S(2)}) async-start(bf16[8,80,2048]{2,1,0:T(8,128)(2,1)} %add_convert_fusion.1), calls=%async_computation.1 | async-start | bytes 5242880 | tf_op jit(solution)/shard_map/all_to_all | solution.py:122
  282.5 6.6 copy-start.17
  285.8 3.3 copy-start.20
  294.3 5.9 copy-start.14
  294.3 6.2 copy-start.15
  294.3 65.8 %all-to-all-start.2 = ((bf16[8,80,2048]{2,1,0:T(8,128)(2,1)}), bf16[8,80,2048]{2,1,0:T(8,128)(2,1)}, u32[]{:S(2)}, u32[]{:S(2)}) async-start(bf16[8,80,2048]{2,1,0:T(8,128)(2,1)} %add_convert_fusion), calls=%async_computation.2 | async-start | bytes 5242880 | tf_op jit(solution)/shard_map/all_to_all | solution.py:122
  363.2 3.0 copy-start.7
  366.3 5.5 copy-start.13
  370.4 1.3 copy-start.4
  451.7 1.6 copy-start.11
  465.5 2.7 copy-start.2
  473.2 76.6 %all-to-all-start.3 = ((bf16[3,16,256,128]{2,3,0,1:T(8,128)(2,1)}), bf16[3,16,256,128]{2,3,0,1:T(8,128)(2,1)S(1)}, u32[]{:S(2)}, u32[]{:S(2)}) async-start(bf16[3,16,256,128]{2,3,0,1:T(8,128)(2,1)} %copy.79), calls=%async_computation.3 | async-start | bytes 6291456 | tf_op jit(solution)/shard_map/all_to_all | solution.py:166
  478.7 214.2 %all-gather.17.cloned.1.call-start = ((), (), s32[]{:S(2)}) async-start(), calls=%async_computation.8 | async-start | bytes 10485760 | tf_op jit(solution)/shard_map/all_gather | solution.py:86
  479.5 1.9 copy-start.8
  479.5 2.2 copy-start.9
  549.9 74.8 %all-to-all-start.5 = ((bf16[3,16,256,128]{2,3,0,1:T(8,128)(2,1)}), bf16[3,16,256,128]{2,3,0,1:T(8,128)(2,1)}, u32[]{:S(2)}, u32[]{:S(2)}) async-start(bf16[3,16,256,128]{2,3,0,1:T(8,128)(2,1)} %copy.85), calls=%async_computation.5 | async-start | bytes 6291456 | tf_op jit(solution)/shard_map/all_to_all | solution.py:166
  624.7 35.1 %all-to-all-start.4 = ((bf16[2,2048,128]{2,0,1:T(2,128)(2,1)}), bf16[2,2048,128]{2,0,1:T(2,128)(2,1)S(1)}, u32[]{:S(2)}, u32[]{:S(2)}) async-start(bf16[2,2048,128]{2,0,1:T(2,128)(2,1)} %copy.81), calls=%async_computation.4 | async-start | bytes 2097152 | tf_op jit(solution)/shard_map/all_to_all | solution.py:168
  659.8 31.6 %all-to-all-start.6 = ((bf16[2,2048,128]{2,0,1:T(2,128)(2,1)}), bf16[2,2048,128]{2,0,1:T(2,128)(2,1)}, u32[]{:S(2)}, u32[]{:S(2)}) async-start(bf16[2,2048,128]{2,0,1:T(2,128)(2,1)} %copy.87), calls=%async_computation.6 | async-start | bytes 2097152 | tf_op jit(solution)/shard_map/all_to_all | solution.py:168
  692.9 5.4 copy-start.1
  698.3 1.6 copy-start.6
  699.9 2.2 copy-start.18
  705.1 1.6 copy-start.5
Sparse Core Ops, SparseCore 0:
  11.4 46.1 all-gather.18
  59.1 43.3 all-gather.20
  104.6 43.3 all-gather.22
  149.5 43.3 all-gather.24
  194.3 43.3 all-gather.26
  239.1 43.3 all-gather.28
  284.1 154.8 all-gather.14
  481.1 58.7 all-gather.16

commit v9 on v8

--- a/solution.py
+++ b/solution.py
@@ -73,13 +73,10 @@
     exp_local = expert_gate.shape[0]
     expert_total = exp_local * n_owner
     capacity = max(2, tok_count * 10 // (4 * expert_total))
-    expert_weights = [
-        (
-            lax.all_gather(expert_gate[j], "rep", axis=1, tiled=True),
-            lax.all_gather(expert_up[j], "rep", axis=1, tiled=True),
-            lax.all_gather(expert_down[j], "rep", axis=0, tiled=True),
-        )
-        for j in range(exp_local)
+    gate_full = lax.all_gather(expert_gate, "rep", axis=2, tiled=True)
+    up_full = lax.all_gather(expert_up, "rep", axis=2, tiled=True)
+    down_parts = [
+        lax.all_gather(expert_down[j], "rep", axis=0, tiled=True) for j in range(exp_local)
     ]
     qkv_full = lax.all_gather(teacher_qkv, "rep", axis=2, tiled=True)
     qk_gain_full = lax.all_gather(qk_gain, "rep", axis=1, tiled=True)
@@ -101,20 +98,21 @@
     outgoing = outgoing.reshape(n_owner, exp_local * capacity, width)
     arrived = lax.all_to_all(outgoing, "expert", split_axis=0, concat_axis=0, tiled=True)
     arrived = arrived.reshape(n_owner, exp_local, capacity, width)
+    gate_part = jnp.einsum(
+        "sjcd,jdf->sjcf", arrived, gate_full, preferred_element_type=jnp.float32
+    )
+    up_part = jnp.einsum("sjcd,jdf->sjcf", arrived, up_full, preferred_element_type=jnp.float32)
+    hidden = (jax.nn.silu(gate_part) * up_part).astype(jnp.bfloat16)
+    ff_total = hidden.shape[-1]
+    ff_part = ff_total // n_replica
     returned_parts = []
-    for j, (gate_w, up_w, down_w) in enumerate(expert_weights):
-        rows = arrived[:, j]
-        gate_part = jnp.einsum("scd,df->scf", rows, gate_w, preferred_element_type=jnp.float32)
-        up_part = jnp.einsum("scd,df->scf", rows, up_w, preferred_element_type=jnp.float32)
-        hidden = (jax.nn.silu(gate_part) * up_part).astype(jnp.bfloat16)
-        ff_total = hidden.shape[-1]
-        ff_part = ff_total // n_replica
-        produced = jnp.zeros(rows.shape, jnp.float32)
+    for j, down_w in enumerate(down_parts):
+        produced = jnp.zeros(arrived[:, j].shape, jnp.float32)
         for part in range(n_replica):
             low = part * ff_part
             produced = produced + jnp.einsum(
                 "scf,fd->scd",
-                hidden[..., low:low + ff_part],
+                hidden[:, j, :, low:low + ff_part],
                 down_w[low:low + ff_part],
                 preferred_element_type=jnp.float32,
             ).astype(jnp.bfloat16).astype(jnp.float32)

time: 730 us -> 704 us (0.964)
  waiting for transfers between devices: 411 us -> 280 us
  blocking collectives: 5.39 us -> 129 us
  starting transfers between devices: 37.4 us -> 29.7 us
  local copies, waits for them, and re-layouts: 75.1 us -> 67.4 us
    all_to_all x0 -> x1, blocking collectives: none -> 123 us  [local(): lax.all_to_all(outgoing, 'expert', split_axis=0, concat_axis=0, tiled=True)]
    all_to_all x1 -> x0, waiting for transfers between devices: 116 us -> none  [local(): lax.all_to_all(outgoing, 'expert', split_axis=0, concat_axis=0, tiled=True)]
    all_gather x4 -> x2, waiting for transfers between devices: 22 us -> 0.01 us  [the longest x1 0.01 us: local(): up_full = lax.all_gather(expert_up, 'rep', axis=2, tiled=True)]
    all_gather x1, waiting for transfers between devices: 58 us -> 37.7 us  [local(): qkv_full = lax.all_gather(teacher_qkv, 'rep', axis=2, tiled=True)]
    all_to_all x2, waiting for transfers between devices: 54.2 us -> 73.7 us  [local(): lax.all_to_all(produced.astype(jnp.bfloat16), 'expert', split_axis=0, con...]
    all_to_all x1 -> x0, starting transfers between devices: 7.55 us -> none  [local(): lax.all_to_all(outgoing, 'expert', split_axis=0, concat_axis=0, tiled=True)]
    all_gather x2, waiting for transfers between devices: 34.8 us -> 42.3 us  [local(): lax.all_gather(expert_down[j], 'rep', axis=0, tiled=True)]
    dot_general x12 -> x10, matrix products: 60.6 us -> 59 us  [the longest x8 27.2 us: local(): jnp.einsum('scf,fd->scd', hidden[:, j, :, low:low + ff_part], down_w[low:...]
  transfers between devices with their start and end apart: 15 -> 12, of which waited for: 9 -> 8; matrix products, arithmetic and copies ran while one was open for 20% -> 20% of each run, Pallas kernels for 6% -> 7%
where the time goes in v9:
time: 704 us; the launch traced here: 696 us
  waiting for transfers between devices  280 us (40%)
  blocking collectives  129 us (18%)
  matrix products  112 us (16%)
  local copies, waits for them, and re-layouts  67.4 us (10%)
  Pallas kernels  46.5 us (7%)
  starting transfers between devices  29.7 us (4%)
  other arithmetic  17.4 us (2%)
  between operations  15.1 us (2%)
    all_to_all x1, blocking collectives, local(): lax.all_to_all(outgoing, 'expert', split_axis=0, concat_axis=0, tiled=True)  123 us
    all_to_all x2, waiting for transfers between devices, teach(): lax.all_to_all(grouped, 'expert', split_axis=1, concat_axis=2, tiled=True)  106 us
    all_to_all x2, waiting for transfers between devices, local(): lax.all_to_all(produced.astype(jnp.bfloat16), 'expert', split_axis=0, con...  73.7 us
    pallas_call x2, Pallas kernels, attention(): pl.pallas_call(functools.partial(attention_kernel, scale=scale), grid=(pa...  46.5 us
    all_gather x2, waiting for transfers between devices, local(): lax.all_gather(expert_down[j], 'rep', axis=0, tiled=True)  42.3 us
    all_gather x1, waiting for transfers between devices, local(): qkv_full = lax.all_gather(teacher_qkv, 'rep', axis=2, tiled=True)  37.7 us
    dot_general x8, matrix products, local(): jnp.einsum('scf,fd->scd', hidden[:, j, :, low:low + ff_part], down_w[low:...  27.2 us
    unnamed x2, matrix products  24.9 us
  transfers between devices with their start and end apart: 12, of which 8 were waited for; matrix products, arithmetic and copies ran while one was open for 20% of the time, Pallas kernels for 7%

profile of v9, /device:TPU:0, one launch (start us, length us, event | category | flops | bytes accessed | tf_op | source)
XLA Modules:
  0.0 696.5 jit_solution(2884602573657813367)
XLA Ops:
  9.0 1.8 fusion.97
  11.5 10.9 %copy.63 = bf16[2048,3,4,128]{0,3,2,1:T(8,128)(2,1)} copy(bf16[2048,3,4,128]{3,2,1,0:T(4,128)(2,1)} %param.21) | data formatting | bytes 12582912 | tf_op args[8]
  23.9 4.5 reduce-window.6
  29.5 2.8 reshape.350
  32.3 2.2 multiply_reduce_fusion
  34.8 5.4 convolution_convert_fusion
  40.2 123.1 %all_to_all.81 = bf16[8,160,2048]{2,1,0:T(8,128)(2,1)} all-to-all(bf16[8,160,2048]{2,1,0:T(8,128)(2,1)S(1)} %bitcast.343), channel_id=1, replica_groups=mesh['expert'=8,'rep'=4] {'expert'}, dimensions={0} | all-to-all | bytes 10485760 | tf_op jit(solution)/shard_map/all_to_all | solution.py:99
  163.3 14.7 %fusion = f32[2,8,80,1408]{3,2,1,0:T(8,128)} fusion(bf16[2,2048,1408]{1,2,0:T(8,128)(2,1)} %all-gather.11.cloned.1.call-done, bf16[8,2,80,2048]{3,2,1,0:T(8,128)(2,1)} %bitcast.339), kind=kOutput, calls=%fused_computation | convolution fusion | flops 7381975040 | bytes 23986176 | tf_op jit(solution)/shard_map/sjcd,jdf->sjcf/dot_general | solution.py:104
  178.1 17.1 %fusion.4 = bf16[8,2,80,1408]{3,2,0,1:T(8,128)(2,1)} fusion(f32[2,8,80,1408]{3,2,1,0:T(8,128)} %fusion, bf16[2,2048,1408]{1,2,0:T(8,128)(2,1)} %all-gather.9.cloned.1.call-done, bf16[8,2,80,2048]{3,2,1,0:T(8,128)(2,1)} %bitcast.340), kind=kOutput, calls=%fused_computation.6 | convolution fusion | flops 7392788480 | bytes 27590656 | tf_op jit(solution)/shard_map/sjcd,jdf->sjcf/dot_general | solution.py:101
  195.2 16.5 %all-gather.17.cloned.1.call-done = bf16[1,1408,2048]{2,1,0:T(8,128)(2,1)} async-done(((bf16[1,352,2048]{2,1,0:T(8,128)(2,1)}), bf16[1,1408,2048]{2,1,0:T(8,128)(2,1)}) %all-gather.17.cloned.1.call-update) | async-done | bytes 5767184 | tf_op jit(solution)/shard_map/all_gather | solution.py:79
  211.7 3.2 convolution_convert_fusion.5
  215.0 3.1 convolution_convert_fusion.6
  218.1 2.7 convolution_convert_fusion.7
  220.8 4.4 add_convert_fusion.1
  225.3 5.5 all-to-all-start.1
  230.8 25.8 %all-gather.19.cloned.1.call-done = bf16[1,1408,2048]{2,1,0:T(8,128)(2,1)} async-done(((bf16[1,352,2048]{2,1,0:T(8,128)(2,1)}), bf16[1,1408,2048]{2,1,0:T(8,128)(2,1)}) %all-gather.19.cloned.1.call-update) | async-done | bytes 5767184 | tf_op jit(solution)/shard_map/all_gather | solution.py:79
  256.6 3.3 convolution_convert_fusion.3
  259.9 3.1 convolution_convert_fusion.2
  263.0 2.7 convolution_convert_fusion.1
  265.7 4.5 add_convert_fusion
  270.2 20.5 %all-to-all-done.1 = bf16[8,80,2048]{2,1,0:T(8,128)(2,1)S(1)} async-done(((bf16[8,80,2048]{2,1,0:T(8,128)(2,1)}), bf16[8,80,2048]{2,1,0:T(8,128)(2,1)S(1)}, u32[]{:S(2)}, u32[]{:S(2)}) %all-to-all-start.1) | async-done | bytes 2621472 | tf_op jit(solution)/shard_map/all_to_all | solution.py:120
  290.7 4.4 all-to-all-start.2
  295.5 5.4 all_gather.26
  300.9 53.3 %all-to-all-done.2 = bf16[8,80,2048]{2,1,0:T(8,128)(2,1)} async-done(((bf16[8,80,2048]{2,1,0:T(8,128)(2,1)}), bf16[8,80,2048]{2,1,0:T(8,128)(2,1)}, u32[]{:S(2)}, u32[]{:S(2)}) %all-to-all-start.2) | async-done | bytes 2621472 | tf_op jit(solution)/shard_map/all_to_all | solution.py:120
  354.2 2.2 pad_maximum_fusion
  357.2 3.0 fusion.16
  360.3 4.3 fusion.12
  364.6 1.3 copy-done.4
  366.0 1.9 fusion.14
  367.8 3.2 reshape.331
  371.0 4.2 fusion.99
  375.2 37.7 %all-gather.13.cloned.1.call-done = bf16[2048,3,16,128]{0,3,2,1:T(8,128)(2,1)} async-done(((bf16[2048,3,4,128]{0,3,2,1:T(8,128)(2,1)}), bf16[2048,3,16,128]{0,3,2,1:T(8,128)(2,1)}) %all-gather.13.cloned.1.call-update) | async-done | bytes 25165840 | tf_op jit(solution)/shard_map/all_gather | solution.py:81
  412.9 12.7 %fusion.84 = f32[256,6144]{0,1:S(1)} fusion(bf16[2048,6144]{0,1:T(8,128)(2,1)} %bitcast.363, bf16[256,1,2048]{2,1,0:T(2,128)(2,1)} %get-tuple-element.20), kind=kOutput, calls=%fused_computation.137 | convolution fusion | flops 6442450944 | bytes 32505856
  426.0 1.2 copy-done.9
  427.2 12.2 %fusion.83 = f32[256,6144]{0,1:S(1)} fusion(bf16[2048,6144]{0,1:T(8,128)(2,1)} %bitcast.364, bf16[256,1,2048]{2,1,0:T(2,128)(2,1)S(1)} %copy-done.9), kind=kOutput, calls=%fused_computation.135 | convolution fusion | flops 6442450944 | bytes 32505856
  440.0 2.1 copy-done.2
  442.1 2.5 fusion.79
  444.9 2.0 copy.67
  446.9 5.5 all-to-all-start.3
  453.0 1.7 fusion.82
  454.7 1.9 pad_maximum_fusion.2
  456.6 2.0 copy.73
  458.6 64.9 %all-to-all-done.3 = bf16[3,16,256,128]{2,3,0,1:T(8,128)(2,1)S(1)} async-done(((bf16[3,16,256,128]{2,3,0,1:T(8,128)(2,1)}), bf16[3,16,256,128]{2,3,0,1:T(8,128)(2,1)S(1)}, u32[]{:S(2)}, u32[]{:S(2)}) %all-to-all-start.3) | async-done | bytes 3145760 | tf_op jit(solution)/shard_map/all_to_all | solution.py:164
  523.6 4.5 all-to-all-start.5
  528.1 2.8 copy.68
  530.9 23.2 %shard_map.140 = bf16[2,2048,128]{2,1,0:T(8,128)(2,1)} custom-call(bf16[3,2,2048,128]{3,2,1,0:T(8,128)(2,1)} %bitcast.325, bf16[3,2,2048,128]{3,2,1,0:T(8,128)(2,1)} %bitcast.326, bf16[3,2,2048,128]{3,2,1,0:T(8,128)(2,1)} %bitcast.327), custom_call_target="tpu_custom_call" | custom-call | tf_op jit(solution)/shard_map/pallas_call | solution.py:38
  554.1 3.6 copy.69
  557.7 40.6 %all-to-all-done.5 = bf16[3,16,256,128]{2,3,0,1:T(8,128)(2,1)} async-done(((bf16[3,16,256,128]{2,3,0,1:T(8,128)(2,1)}), bf16[3,16,256,128]{2,3,0,1:T(8,128)(2,1)}, u32[]{:S(2)}, u32[]{:S(2)}) %all-to-all-start.5) | async-done | bytes 3145760 | tf_op jit(solution)/shard_map/all_to_all | solution.py:164
  598.4 3.6 all-to-all-start.4
  602.0 4.7 copy.74
  606.7 23.2 %shard_map.141 = bf16[2,2048,128]{2,1,0:T(8,128)(2,1)} custom-call(bf16[3,2,2048,128]{3,2,1,0:T(8,128)(2,1)} %bitcast.328, bf16[3,2,2048,128]{3,2,1,0:T(8,128)(2,1)} %bitcast.329, bf16[3,2,2048,128]{3,2,1,0:T(8,128)(2,1)} %bitcast.330), custom_call_target="tpu_custom_call" | custom-call | tf_op jit(solution)/shard_map/pallas_call | solution.py:38
  629.9 3.6 copy.75
  633.5 6.0 all-to-all-start.6
  639.5 3.2 reshape.330
  642.7 4.5 fusion.98
  647.4 17.8 %all-to-all-done.6 = bf16[2,2048,128]{2,0,1:T(2,128)(2,1)} async-done(((bf16[2,2048,128]{2,0,1:T(2,128)(2,1)}), bf16[2,2048,128]{2,0,1:T(2,128)(2,1)}, u32[]{:S(2)}, u32[]{:S(2)}) %all-to-all-start.6) | async-done | bytes 1048608 | tf_op jit(solution)/shard_map/all_to_all | solution.py:166
  665.2 1.4 copy.76
  666.6 2.5 fusion.45
  669.1 2.9 fusion.44
  673.6 1.2 fusion.40
  675.8 1.5 fusion.69
  680.4 1.2 fusion.30
  681.6 1.5 fusion.76
  685.1 3.5 copy.77
  (91 shorter events, 16.8 us)
Async XLA Ops:
  7.2 676.1 %copy-start = (f32[1024]{0:T(1024)S(1)}, f32[1024]{0:T(1024)}, u32[]{:S(2)}) copy-start(f32[1024]{0:T(1024)} %param.25) | copy-start | bytes 12292
  7.2 1.8 copy-start.8
  7.2 156.1 %all-gather.11.cloned.1.call-start = ((), (), s32[]{:S(2)}) async-start(), calls=%async_computation.8 | async-start | bytes 14417920 | tf_op jit(solution)/shard_map/all_gather | solution.py:77
  7.9 170.1 %all-gather.9.cloned.1.call-start = ((), (), s32[]{:S(2)}) async-start(), calls=%async_computation.7 | async-start | bytes 14417920 | tf_op jit(solution)/shard_map/all_gather | solution.py:76
  8.7 203.1 %all-gather.17.cloned.1.call-start = ((), (), s32[]{:S(2)}) async-start(), calls=%async_computation.11 | async-start | bytes 7208960 | tf_op jit(solution)/shard_map/all_gather | solution.py:79
  10.8 245.7 %all-gather.19.cloned.1.call-start = ((), (), s32[]{:S(2)}) async-start(), calls=%async_computation.12 | async-start | bytes 7208960 | tf_op jit(solution)/shard_map/all_gather | solution.py:79
  11.4 401.5 %all-gather.13.cloned.1.call-start = ((), (), s32[]{:S(2)}) async-start(), calls=%async_computation.9 | async-start | bytes 31457280 | tf_op jit(solution)/shard_map/all_gather | solution.py:81
  22.3 0.7 copy-start.10
  22.3 7.2 %copy-start.3 = (bf16[1,256,2,2048]{3,2,1,0:T(2,128)(2,1)S(1)}, bf16[1,256,2,2048]{3,2,1,0:T(2,128)(2,1)}, u32[]{:S(2)}) copy-start(bf16[1,256,2,2048]{3,2,1,0:T(2,128)(2,1)} %param.13) | copy-start | bytes 6291460
  29.5 5.2 copy-start.17
  211.7 6.4 copy-start.15
  225.3 65.4 %all-to-all-start.1 = ((bf16[8,80,2048]{2,1,0:T(8,128)(2,1)}), bf16[8,80,2048]{2,1,0:T(8,128)(2,1)S(1)}, u32[]{:S(2)}, u32[]{:S(2)}) async-start(bf16[8,80,2048]{2,1,0:T(8,128)(2,1)} %add_convert_fusion.1), calls=%async_computation.1 | async-start | bytes 5242880 | tf_op jit(solution)/shard_map/all_to_all | solution.py:120
  256.6 6.4 copy-start.14
  270.2 24.9 %copy-start.12 = (f32[1,256,2,2]{1,3,2,0:T(2,128)S(1)}, f32[1,256,2,2]{1,3,2,0:T(2,128)}, u32[]{:S(2)}) copy-start(f32[1,256,2,2]{1,3,2,0:T(2,128)} %param.15) | copy-start | bytes 12292
  270.2 25.2 %copy-start.13 = (f32[2,4,128]{2,1,0:T(4,128)S(1)}, f32[2,4,128]{2,1,0:T(4,128)}, u32[]{:S(2)}) copy-start(f32[2,4,128]{2,1,0:T(4,128)} %param.22) | copy-start | bytes 12292
  290.7 63.5 %all-to-all-start.2 = ((bf16[8,80,2048]{2,1,0:T(8,128)(2,1)}), bf16[8,80,2048]{2,1,0:T(8,128)(2,1)}, u32[]{:S(2)}, u32[]{:S(2)}) async-start(bf16[8,80,2048]{2,1,0:T(8,128)(2,1)} %add_convert_fusion), calls=%async_computation.2 | async-start | bytes 5242880 | tf_op jit(solution)/shard_map/all_to_all | solution.py:120
  357.2 3.0 copy-start.7
  360.3 5.7 copy-start.11
  364.6 1.4 copy-start.4
  425.6 1.6 copy-start.9
  439.4 2.7 copy-start.2
  446.9 76.6 %all-to-all-start.3 = ((bf16[3,16,256,128]{2,3,0,1:T(8,128)(2,1)}), bf16[3,16,256,128]{2,3,0,1:T(8,128)(2,1)S(1)}, u32[]{:S(2)}, u32[]{:S(2)}) async-start(bf16[3,16,256,128]{2,3,0,1:T(8,128)(2,1)} %copy.67), calls=%async_computation.3 | async-start | bytes 6291456 | tf_op jit(solution)/shard_map/all_to_all | solution.py:164
  452.4 214.2 %all-gather.15.cloned.1.call-start = ((), (), s32[]{:S(2)}) async-start(), calls=%async_computation.10 | async-start | bytes 10485760 | tf_op jit(solution)/shard_map/all_gather | solution.py:83
  523.6 74.8 %all-to-all-start.5 = ((bf16[3,16,256,128]{2,3,0,1:T(8,128)(2,1)}), bf16[3,16,256,128]{2,3,0,1:T(8,128)(2,1)}, u32[]{:S(2)}, u32[]{:S(2)}) async-start(bf16[3,16,256,128]{2,3,0,1:T(8,128)(2,1)} %copy.73), calls=%async_computation.5 | async-start | bytes 6291456 | tf_op jit(solution)/shard_map/all_to_all | solution.py:164
  598.4 35.2 %all-to-all-start.4 = ((bf16[2,2048,128]{2,0,1:T(2,128)(2,1)}), bf16[2,2048,128]{2,0,1:T(2,128)(2,1)S(1)}, u32[]{:S(2)}, u32[]{:S(2)}) async-start(bf16[2,2048,128]{2,0,1:T(2,128)(2,1)} %copy.69), calls=%async_computation.4 | async-start | bytes 2097152 | tf_op jit(solution)/shard_map/all_to_all | solution.py:166
  633.5 31.6 %all-to-all-start.6 = ((bf16[2,2048,128]{2,0,1:T(2,128)(2,1)}), bf16[2,2048,128]{2,0,1:T(2,128)(2,1)}, u32[]{:S(2)}, u32[]{:S(2)}) async-start(bf16[2,2048,128]{2,0,1:T(2,128)(2,1)} %copy.75), calls=%async_computation.6 | async-start | bytes 2097152 | tf_op jit(solution)/shard_map/all_to_all | solution.py:166
  666.6 5.4 copy-start.1
  672.0 1.6 copy-start.6
  673.6 2.2 copy-start.16
  678.8 1.6 copy-start.5
Sparse Core Ops, SparseCore 0:
  9.6 78.8 all-gather.10
  90.0 76.1 all-gather.8
  168.3 43.3 all-gather.16
  213.1 43.3 all-gather.18
  258.0 154.8 all-gather.12
  454.5 58.7 all-gather.14

commit v10 on v9

--- a/solution.py
+++ b/solution.py
@@ -136,11 +136,16 @@
     per_chunk = images // chunks
     features_parts = []
     logits_parts = []
+    grouped_parts = []
     for chunk in range(chunks):
-        sel = slice(chunk * per_chunk, (chunk + 1) * per_chunk)
+        chunk_in = teacher_in[:, chunk * per_chunk:(chunk + 1) * per_chunk]
+        if grouped_parts:
+            chunk_in, grouped_parts[-1] = lax.optimization_barrier((chunk_in, grouped_parts[-1]))
+        grouped_parts.append(project(chunk_in, qkv_full, qk_gain_full))
+    for chunk in range(chunks):
         features, logits = teach(
-            teacher_in[:, sel], mixed[:, sel], qkv_full, qk_gain_full, out_full, critic_in, critic_out,
-            n_replica,
+            grouped_parts[chunk], mixed[:, chunk * per_chunk:(chunk + 1) * per_chunk], out_full,
+            critic_in, critic_out, n_replica,
         )
         features_parts.append(features)
         logits_parts.append(logits)
@@ -149,7 +154,7 @@
     return (features.reshape(1, seq_dev, images, width), logits.reshape(1, seq_dev, images))
 
 
-def teach(teacher_in, mixed, qkv_full, qk_gain_full, out_full, critic_in, critic_out, n_replica):
+def project(teacher_in, qkv_full, qk_gain_full):
     seq_dev, images, width = teacher_in.shape
     heads_all = qkv_full.shape[2]
     head_size = qkv_full.shape[3]
@@ -159,8 +164,13 @@
     query = norm_rows(projected[0], qk_gain_full[0][:, None, :])
     keyed = norm_rows(projected[1], qk_gain_full[1][:, None, :])
     projected = jnp.stack([query, keyed, projected[2]]).astype(jnp.bfloat16)
-    pairs_all = images * heads_all
-    grouped = projected.reshape(3, pairs_all, seq_dev, head_size)
+    return projected.reshape(3, images * heads_all, seq_dev, head_size)
+
+
+def teach(grouped, mixed, out_full, critic_in, critic_out, n_replica):
+    seq_dev, images, width = mixed.shape
+    heads_all = out_full.shape[0]
+    head_size = out_full.shape[1]
     whole = lax.all_to_all(grouped, "expert", split_axis=1, concat_axis=2, tiled=True)
     attended = attention(whole, head_size ** (-0.5))
     gathered_heads = lax.all_to_all(attended, "expert", split_axis=1, concat_axis=0, tiled=True)

time: 704 us -> 686 us (0.974)
  waiting for transfers between devices: 280 us -> 267 us
    all_to_all x2, waiting for transfers between devices: 106 us -> 94.3 us  [teach(): lax.all_to_all(grouped, 'expert', split_axis=1, concat_axis=2, tiled=True)]
    unnamed x41 -> x39, local copies, waits for them, and re-layouts: 22.9 us -> 19.6 us
  transfers between devices with their start and end apart: 12 -> 12, of which waited for: 8 -> 8; matrix products, arithmetic and copies ran while one was open for 20% -> 22% of each run, Pallas kernels for 7% -> 7%
where the time goes in v10:
time: 686 us; the launch traced here: 678 us
  waiting for transfers between devices  267 us (39%)
  blocking collectives  129 us (19%)
  matrix products  112 us (16%)
  local copies, waits for them, and re-layouts  63.7 us (9%)
  Pallas kernels  46.5 us (7%)
  starting transfers between devices  29.7 us (4%)
  between operations  14.9 us (2%)
  other arithmetic  14.8 us (2%)
    all_to_all x1, blocking collectives, local(): lax.all_to_all(outgoing, 'expert', split_axis=0, concat_axis=0, tiled=True)  123 us
    all_to_all x2, waiting for transfers between devices, teach(): lax.all_to_all(grouped, 'expert', split_axis=1, concat_axis=2, tiled=True)  94.3 us
    all_to_all x2, waiting for transfers between devices, local(): lax.all_to_all(produced.astype(jnp.bfloat16), 'expert', split_axis=0, con...  73.5 us
    pallas_call x2, Pallas kernels, attention(): pl.pallas_call(functools.partial(attention_kernel, scale=scale), grid=(pa...  46.5 us
    all_gather x2, waiting for transfers between devices, local(): lax.all_gather(expert_down[j], 'rep', axis=0, tiled=True)  42.4 us
    all_gather x1, waiting for transfers between devices, local(): qkv_full = lax.all_gather(teacher_qkv, 'rep', axis=2, tiled=True)  36.7 us
    dot_general x8, matrix products, local(): jnp.einsum('scf,fd->scd', hidden[:, j, :, low:low + ff_part], down_w[low:...  27.2 us
    unnamed x2, matrix products  25.6 us
  transfers between devices with their start and end apart: 12, of which 8 were waited for; matrix products, arithmetic and copies ran while one was open for 22% of the time, Pallas kernels for 7%

profile of v10, /device:TPU:0, one launch (start us, length us, event | category | flops | bytes accessed | tf_op | source)
XLA Modules:
  0.0 678.3 jit_solution(2944934210767052312)
XLA Ops:
  9.0 1.8 fusion.98
  11.5 10.9 %copy.64 = bf16[2048,3,4,128]{0,3,2,1:T(8,128)(2,1)} copy(bf16[2048,3,4,128]{3,2,1,0:T(4,128)(2,1)} %param.21) | data formatting | bytes 12582912 | tf_op args[8]
  23.9 4.5 reduce-window.6
  29.5 2.8 reshape.350
  32.3 2.2 multiply_reduce_fusion
  34.7 5.4 convolution_convert_fusion
  40.2 123.4 %all_to_all.81 = bf16[8,160,2048]{2,1,0:T(8,128)(2,1)} all-to-all(bf16[8,160,2048]{2,1,0:T(8,128)(2,1)S(1)} %bitcast.343), channel_id=1, replica_groups=mesh['expert'=8,'rep'=4] {'expert'}, dimensions={0} | all-to-all | bytes 10485760 | tf_op jit(solution)/shard_map/all_to_all | solution.py:99
  163.5 14.8 %fusion = f32[2,8,80,1408]{3,2,1,0:T(8,128)} fusion(bf16[2,2048,1408]{1,2,0:T(8,128)(2,1)} %all-gather.11.cloned.1.call-done, bf16[8,2,80,2048]{3,2,1,0:T(8,128)(2,1)} %bitcast.339), kind=kOutput, calls=%fused_computation | convolution fusion | flops 7381975040 | bytes 23986176 | tf_op jit(solution)/shard_map/sjcd,jdf->sjcf/dot_general | solution.py:104
  178.3 16.8 %fusion.4 = bf16[8,2,80,1408]{3,2,0,1:T(8,128)(2,1)} fusion(f32[2,8,80,1408]{3,2,1,0:T(8,128)} %fusion, bf16[2,2048,1408]{1,2,0:T(8,128)(2,1)} %all-gather.9.cloned.1.call-done, bf16[8,2,80,2048]{3,2,1,0:T(8,128)(2,1)} %bitcast.340), kind=kOutput, calls=%fused_computation.6 | convolution fusion | flops 7392788480 | bytes 27590656 | tf_op jit(solution)/shard_map/sjcd,jdf->sjcf/dot_general | solution.py:101
  195.1 16.6 %all-gather.17.cloned.1.call-done = bf16[1,1408,2048]{2,1,0:T(8,128)(2,1)} async-done(((bf16[1,352,2048]{2,1,0:T(8,128)(2,1)}), bf16[1,1408,2048]{2,1,0:T(8,128)(2,1)}) %all-gather.17.cloned.1.call-update) | async-done | bytes 5767184 | tf_op jit(solution)/shard_map/all_gather | solution.py:79
  211.7 3.2 convolution_convert_fusion.5
  215.0 3.1 convolution_convert_fusion.6
  218.1 2.7 convolution_convert_fusion.7
  220.8 4.4 add_convert_fusion.1
  225.3 5.5 all-to-all-start.1
  230.8 25.8 %all-gather.19.cloned.1.call-done = bf16[1,1408,2048]{2,1,0:T(8,128)(2,1)} async-done(((bf16[1,352,2048]{2,1,0:T(8,128)(2,1)}), bf16[1,1408,2048]{2,1,0:T(8,128)(2,1)}) %all-gather.19.cloned.1.call-update) | async-done | bytes 5767184 | tf_op jit(solution)/shard_map/all_gather | solution.py:79
  256.6 3.3 convolution_convert_fusion.3
  259.8 3.1 convolution_convert_fusion.2
  263.0 2.7 convolution_convert_fusion.1
  265.7 4.5 add_convert_fusion
  270.2 20.5 %all-to-all-done.1 = bf16[8,80,2048]{2,1,0:T(8,128)(2,1)S(1)} async-done(((bf16[8,80,2048]{2,1,0:T(8,128)(2,1)}), bf16[8,80,2048]{2,1,0:T(8,128)(2,1)S(1)}, u32[]{:S(2)}, u32[]{:S(2)}) %all-to-all-start.1) | async-done | bytes 2621472 | tf_op jit(solution)/shard_map/all_to_all | solution.py:120
  290.7 4.4 all-to-all-start.2
  295.5 5.6 all_gather.26
  301.1 53.1 %all-to-all-done.2 = bf16[8,80,2048]{2,1,0:T(8,128)(2,1)} async-done(((bf16[8,80,2048]{2,1,0:T(8,128)(2,1)}), bf16[8,80,2048]{2,1,0:T(8,128)(2,1)}, u32[]{:S(2)}, u32[]{:S(2)}) %all-to-all-start.2) | async-done | bytes 2621472 | tf_op jit(solution)/shard_map/all_to_all | solution.py:120
  354.2 2.2 pad_maximum_fusion
  356.4 0.8 copy.59
  357.2 3.0 fusion.16
  360.3 4.2 fusion.12
  364.5 1.3 copy-done.3
  365.7 1.9 fusion.14
  367.6 3.2 reshape.331
  370.8 3.8 fusion.100
  374.6 1.6 copy.81
  376.2 36.7 %all-gather.13.cloned.1.call-done = bf16[2048,3,16,128]{0,3,2,1:T(8,128)(2,1)} async-done(((bf16[2048,3,4,128]{0,3,2,1:T(8,128)(2,1)}), bf16[2048,3,16,128]{0,3,2,1:T(8,128)(2,1)}) %all-gather.13.cloned.1.call-update) | async-done | bytes 25165840 | tf_op jit(solution)/shard_map/all_gather | solution.py:81
  412.9 12.5 %fusion.83 = f32[256,6144]{0,1:S(1)} fusion(bf16[2048,6144]{0,1:T(8,128)(2,1)} %bitcast.365, bf16[256,1,2048]{2,1,0:T(2,128)(2,1)S(1)} %copy-done.8), kind=kOutput, calls=%fused_computation.135 | convolution fusion | flops 6442450944 | bytes 32505856
  427.1 2.0 copy.68
  429.1 5.5 all-to-all-start.3
  435.2 13.1 %fusion.92 = f32[256,6144]{0,1:S(1)} fusion(bf16[2048,6144]{0,1:T(8,128)(2,1)} %bitcast.366, bf16[256,1,2048]{2,0,1:T(8,128)(2,1)} %copy.81), kind=kOutput, calls=%fused_computation.140 | convolution fusion | flops 6442450944 | bytes 32505856
  450.0 2.0 copy.73
  452.0 53.7 %all-to-all-done.3 = bf16[3,16,256,128]{2,3,0,1:T(8,128)(2,1)S(1)} async-done(((bf16[3,16,256,128]{2,3,0,1:T(8,128)(2,1)}), bf16[3,16,256,128]{2,3,0,1:T(8,128)(2,1)S(1)}, u32[]{:S(2)}, u32[]{:S(2)}) %all-to-all-start.3) | async-done | bytes 3145760 | tf_op jit(solution)/shard_map/all_to_all | solution.py:174
  505.7 4.5 all-to-all-start.5
  510.2 2.9 copy.69
  513.0 23.2 %shard_map.140 = bf16[2,2048,128]{2,1,0:T(8,128)(2,1)} custom-call(bf16[3,2,2048,128]{3,2,1,0:T(8,128)(2,1)} %bitcast.325, bf16[3,2,2048,128]{3,2,1,0:T(8,128)(2,1)} %bitcast.326, bf16[3,2,2048,128]{3,2,1,0:T(8,128)(2,1)} %bitcast.327), custom_call_target="tpu_custom_call" | custom-call | tf_op jit(solution)/shard_map/pallas_call | solution.py:38
  536.3 3.6 copy.70
  539.9 40.6 %all-to-all-done.5 = bf16[3,16,256,128]{2,3,0,1:T(8,128)(2,1)} async-done(((bf16[3,16,256,128]{2,3,0,1:T(8,128)(2,1)}), bf16[3,16,256,128]{2,3,0,1:T(8,128)(2,1)}, u32[]{:S(2)}, u32[]{:S(2)}) %all-to-all-start.5) | async-done | bytes 3145760 | tf_op jit(solution)/shard_map/all_to_all | solution.py:174
  580.5 3.6 all-to-all-start.4
  584.1 4.7 copy.74
  588.8 23.2 %shard_map.141 = bf16[2,2048,128]{2,1,0:T(8,128)(2,1)} custom-call(bf16[3,2,2048,128]{3,2,1,0:T(8,128)(2,1)} %bitcast.328, bf16[3,2,2048,128]{3,2,1,0:T(8,128)(2,1)} %bitcast.329, bf16[3,2,2048,128]{3,2,1,0:T(8,128)(2,1)} %bitcast.330), custom_call_target="tpu_custom_call" | custom-call | tf_op jit(solution)/shard_map/pallas_call | solution.py:38
  612.0 3.6 copy.75
  615.6 6.0 all-to-all-start.6
  621.6 3.2 reshape.330
  624.8 4.3 fusion.99
  629.4 17.9 %all-to-all-done.6 = bf16[2,2048,128]{2,0,1:T(2,128)(2,1)} async-done(((bf16[2,2048,128]{2,0,1:T(2,128)(2,1)}), bf16[2,2048,128]{2,0,1:T(2,128)(2,1)}, u32[]{:S(2)}, u32[]{:S(2)}) %all-to-all-start.6) | async-done | bytes 1048608 | tf_op jit(solution)/shard_map/all_to_all | solution.py:176
  647.3 1.4 copy.76
  648.8 2.5 fusion.45
  651.3 2.9 fusion.44
  655.7 1.2 fusion.40
  656.9 1.0 copy-done.15
  657.9 1.5 fusion.69
  662.5 1.2 fusion.30
  663.7 1.5 fusion.76
  665.4 0.9 convolution_bitcast_fusion.9
  666.3 0.9 convolution_bitcast_fusion.8
  667.2 3.5 copy.77
  (92 shorter events, 15.1 us)
Async XLA Ops:
  7.2 658.2 %copy-start = (f32[1024]{0:T(1024)S(1)}, f32[1024]{0:T(1024)}, u32[]{:S(2)}) copy-start(f32[1024]{0:T(1024)} %param.25) | copy-start | bytes 12292
  7.2 1.8 copy-start.7
  7.2 156.4 %all-gather.11.cloned.1.call-start = ((), (), s32[]{:S(2)}) async-start(), calls=%async_computation.8 | async-start | bytes 14417920 | tf_op jit(solution)/shard_map/all_gather | solution.py:77
  7.9 170.4 %all-gather.9.cloned.1.call-start = ((), (), s32[]{:S(2)}) async-start(), calls=%async_computation.7 | async-start | bytes 14417920 | tf_op jit(solution)/shard_map/all_gather | solution.py:76
  8.7 203.1 %all-gather.17.cloned.1.call-start = ((), (), s32[]{:S(2)}) async-start(), calls=%async_computation.11 | async-start | bytes 7208960 | tf_op jit(solution)/shard_map/all_gather | solution.py:79
  10.8 245.7 %all-gather.19.cloned.1.call-start = ((), (), s32[]{:S(2)}) async-start(), calls=%async_computation.12 | async-start | bytes 7208960 | tf_op jit(solution)/shard_map/all_gather | solution.py:79
  11.4 401.5 %all-gather.13.cloned.1.call-start = ((), (), s32[]{:S(2)}) async-start(), calls=%async_computation.9 | async-start | bytes 31457280 | tf_op jit(solution)/shard_map/all_gather | solution.py:81
  22.3 0.7 copy-start.9
  22.3 7.2 %copy-start.2 = (bf16[1,256,2,2048]{3,2,1,0:T(2,128)(2,1)S(1)}, bf16[1,256,2,2048]{3,2,1,0:T(2,128)(2,1)}, u32[]{:S(2)}) copy-start(bf16[1,256,2,2048]{3,2,1,0:T(2,128)(2,1)} %param.13) | copy-start | bytes 6291460
  29.5 5.2 copy-start.16
  211.7 6.4 copy-start.14
  225.3 65.4 %all-to-all-start.1 = ((bf16[8,80,2048]{2,1,0:T(8,128)(2,1)}), bf16[8,80,2048]{2,1,0:T(8,128)(2,1)S(1)}, u32[]{:S(2)}, u32[]{:S(2)}) async-start(bf16[8,80,2048]{2,1,0:T(8,128)(2,1)} %add_convert_fusion.1), calls=%async_computation.1 | async-start | bytes 5242880 | tf_op jit(solution)/shard_map/all_to_all | solution.py:120
  256.6 6.4 copy-start.13
  270.2 24.9 %copy-start.11 = (f32[1,256,2,2]{1,3,2,0:T(2,128)S(1)}, f32[1,256,2,2]{1,3,2,0:T(2,128)}, u32[]{:S(2)}) copy-start(f32[1,256,2,2]{1,3,2,0:T(2,128)} %param.15) | copy-start | bytes 12292
  270.2 25.2 %copy-start.12 = (f32[2,4,128]{2,1,0:T(4,128)S(1)}, f32[2,4,128]{2,1,0:T(4,128)}, u32[]{:S(2)}) copy-start(f32[2,4,128]{2,1,0:T(4,128)} %param.22) | copy-start | bytes 12292
  290.7 63.5 %all-to-all-start.2 = ((bf16[8,80,2048]{2,1,0:T(8,128)(2,1)}), bf16[8,80,2048]{2,1,0:T(8,128)(2,1)}, u32[]{:S(2)}, u32[]{:S(2)}) async-start(bf16[8,80,2048]{2,1,0:T(8,128)(2,1)} %add_convert_fusion), calls=%async_computation.2 | async-start | bytes 5242880 | tf_op jit(solution)/shard_map/all_to_all | solution.py:120
  357.2 3.0 copy-start.6
  360.3 5.5 copy-start.10
  364.4 1.3 copy-start.3
  374.6 38.3 %copy-start.8 = (bf16[256,1,2048]{2,1,0:T(2,128)(2,1)S(1)}, bf16[256,1,2048]{2,1,0:T(2,128)(2,1)}, u32[]{:S(2)}) copy-start(bf16[256,1,2048]{2,1,0:T(2,128)(2,1)} %get-tuple-element.24) | copy-start | bytes 3145732
  429.1 76.6 %all-to-all-start.3 = ((bf16[3,16,256,128]{2,3,0,1:T(8,128)(2,1)}), bf16[3,16,256,128]{2,3,0,1:T(8,128)(2,1)S(1)}, u32[]{:S(2)}, u32[]{:S(2)}) async-start(bf16[3,16,256,128]{2,3,0,1:T(8,128)(2,1)} %copy.68), calls=%async_computation.3 | async-start | bytes 6291456 | tf_op jit(solution)/shard_map/all_to_all | solution.py:174
  434.6 214.2 %all-gather.15.cloned.1.call-start = ((), (), s32[]{:S(2)}) async-start(), calls=%async_computation.10 | async-start | bytes 10485760 | tf_op jit(solution)/shard_map/all_gather | solution.py:83
  505.7 74.8 %all-to-all-start.5 = ((bf16[3,16,256,128]{2,3,0,1:T(8,128)(2,1)}), bf16[3,16,256,128]{2,3,0,1:T(8,128)(2,1)}, u32[]{:S(2)}, u32[]{:S(2)}) async-start(bf16[3,16,256,128]{2,3,0,1:T(8,128)(2,1)} %copy.73), calls=%async_computation.5 | async-start | bytes 6291456 | tf_op jit(solution)/shard_map/all_to_all | solution.py:174
  580.5 35.2 %all-to-all-start.4 = ((bf16[2,2048,128]{2,0,1:T(2,128)(2,1)}), bf16[2,2048,128]{2,0,1:T(2,128)(2,1)S(1)}, u32[]{:S(2)}, u32[]{:S(2)}) async-start(bf16[2,2048,128]{2,0,1:T(2,128)(2,1)} %copy.70), calls=%async_computation.4 | async-start | bytes 2097152 | tf_op jit(solution)/shard_map/all_to_all | solution.py:176
  615.6 31.7 %all-to-all-start.6 = ((bf16[2,2048,128]{2,0,1:T(2,128)(2,1)}), bf16[2,2048,128]{2,0,1:T(2,128)(2,1)}, u32[]{:S(2)}, u32[]{:S(2)}) async-start(bf16[2,2048,128]{2,0,1:T(2,128)(2,1)} %copy.75), calls=%async_computation.6 | async-start | bytes 2097152 | tf_op jit(solution)/shard_map/all_to_all | solution.py:176
  648.8 5.4 copy-start.1
  654.2 1.6 copy-start.5
  655.7 2.2 copy-start.15
  660.9 1.6 copy-start.4
Sparse Core Ops, SparseCore 0:
  9.6 78.8 all-gather.10
  90.0 76.1 all-gather.8
  168.3 43.3 all-gather.16
  213.1 43.3 all-gather.18
  258.0 154.8 all-gather.12
  436.6 58.7 all-gather.14

commit v11 on v10

--- a/solution.py
+++ b/solution.py
@@ -32,21 +32,22 @@
     )
 
 
-def attention(whole, scale, interpret=False):
-    _, pairs, seq_len, head_size = whole.shape
+def attention(sent, scale, interpret=False):
+    query, key, value = sent
+    pairs, seq_len, head_size = query.shape
     block = min(256, seq_len)
     return pl.pallas_call(
         functools.partial(attention_kernel, scale=scale),
         grid=(pairs, seq_len // block),
         in_specs=[
-            pl.BlockSpec((None, None, block, head_size), lambda p, i: (0, p, i, 0)),
-            pl.BlockSpec((None, None, seq_len, head_size), lambda p, i: (1, p, 0, 0)),
-            pl.BlockSpec((None, None, seq_len, head_size), lambda p, i: (2, p, 0, 0)),
+            pl.BlockSpec((None, block, head_size), lambda p, i: (p, i, 0)),
+            pl.BlockSpec((None, seq_len, head_size), lambda p, i: (p, 0, 0)),
+            pl.BlockSpec((None, seq_len, head_size), lambda p, i: (p, 0, 0)),
         ],
         out_specs=pl.BlockSpec((None, block, head_size), lambda p, i: (p, i, 0)),
-        out_shape=jax.ShapeDtypeStruct((pairs, seq_len, head_size), whole.dtype),
+        out_shape=jax.ShapeDtypeStruct((pairs, seq_len, head_size), query.dtype),
         interpret=interpret,
-    )(whole, whole, whole)
+    )(query, key, value)
 
 
 def local(
@@ -78,7 +79,9 @@
     down_parts = [
         lax.all_gather(expert_down[j], "rep", axis=0, tiled=True) for j in range(exp_local)
     ]
-    qkv_full = lax.all_gather(teacher_qkv, "rep", axis=2, tiled=True)
+    qkv_full = [
+        lax.all_gather(teacher_qkv[:, j], "rep", axis=1, tiled=True) for j in range(3)
+    ]
     qk_gain_full = lax.all_gather(qk_gain, "rep", axis=1, tiled=True)
     out_full = lax.all_gather(teacher_out, "rep", axis=0, tiled=True)
     residual = tokens.reshape(tok_count, width).astype(jnp.float32)
@@ -130,21 +133,25 @@
     teacher_in = norm_rows(mixed.astype(jnp.float32), teacher_gain).astype(jnp.bfloat16)
     teacher_in = teacher_in.reshape(seq_dev, images, width)
     mixed = mixed.reshape(seq_dev, images, width)
-    heads_all = qkv_full.shape[2]
-    head_size = qkv_full.shape[3]
+    heads_all = qkv_full[0].shape[1]
+    head_size = qkv_full[0].shape[2]
     chunks = images if (heads_all % n_owner == 0) else 1
     per_chunk = images // chunks
     features_parts = []
     logits_parts = []
-    grouped_parts = []
+    sent_parts = []
     for chunk in range(chunks):
         chunk_in = teacher_in[:, chunk * per_chunk:(chunk + 1) * per_chunk]
-        if grouped_parts:
-            chunk_in, grouped_parts[-1] = lax.optimization_barrier((chunk_in, grouped_parts[-1]))
-        grouped_parts.append(project(chunk_in, qkv_full, qk_gain_full))
+        if sent_parts:
+            chunk_in, sent_parts[-1] = lax.optimization_barrier((chunk_in, sent_parts[-1]))
+        sent = []
+        for j in range(3):
+            gain = qk_gain_full[j] if j < 2 else None
+            sent.append(project(chunk_in, qkv_full[j], gain))
+        sent_parts.append(tuple(sent))
     for chunk in range(chunks):
         features, logits = teach(
-            grouped_parts[chunk], mixed[:, chunk * per_chunk:(chunk + 1) * per_chunk], out_full,
+            sent_parts[chunk], mixed[:, chunk * per_chunk:(chunk + 1) * per_chunk], out_full,
             critic_in, critic_out, n_replica,
         )
         features_parts.append(features)
@@ -154,25 +161,24 @@
     return (features.reshape(1, seq_dev, images, width), logits.reshape(1, seq_dev, images))
 
 
-def project(teacher_in, qkv_full, qk_gain_full):
+def project(teacher_in, weights, gain):
     seq_dev, images, width = teacher_in.shape
-    heads_all = qkv_full.shape[2]
-    head_size = qkv_full.shape[3]
+    heads_all = weights.shape[1]
+    head_size = weights.shape[2]
     projected = jnp.einsum(
-        "sid,djhe->jihse", teacher_in, qkv_full, preferred_element_type=jnp.float32
-    )
-    query = norm_rows(projected[0], qk_gain_full[0][:, None, :])
-    keyed = norm_rows(projected[1], qk_gain_full[1][:, None, :])
-    projected = jnp.stack([query, keyed, projected[2]]).astype(jnp.bfloat16)
-    return projected.reshape(3, images * heads_all, seq_dev, head_size)
-
-
-def teach(grouped, mixed, out_full, critic_in, critic_out, n_replica):
+        "sid,dhe->ihse", teacher_in, weights, preferred_element_type=jnp.float32
+    )
+    if gain is not None:
+        projected = norm_rows(projected, gain[:, None, :])
+    projected = projected.astype(jnp.bfloat16).reshape(images * heads_all, seq_dev, head_size)
+    return lax.all_to_all(projected, "expert", split_axis=0, concat_axis=1, tiled=True)
+
+
+def teach(sent, mixed, out_full, critic_in, critic_out, n_replica):
     seq_dev, images, width = mixed.shape
     heads_all = out_full.shape[0]
     head_size = out_full.shape[1]
-    whole = lax.all_to_all(grouped, "expert", split_axis=1, concat_axis=2, tiled=True)
-    attended = attention(whole, head_size ** (-0.5))
+    attended = attention(sent, head_size ** (-0.5))
     gathered_heads = lax.all_to_all(attended, "expert", split_axis=1, concat_axis=0, tiled=True)
     gathered_heads = gathered_heads.reshape(images, heads_all, seq_dev, head_size)
     heads_part = heads_all // n_replica

time: 686 us -> 730 us (1.064)
  blocking collectives: 129 us -> 5.4 us
  waiting for transfers between devices: 267 us -> 359 us
  local copies, waits for them, and re-layouts: 63.7 us -> 88.8 us
  matrix products: 112 us -> 137 us
  starting transfers between devices: 29.7 us -> 51.2 us
    all_to_all x1 -> x0, blocking collectives: 123 us -> none  [local(): lax.all_to_all(outgoing, 'expert', split_axis=0, concat_axis=0, tiled=True)]
    all_to_all x2 -> x7, waiting for transfers between devices: 94.3 us -> 202 us  [the longest x1 114 us: local(): lax.all_to_all(outgoing, 'expert', split_axis=0, concat_axis=0, tiled=True)]
    all_to_all x2, waiting for transfers between devices: 73.5 us -> 45.6 us  [local(): lax.all_to_all(produced.astype(jnp.bfloat16), 'expert', split_axis=0, con...]
    all_gather x0 -> x2, local copies, waits for them, and re-layouts: none -> 25.3 us  [local(): lax.all_gather(teacher_qkv[:, j], 'rep', axis=1, tiled=True)]
    all_to_all x2 -> x7, starting transfers between devices: 9.97 us -> 33.1 us  [the longest x6 25.7 us: project(): lax.all_to_all(projected, 'expert', split_axis=0, concat_axis=1, tiled=True)]
    all_to_all x2, waiting for transfers between devices: 17.9 us -> 33.4 us  [teach(): lax.all_to_all(attended, 'expert', split_axis=1, concat_axis=0, tiled=True)]
    dot_general x0 -> x2, matrix products: none -> 15 us  [project(): jnp.einsum('sid,dhe->ihse', teacher_in, weights, preferred_element_type=j...]
    unnamed x39 -> x57, local copies, waits for them, and re-layouts: 19.6 us -> 15.7 us
  transfers between devices with their start and end apart: 12 -> 19, of which waited for: 8 -> 14; matrix products, arithmetic and copies ran while one was open for 22% -> 31% of each run, Pallas kernels for 7% -> 6%
where the time goes in v11:
time: 730 us; the launch traced here: 720 us
  waiting for transfers between devices  359 us (49%)
  matrix products  137 us (19%)
  local copies, waits for them, and re-layouts  88.8 us (12%)
  starting transfers between devices  51.2 us (7%)
  Pallas kernels  46.5 us (6%)
  other arithmetic  17.9 us (2%)
  between operations  15.3 us (2%)
    all_to_all x1, waiting for transfers between devices, local(): lax.all_to_all(outgoing, 'expert', split_axis=0, concat_axis=0, tiled=True)  114 us
    all_to_all x6, waiting for transfers between devices, project(): lax.all_to_all(projected, 'expert', split_axis=0, concat_axis=1, tiled=True)  88.1 us
    pallas_call x2, Pallas kernels, attention(): pl.pallas_call(functools.partial(attention_kernel, scale=scale), grid=(pa...  46.5 us
    all_to_all x2, waiting for transfers between devices, local(): lax.all_to_all(produced.astype(jnp.bfloat16), 'expert', split_axis=0, con...  45.6 us
    all_gather x2, waiting for transfers between devices, local(): lax.all_gather(expert_down[j], 'rep', axis=0, tiled=True)  40.2 us
    all_gather x3, waiting for transfers between devices, local(): lax.all_gather(teacher_qkv[:, j], 'rep', axis=1, tiled=True)  34.8 us
    all_to_all x2, waiting for transfers between devices, teach(): lax.all_to_all(attended, 'expert', split_axis=1, concat_axis=0, tiled=True)  33.4 us
    dot_general x8, matrix products, local(): jnp.einsum('scf,fd->scd', hidden[:, j, :, low:low + ff_part], down_w[low:...  27.1 us
  transfers between devices with their start and end apart: 19, of which 14 were waited for; matrix products, arithmetic and copies ran while one was open for 31% of the time, Pallas kernels for 6%

profile of v11, /device:TPU:0, one launch (start us, length us, event | category | flops | bytes accessed | tf_op | source)
XLA Modules:
  0.0 720.5 jit_solution(376997714351190815)
XLA Ops:
  11.5 5.4 fusion.122
  19.4 4.5 reduce-window.6
  25.0 2.7 reshape.276
  30.1 7.8 %convolution_convert_fusion = bf16[1280,2048]{1,0:T(8,128)(2,1)} fusion(f32[512,2048]{1,0:T(8,128)} %reshape.276, f32[2048]{0:T(1024)S(1)} %copy-done.24, f32[512]{0:T(512)S(1)} %rsqrt.52, s32[512]{0:T(512)S(1)} %bitcast.436, s32[512]{0:T(512)S(1)} %bitcast.438), kind=kOutput, calls=%fused_computation.8 | convolution fusion | flops 2695364608 | bytes 9451520 | tf_op jit(solution)/shard_map/tr,td->rd/dot_general | solution.py:98
  37.9 7.4 %all-to-all-start = ((bf16[8,160,2048]{2,1,0:T(8,128)(2,1)}), bf16[8,160,2048]{2,1,0:T(8,128)(2,1)}, u32[]{:S(2)}, u32[]{:S(2)}) async-start(bf16[8,160,2048]{2,1,0:T(8,128)(2,1)} %bitcast.408), calls=%async_computation | async-start | bytes 10485760 | tf_op jit(solution)/shard_map/all_to_all | solution.py:102
  47.2 114.0 %all-to-all-done = bf16[8,160,2048]{2,1,0:T(8,128)(2,1)} async-done(((bf16[8,160,2048]{2,1,0:T(8,128)(2,1)}), bf16[8,160,2048]{2,1,0:T(8,128)(2,1)}, u32[]{:S(2)}, u32[]{:S(2)}) %all-to-all-start) | async-done | bytes 5242912 | tf_op jit(solution)/shard_map/all_to_all | solution.py:102
  161.2 14.7 %fusion = f32[2,8,80,1408]{3,2,1,0:T(8,128)} fusion(bf16[2,2048,1408]{1,2,0:T(8,128)(2,1)} %all-gather.16.cloned.1.call-done, bf16[8,2,80,2048]{3,2,1,0:T(8,128)(2,1)} %bitcast.5), kind=kOutput, calls=%fused_computation | convolution fusion | flops 7381975040 | bytes 23986176 | tf_op jit(solution)/shard_map/sjcd,jdf->sjcf/dot_general | solution.py:107
  176.0 17.5 %fusion.8 = bf16[8,2,80,1408]{3,2,0,1:T(8,128)(2,1)} fusion(f32[2,8,80,1408]{3,2,1,0:T(8,128)} %fusion, bf16[2,2048,1408]{1,2,0:T(8,128)(2,1)} %all-gather.14.cloned.1.call-done, bf16[8,2,80,2048]{3,2,1,0:T(8,128)(2,1)} %bitcast.5), kind=kOutput, calls=%fused_computation.10 | convolution fusion | flops 7392788480 | bytes 27590656 | tf_op jit(solution)/shard_map/sjcd,jdf->sjcf/dot_general | solution.py:104
  193.5 17.7 %all-gather.20.cloned.1.call-done = bf16[1,1408,2048]{2,1,0:T(8,128)(2,1)} async-done(((bf16[1,352,2048]{2,1,0:T(8,128)(2,1)}), bf16[1,1408,2048]{2,1,0:T(8,128)(2,1)}) %all-gather.20.cloned.1.call-update) | async-done | bytes 5767184 | tf_op jit(solution)/shard_map/all_gather | solution.py:80
  211.2 3.2 convolution_convert_fusion.5
  214.4 3.1 convolution_convert_fusion.6
  217.5 2.7 convolution_convert_fusion.7
  220.3 4.5 add_convert_fusion.1
  224.7 5.5 all-to-all-start.1
  230.3 3.2 copy.95
  233.5 22.5 %all-gather.22.cloned.1.call-done = bf16[1,1408,2048]{2,1,0:T(8,128)(2,1)} async-done(((bf16[1,352,2048]{2,1,0:T(8,128)(2,1)}), bf16[1,1408,2048]{2,1,0:T(8,128)(2,1)}) %all-gather.22.cloned.1.call-update) | async-done | bytes 5767184 | tf_op jit(solution)/shard_map/all_gather | solution.py:80
  256.0 3.2 convolution_convert_fusion.1
  259.2 3.1 convolution_convert_fusion.2
  262.4 2.7 convolution_convert_fusion.3
  265.1 4.5 add_convert_fusion
  269.6 20.6 %all-to-all-done.1 = bf16[8,80,2048]{2,1,0:T(8,128)(2,1)S(1)} async-done(((bf16[8,80,2048]{2,1,0:T(8,128)(2,1)}), bf16[8,80,2048]{2,1,0:T(8,128)(2,1)S(1)}, u32[]{:S(2)}, u32[]{:S(2)}) %all-to-all-start.1) | async-done | bytes 2621472 | tf_op jit(solution)/shard_map/all_to_all | solution.py:123
  290.1 4.4 all-to-all-start.2
  294.9 5.4 all_gather.32
  300.3 15.4 %all-gather.26.cloned.1.call-done = bf16[2048,1,16,128]{3,0,1,2:T(8,128)(2,1)} async-done(((bf16[2048,1,4,128]{3,0,1,2:T(8,128)(2,1)}), bf16[2048,1,16,128]{3,0,1,2:T(8,128)(2,1)}) %all-gather.26.cloned.1.call-update) | async-done | bytes 8388624 | tf_op jit(solution)/shard_map/all_gather | solution.py:83
  315.8 12.9 %copy.77 = bf16[2048,1,16,128]{0,3,2,1:T(8,128)(2,1)} copy(bf16[2048,1,16,128]{3,0,1,2:T(8,128)(2,1)} %all-gather.26.cloned.1.call-done) | data formatting | bytes 16777216 | tf_op jit(solution)/shard_map/all_gather | solution.py:83
  328.6 25.0 %all-to-all-done.2 = bf16[8,80,2048]{2,1,0:T(8,128)(2,1)} async-done(((bf16[8,80,2048]{2,1,0:T(8,128)(2,1)}), bf16[8,80,2048]{2,1,0:T(8,128)(2,1)}, u32[]{:S(2)}, u32[]{:S(2)}) %all-to-all-start.2) | async-done | bytes 2621472 | tf_op jit(solution)/shard_map/all_to_all | solution.py:123
  356.7 3.0 fusion.20
  359.7 4.2 fusion.16
  367.1 3.2 reshape.251
  370.3 3.8 fusion.125
  374.2 6.8 fusion.111
  382.5 3.9 all-to-all-start.4
  387.2 8.3 %fusion.69 = bf16[16,256,128]{2,1,0:T(8,128)(2,1)} fusion(bf16[2048,1,16,128]{3,0,1,2:T(8,128)(2,1)} %all-gather.28.cloned.1.call-done, bf16[256,1,2048]{2,1,0:T(2,128)(2,1)S(1)} %copy-done.14), kind=kOutput, calls=%fused_computation.110 | convolution fusion | flops 2148007936 | bytes 10485760 | tf_op jit(solution)/shard_map/sid,dhe->ihse/dot_general | solution.py:168
  395.5 16.7 %all-to-all-done.4 = bf16[16,256,128]{1,2,0:T(8,128)(2,1)S(1)} async-done(((bf16[16,256,128]{1,2,0:T(8,128)(2,1)}), bf16[16,256,128]{1,2,0:T(8,128)(2,1)S(1)}, u32[]{:S(2)}, u32[]{:S(2)}) %all-to-all-start.4) | async-done | bytes 1048608 | tf_op jit(solution)/shard_map/all_to_all | solution.py:174
  412.3 4.3 all-to-all-start.5
  416.5 19.4 %all-gather.24.cloned.1.call-done = bf16[2048,1,16,128]{3,0,1,2:T(8,128)(2,1)} async-done(((bf16[2048,1,4,128]{3,0,1,2:T(8,128)(2,1)}), bf16[2048,1,16,128]{3,0,1,2:T(8,128)(2,1)}) %all-gather.24.cloned.1.call-update) | async-done | bytes 8388624 | tf_op jit(solution)/shard_map/all_gather | solution.py:83
  435.9 12.4 %copy.73 = bf16[2048,1,16,128]{0,3,2,1:T(8,128)(2,1)} copy(bf16[2048,1,16,128]{3,0,1,2:T(8,128)(2,1)} %all-gather.24.cloned.1.call-done) | data formatting | bytes 16777216 | tf_op jit(solution)/shard_map/all_gather | solution.py:83
  448.3 6.5 fusion.113
  456.4 5.8 all-to-all-start.3
  467.4 21.0 %all-to-all-done.3 = bf16[16,256,128]{1,2,0:T(8,128)(2,1)} async-done(((bf16[16,256,128]{1,2,0:T(8,128)(2,1)}), bf16[16,256,128]{1,2,0:T(8,128)(2,1)}, u32[]{:S(2)}, u32[]{:S(2)}) %all-to-all-start.3) | async-done | bytes 1048608 | tf_op jit(solution)/shard_map/all_to_all | solution.py:174
  490.7 23.2 %shard_map.140 = bf16[2,2048,128]{2,1,0:T(8,128)(2,1)} custom-call(bf16[2,2048,128]{2,1,0:T(8,128)(2,1)} %bitcast.428, bf16[2,2048,128]{2,1,0:T(8,128)(2,1)} %bitcast.424, bf16[2,2048,128]{2,1,0:T(8,128)(2,1)} %bitcast.426), custom_call_target="tpu_custom_call" | custom-call | tf_op jit(solution)/shard_map/pallas_call | solution.py:39
  513.9 3.7 copy.81
  517.6 3.7 all-to-all-start.6
  521.3 6.7 fusion.66
  528.0 19.2 %all-to-all-done.6 = bf16[2,2048,128]{2,0,1:T(2,128)(2,1)S(1)} async-done(((bf16[2,2048,128]{2,0,1:T(2,128)(2,1)}), bf16[2,2048,128]{2,0,1:T(2,128)(2,1)S(1)}, u32[]{:S(2)}, u32[]{:S(2)}) %all-to-all-start.6) | async-done | bytes 1048608 | tf_op jit(solution)/shard_map/all_to_all | solution.py:182
  547.2 3.9 all-to-all-start.9
  551.1 5.9 fusion.106
  558.6 18.4 %all-to-all-done.9 = bf16[16,256,128]{2,1,0:T(8,128)(2,1)S(1)} async-done(((bf16[16,256,128]{2,1,0:T(8,128)(2,1)}), bf16[16,256,128]{2,1,0:T(8,128)(2,1)S(1)}, u32[]{:S(2)}, u32[]{:S(2)}) %all-to-all-start.9) | async-done | bytes 1048608 | tf_op jit(solution)/shard_map/all_to_all | solution.py:174
  577.0 3.6 all-to-all-start.8
  580.7 6.2 fusion.108
  588.4 18.2 %all-to-all-done.8 = bf16[16,256,128]{1,2,0:T(8,128)(2,1)S(1)} async-done(((bf16[16,256,128]{1,2,0:T(8,128)(2,1)}), bf16[16,256,128]{1,2,0:T(8,128)(2,1)S(1)}, u32[]{:S(2)}, u32[]{:S(2)}) %all-to-all-start.8) | async-done | bytes 1048608 | tf_op jit(solution)/shard_map/all_to_all | solution.py:174
  607.6 4.3 all-to-all-start.7
  611.9 3.2 reshape.250
  615.0 4.2 fusion.124
  623.8 13.7 %all-to-all-done.7 = bf16[16,256,128]{1,2,0:T(8,128)(2,1)} async-done(((bf16[16,256,128]{1,2,0:T(8,128)(2,1)}), bf16[16,256,128]{1,2,0:T(8,128)(2,1)}, u32[]{:S(2)}, u32[]{:S(2)}) %all-to-all-start.7) | async-done | bytes 1048608 | tf_op jit(solution)/shard_map/all_to_all | solution.py:174
  639.7 23.2 %shard_map.141 = bf16[2,2048,128]{2,1,0:T(8,128)(2,1)} custom-call(bf16[2,2048,128]{2,1,0:T(8,128)(2,1)} %bitcast.429, bf16[2,2048,128]{2,1,0:T(8,128)(2,1)} %bitcast.427, bf16[2,2048,128]{2,1,0:T(8,128)(2,1)} %bitcast.425), custom_call_target="tpu_custom_call" | custom-call | tf_op jit(solution)/shard_map/pallas_call | solution.py:39
  662.9 3.6 copy.87
  666.6 3.8 all-to-all-start.10
  670.4 2.5 fusion.49
  672.9 2.9 fusion.48
  682.0 14.2 %all-to-all-done.10 = bf16[2,2048,128]{2,0,1:T(2,128)(2,1)S(1)} async-done(((bf16[2,2048,128]{2,0,1:T(2,128)(2,1)}), bf16[2,2048,128]{2,0,1:T(2,128)(2,1)S(1)}, u32[]{:S(2)}, u32[]{:S(2)}) %all-to-all-start.10) | async-done | bytes 1048608 | tf_op jit(solution)/shard_map/all_to_all | solution.py:182
  701.1 2.5 fusion.36
  703.6 2.9 fusion.34
  709.1 3.5 copy.89
  (135 shorter events, 55.0 us)
Async XLA Ops:
  7.2 673.9 %copy-start = (f32[1024]{0:T(1024)S(1)}, f32[1024]{0:T(1024)}, u32[]{:S(2)}) copy-start(f32[1024]{0:T(1024)} %param.25) | copy-start | bytes 12292
  7.2 1.8 copy-start.12
  7.2 154.0 %all-gather.16.cloned.1.call-start = ((), (), s32[]{:S(2)}) async-start(), calls=%async_computation.12 | async-start | bytes 14417920 | tf_op jit(solution)/shard_map/all_gather | solution.py:78
  7.9 168.0 %all-gather.14.cloned.1.call-start = ((), (), s32[]{:S(2)}) async-start(), calls=%async_computation.11 | async-start | bytes 14417920 | tf_op jit(solution)/shard_map/all_gather | solution.py:77
  8.7 202.5 %all-gather.20.cloned.1.call-start = ((), (), s32[]{:S(2)}) async-start(), calls=%async_computation.14 | async-start | bytes 7208960 | tf_op jit(solution)/shard_map/all_gather | solution.py:80
  10.8 245.2 %all-gather.22.cloned.1.call-start = ((), (), s32[]{:S(2)}) async-start(), calls=%async_computation.15 | async-start | bytes 7208960 | tf_op jit(solution)/shard_map/all_gather | solution.py:80
  11.4 304.4 %all-gather.26.cloned.1.call-start = ((), (), s32[]{:S(2)}) async-start(), calls=%async_computation.17 | async-start | bytes 10485760 | tf_op jit(solution)/shard_map/all_gather | solution.py:83
  16.9 1.6 copy-start.16
  18.5 6.5 copy-start.2
  27.7 2.4 copy-start.24
  37.9 7.6 %copy-start.4 = (bf16[2048,1,4,128]{3,2,1,0:T(4,128)(2,1)S(1)}, bf16[2048,1,4,128]{3,2,1,0:T(4,128)(2,1)}, u32[]{:S(2)}) copy-start(bf16[2048,1,4,128]{3,2,1,0:T(4,128)(2,1)} %get-tuple-element.16) | copy-start | bytes 6291460
  37.9 123.3 %all-to-all-start = ((bf16[8,160,2048]{2,1,0:T(8,128)(2,1)}), bf16[8,160,2048]{2,1,0:T(8,128)(2,1)}, u32[]{:S(2)}, u32[]{:S(2)}) async-start(bf16[8,160,2048]{2,1,0:T(8,128)(2,1)} %bitcast.408), calls=%async_computation | async-start | bytes 10485760 | tf_op jit(solution)/shard_map/all_to_all | solution.py:102
  45.4 341.8 %all-gather.28.cloned.1.call-start = ((), (), s32[]{:S(2)}) async-start(), calls=%async_computation.18 | async-start | bytes 10485760 | tf_op jit(solution)/shard_map/all_gather | solution.py:83
  211.2 6.4 copy-start.21
  224.7 65.4 %all-to-all-start.1 = ((bf16[8,80,2048]{2,1,0:T(8,128)(2,1)}), bf16[8,80,2048]{2,1,0:T(8,128)(2,1)S(1)}, u32[]{:S(2)}, u32[]{:S(2)}) async-start(bf16[8,80,2048]{2,1,0:T(8,128)(2,1)} %add_convert_fusion.1), calls=%async_computation.1 | async-start | bytes 5242880 | tf_op jit(solution)/shard_map/all_to_all | solution.py:123
  230.2 205.7 %all-gather.24.cloned.1.call-start = ((), (), s32[]{:S(2)}) async-start(), calls=%async_computation.16 | async-start | bytes 10485760 | tf_op jit(solution)/shard_map/all_gather | solution.py:83
  256.0 6.4 copy-start.20
  269.6 25.0 %copy-start.18 = (f32[1,256,2,2]{1,3,2,0:T(2,128)S(1)}, f32[1,256,2,2]{1,3,2,0:T(2,128)}, u32[]{:S(2)}) copy-start(f32[1,256,2,2]{1,3,2,0:T(2,128)} %param.15) | copy-start | bytes 12292
  269.6 25.3 %copy-start.19 = (f32[2,4,128]{2,1,0:T(4,128)S(1)}, f32[2,4,128]{2,1,0:T(4,128)}, u32[]{:S(2)}) copy-start(f32[2,4,128]{2,1,0:T(4,128)} %param.22) | copy-start | bytes 12292
  290.1 63.5 %all-to-all-start.2 = ((bf16[8,80,2048]{2,1,0:T(8,128)(2,1)}), bf16[8,80,2048]{2,1,0:T(8,128)(2,1)}, u32[]{:S(2)}, u32[]{:S(2)}) async-start(bf16[8,80,2048]{2,1,0:T(8,128)(2,1)} %add_convert_fusion), calls=%async_computation.2 | async-start | bytes 5242880 | tf_op jit(solution)/shard_map/all_to_all | solution.py:123
  356.7 3.0 copy-start.8
  359.7 5.5 copy-start.17
  363.9 1.3 copy-start.3
  374.2 6.8 copy-start.13
  382.5 4.6 copy-start.14
  382.5 29.7 %all-to-all-start.4 = ((bf16[16,256,128]{1,2,0:T(8,128)(2,1)}), bf16[16,256,128]{1,2,0:T(8,128)(2,1)S(1)}, u32[]{:S(2)}, u32[]{:S(2)}) async-start(bf16[16,256,128]{1,2,0:T(8,128)(2,1)} %fusion.94), calls=%async_computation.4 | async-start | bytes 2097152 | tf_op jit(solution)/shard_map/all_to_all | solution.py:174
  386.4 284.0 %all-gather.18.cloned.1.call-start = ((), (), s32[]{:S(2)}) async-start(), calls=%async_computation.13 | async-start | bytes 10485760 | tf_op jit(solution)/shard_map/all_gather | solution.py:86
  412.3 44.2 %all-to-all-start.5 = ((bf16[16,256,128]{2,1,0:T(8,128)(2,1)}), bf16[16,256,128]{2,1,0:T(8,128)(2,1)}, u32[]{:S(2)}, u32[]{:S(2)}) async-start(bf16[16,256,128]{2,1,0:T(8,128)(2,1)} %fusion.69), calls=%async_computation.5 | async-start | bytes 2097152 | tf_op jit(solution)/shard_map/all_to_all | solution.py:174
  455.1 7.2 copy-start.5
  456.4 32.0 %all-to-all-start.3 = ((bf16[16,256,128]{1,2,0:T(8,128)(2,1)}), bf16[16,256,128]{1,2,0:T(8,128)(2,1)}, u32[]{:S(2)}, u32[]{:S(2)}) async-start(bf16[16,256,128]{1,2,0:T(8,128)(2,1)} %fusion.93), calls=%async_computation.3 | async-start | bytes 2097152 | tf_op jit(solution)/shard_map/all_to_all | solution.py:174
  513.9 7.4 %copy-start.15 = (bf16[256,1,2048]{2,0,1:T(8,128)(2,1)S(1)}, bf16[256,1,2048]{2,0,1:T(8,128)(2,1)}, u32[]{:S(2)}) copy-start(bf16[256,1,2048]{2,0,1:T(8,128)(2,1)} %copy.93) | copy-start | bytes 3145732
  517.6 29.6 %all-to-all-start.6 = ((bf16[2,2048,128]{2,0,1:T(2,128)(2,1)}), bf16[2,2048,128]{2,0,1:T(2,128)(2,1)S(1)}, u32[]{:S(2)}, u32[]{:S(2)}) async-start(bf16[2,2048,128]{2,0,1:T(2,128)(2,1)} %copy.81), calls=%async_computation.6 | async-start | bytes 2097152 | tf_op jit(solution)/shard_map/all_to_all | solution.py:182
  547.2 29.8 %all-to-all-start.9 = ((bf16[16,256,128]{2,1,0:T(8,128)(2,1)}), bf16[16,256,128]{2,1,0:T(8,128)(2,1)S(1)}, u32[]{:S(2)}, u32[]{:S(2)}) async-start(bf16[16,256,128]{2,1,0:T(8,128)(2,1)} %fusion.66), calls=%async_computation.9 | async-start | bytes 2097152 | tf_op jit(solution)/shard_map/all_to_all | solution.py:174
  577.0 9.9 %copy-start.9 = (bf16[16,256,128]{2,1,0:T(8,128)(2,1)}, bf16[16,256,128]{2,1,0:T(8,128)(2,1)S(1)}, u32[]{:S(2)}) copy-start(bf16[16,256,128]{2,1,0:T(8,128)(2,1)S(1)} %all-to-all-done.9) | copy-start | bytes 3145732
  577.0 29.6 %all-to-all-start.8 = ((bf16[16,256,128]{1,2,0:T(8,128)(2,1)}), bf16[16,256,128]{1,2,0:T(8,128)(2,1)S(1)}, u32[]{:S(2)}, u32[]{:S(2)}) async-start(bf16[16,256,128]{1,2,0:T(8,128)(2,1)} %fusion.96), calls=%async_computation.8 | async-start | bytes 2097152 | tf_op jit(solution)/shard_map/all_to_all | solution.py:174
  606.6 1.0 copy-start.11
  607.6 29.9 %all-to-all-start.7 = ((bf16[16,256,128]{1,2,0:T(8,128)(2,1)}), bf16[16,256,128]{1,2,0:T(8,128)(2,1)}, u32[]{:S(2)}, u32[]{:S(2)}) async-start(bf16[16,256,128]{1,2,0:T(8,128)(2,1)} %fusion.95), calls=%async_computation.7 | async-start | bytes 2097152 | tf_op jit(solution)/shard_map/all_to_all | solution.py:174
  619.2 1.2 copy-start.10
  666.6 29.6 %all-to-all-start.10 = ((bf16[2,2048,128]{2,0,1:T(2,128)(2,1)}), bf16[2,2048,128]{2,0,1:T(2,128)(2,1)S(1)}, u32[]{:S(2)}, u32[]{:S(2)}) async-start(bf16[2,2048,128]{2,0,1:T(2,128)(2,1)} %copy.87), calls=%async_computation.10 | async-start | bytes 2097152 | tf_op jit(solution)/shard_map/all_to_all | solution.py:182
  670.4 5.4 copy-start.1
  675.8 1.6 copy-start.7
  677.4 2.2 copy-start.22
  701.1 2.5 copy-start.6
  703.6 2.9 copy-start.23
Sparse Core Ops, SparseCore 0:
  9.6 78.8 all-gather.15
  90.0 76.0 all-gather.13
  167.7 43.3 all-gather.19
  212.6 43.3 all-gather.21
  257.4 58.3 all-gather.25
  317.2 58.2 all-gather.27
  377.6 58.2 all-gather.23
  437.5 58.2 all-gather.17

commit v12 on v10

--- a/solution.py
+++ b/solution.py
@@ -34,7 +34,7 @@
 
 def attention(whole, scale, interpret=False):
     _, pairs, seq_len, head_size = whole.shape
-    block = min(256, seq_len)
+    block = min(512, seq_len)
     return pl.pallas_call(
         functools.partial(attention_kernel, scale=scale),
         grid=(pairs, seq_len // block),

time: 686 us -> 690 us (level)
  Pallas kernels: 46.5 us -> 54.4 us
    pallas_call x2, Pallas kernels: 46.5 us -> 54.4 us  [attention(): pl.pallas_call(functools.partial(attention_kernel, scale=scale), grid=(pa...]
  transfers between devices with their start and end apart: 12 -> 12, of which waited for: 8 -> 8; matrix products, arithmetic and copies ran while one was open for 22% -> 22% of each run, Pallas kernels for 7% -> 8%
where the time goes in v12:
time: 690 us; the launch traced here: 682 us
  waiting for transfers between devices  264 us (38%)
  blocking collectives  129 us (19%)
  matrix products  112 us (16%)
  local copies, waits for them, and re-layouts  63.7 us (9%)
  Pallas kernels  54.4 us (8%)
  starting transfers between devices  29.7 us (4%)
  between operations  14.9 us (2%)
  other arithmetic  14.8 us (2%)
    all_to_all x1, blocking collectives, local(): lax.all_to_all(outgoing, 'expert', split_axis=0, concat_axis=0, tiled=True)  123 us
    all_to_all x2, waiting for transfers between devices, teach(): lax.all_to_all(grouped, 'expert', split_axis=1, concat_axis=2, tiled=True)  90.7 us
    all_to_all x2, waiting for transfers between devices, local(): lax.all_to_all(produced.astype(jnp.bfloat16), 'expert', split_axis=0, con...  73.2 us
    pallas_call x2, Pallas kernels, attention(): pl.pallas_call(functools.partial(attention_kernel, scale=scale), grid=(pa...  54.4 us
    all_gather x2, waiting for transfers between devices, local(): lax.all_gather(expert_down[j], 'rep', axis=0, tiled=True)  42.5 us
    all_gather x1, waiting for transfers between devices, local(): qkv_full = lax.all_gather(teacher_qkv, 'rep', axis=2, tiled=True)  36.7 us
    dot_general x8, matrix products, local(): jnp.einsum('scf,fd->scd', hidden[:, j, :, low:low + ff_part], down_w[low:...  27.2 us
    unnamed x2, matrix products  25.2 us
  transfers between devices with their start and end apart: 12, of which 8 were waited for; matrix products, arithmetic and copies ran while one was open for 22% of the time, Pallas kernels for 8%

profile of v12, /device:TPU:0, one launch (start us, length us, event | category | flops | bytes accessed | tf_op | source)
XLA Modules:
  0.0 682.4 jit_solution(9312764904859214041)
XLA Ops:
  9.0 1.8 fusion.98
  11.5 10.9 %copy.64 = bf16[2048,3,4,128]{0,3,2,1:T(8,128)(2,1)} copy(bf16[2048,3,4,128]{3,2,1,0:T(4,128)(2,1)} %param.21) | data formatting | bytes 12582912 | tf_op args[8]
  23.9 4.5 reduce-window.6
  29.5 2.8 reshape.350
  32.3 2.2 multiply_reduce_fusion
  34.7 5.4 convolution_convert_fusion
  40.2 123.1 %all_to_all.81 = bf16[8,160,2048]{2,1,0:T(8,128)(2,1)} all-to-all(bf16[8,160,2048]{2,1,0:T(8,128)(2,1)S(1)} %bitcast.343), channel_id=1, replica_groups=mesh['expert'=8,'rep'=4] {'expert'}, dimensions={0} | all-to-all | bytes 10485760 | tf_op jit(solution)/shard_map/all_to_all | solution.py:99
  163.3 14.8 %fusion = f32[2,8,80,1408]{3,2,1,0:T(8,128)} fusion(bf16[2,2048,1408]{1,2,0:T(8,128)(2,1)} %all-gather.11.cloned.1.call-done, bf16[8,2,80,2048]{3,2,1,0:T(8,128)(2,1)} %bitcast.339), kind=kOutput, calls=%fused_computation | convolution fusion | flops 7381975040 | bytes 23986176 | tf_op jit(solution)/shard_map/sjcd,jdf->sjcf/dot_general | solution.py:104
  178.0 16.9 %fusion.4 = bf16[8,2,80,1408]{3,2,0,1:T(8,128)(2,1)} fusion(f32[2,8,80,1408]{3,2,1,0:T(8,128)} %fusion, bf16[2,2048,1408]{1,2,0:T(8,128)(2,1)} %all-gather.9.cloned.1.call-done, bf16[8,2,80,2048]{3,2,1,0:T(8,128)(2,1)} %bitcast.340), kind=kOutput, calls=%fused_computation.6 | convolution fusion | flops 7392788480 | bytes 27590656 | tf_op jit(solution)/shard_map/sjcd,jdf->sjcf/dot_general | solution.py:101
  195.0 16.8 %all-gather.17.cloned.1.call-done = bf16[1,1408,2048]{2,1,0:T(8,128)(2,1)} async-done(((bf16[1,352,2048]{2,1,0:T(8,128)(2,1)}), bf16[1,1408,2048]{2,1,0:T(8,128)(2,1)}) %all-gather.17.cloned.1.call-update) | async-done | bytes 5767184 | tf_op jit(solution)/shard_map/all_gather | solution.py:79
  211.7 3.3 convolution_convert_fusion.5
  215.0 3.1 convolution_convert_fusion.6
  218.1 2.7 convolution_convert_fusion.7
  220.9 4.4 add_convert_fusion.1
  225.3 5.5 all-to-all-start.1
  230.8 25.8 %all-gather.19.cloned.1.call-done = bf16[1,1408,2048]{2,1,0:T(8,128)(2,1)} async-done(((bf16[1,352,2048]{2,1,0:T(8,128)(2,1)}), bf16[1,1408,2048]{2,1,0:T(8,128)(2,1)}) %all-gather.19.cloned.1.call-update) | async-done | bytes 5767184 | tf_op jit(solution)/shard_map/all_gather | solution.py:79
  256.6 3.3 convolution_convert_fusion.3
  259.9 3.1 convolution_convert_fusion.2
  263.0 2.7 convolution_convert_fusion.1
  265.7 4.5 add_convert_fusion
  270.2 20.4 %all-to-all-done.1 = bf16[8,80,2048]{2,1,0:T(8,128)(2,1)S(1)} async-done(((bf16[8,80,2048]{2,1,0:T(8,128)(2,1)}), bf16[8,80,2048]{2,1,0:T(8,128)(2,1)S(1)}, u32[]{:S(2)}, u32[]{:S(2)}) %all-to-all-start.1) | async-done | bytes 2621472 | tf_op jit(solution)/shard_map/all_to_all | solution.py:120
  290.7 4.4 all-to-all-start.2
  295.4 5.9 all_gather.26
  301.3 52.8 %all-to-all-done.2 = bf16[8,80,2048]{2,1,0:T(8,128)(2,1)} async-done(((bf16[8,80,2048]{2,1,0:T(8,128)(2,1)}), bf16[8,80,2048]{2,1,0:T(8,128)(2,1)}, u32[]{:S(2)}, u32[]{:S(2)}) %all-to-all-start.2) | async-done | bytes 2621472 | tf_op jit(solution)/shard_map/all_to_all | solution.py:120
  354.1 2.2 pad_maximum_fusion
  356.4 0.8 copy.59
  357.2 3.0 fusion.16
  360.3 4.2 fusion.12
  364.4 1.3 copy-done.3
  365.7 1.9 fusion.14
  367.6 3.2 reshape.331
  370.8 3.8 fusion.100
  374.6 1.6 copy.81
  376.2 36.7 %all-gather.13.cloned.1.call-done = bf16[2048,3,16,128]{0,3,2,1:T(8,128)(2,1)} async-done(((bf16[2048,3,4,128]{0,3,2,1:T(8,128)(2,1)}), bf16[2048,3,16,128]{0,3,2,1:T(8,128)(2,1)}) %all-gather.13.cloned.1.call-update) | async-done | bytes 25165840 | tf_op jit(solution)/shard_map/all_gather | solution.py:81
  412.9 12.5 %fusion.83 = f32[256,6144]{0,1:S(1)} fusion(bf16[2048,6144]{0,1:T(8,128)(2,1)} %bitcast.365, bf16[256,1,2048]{2,1,0:T(2,128)(2,1)S(1)} %copy-done.8), kind=kOutput, calls=%fused_computation.135 | convolution fusion | flops 6442450944 | bytes 32505856
  427.1 2.0 copy.68
  429.1 5.5 all-to-all-start.3
  435.2 12.7 %fusion.92 = f32[256,6144]{0,1:S(1)} fusion(bf16[2048,6144]{0,1:T(8,128)(2,1)} %bitcast.366, bf16[256,1,2048]{2,0,1:T(8,128)(2,1)} %copy.81), kind=kOutput, calls=%fused_computation.140 | convolution fusion | flops 6442450944 | bytes 32505856
  449.6 2.0 copy.73
  451.6 54.1 %all-to-all-done.3 = bf16[3,16,256,128]{2,3,0,1:T(8,128)(2,1)S(1)} async-done(((bf16[3,16,256,128]{2,3,0,1:T(8,128)(2,1)}), bf16[3,16,256,128]{2,3,0,1:T(8,128)(2,1)S(1)}, u32[]{:S(2)}, u32[]{:S(2)}) %all-to-all-start.3) | async-done | bytes 3145760 | tf_op jit(solution)/shard_map/all_to_all | solution.py:174
  505.7 4.5 all-to-all-start.5
  510.2 2.9 copy.69
  513.0 27.2 %shard_map.140 = bf16[2,2048,128]{2,1,0:T(8,128)(2,1)} custom-call(bf16[3,2,2048,128]{3,2,1,0:T(8,128)(2,1)} %bitcast.325, bf16[3,2,2048,128]{3,2,1,0:T(8,128)(2,1)} %bitcast.326, bf16[3,2,2048,128]{3,2,1,0:T(8,128)(2,1)} %bitcast.327), custom_call_target="tpu_custom_call" | custom-call | tf_op jit(solution)/shard_map/pallas_call | solution.py:38
  540.2 3.6 copy.70
  543.9 36.6 %all-to-all-done.5 = bf16[3,16,256,128]{2,3,0,1:T(8,128)(2,1)} async-done(((bf16[3,16,256,128]{2,3,0,1:T(8,128)(2,1)}), bf16[3,16,256,128]{2,3,0,1:T(8,128)(2,1)}, u32[]{:S(2)}, u32[]{:S(2)}) %all-to-all-start.5) | async-done | bytes 3145760 | tf_op jit(solution)/shard_map/all_to_all | solution.py:174
  580.5 3.6 all-to-all-start.4
  584.1 4.7 copy.74
  588.8 27.2 %shard_map.141 = bf16[2,2048,128]{2,1,0:T(8,128)(2,1)} custom-call(bf16[3,2,2048,128]{3,2,1,0:T(8,128)(2,1)} %bitcast.328, bf16[3,2,2048,128]{3,2,1,0:T(8,128)(2,1)} %bitcast.329, bf16[3,2,2048,128]{3,2,1,0:T(8,128)(2,1)} %bitcast.330), custom_call_target="tpu_custom_call" | custom-call | tf_op jit(solution)/shard_map/pallas_call | solution.py:38
  616.0 3.6 copy.75
  619.6 6.0 all-to-all-start.6
  625.6 3.2 reshape.330
  628.8 4.4 fusion.99
  633.4 17.9 %all-to-all-done.6 = bf16[2,2048,128]{2,0,1:T(2,128)(2,1)} async-done(((bf16[2,2048,128]{2,0,1:T(2,128)(2,1)}), bf16[2,2048,128]{2,0,1:T(2,128)(2,1)}, u32[]{:S(2)}, u32[]{:S(2)}) %all-to-all-start.6) | async-done | bytes 1048608 | tf_op jit(solution)/shard_map/all_to_all | solution.py:176
  651.3 1.4 copy.76
  652.7 2.5 fusion.45
  655.2 2.9 fusion.44
  659.7 1.2 fusion.40
  660.9 1.0 copy-done.15
  661.9 1.5 fusion.69
  666.5 1.2 fusion.30
  667.7 1.5 fusion.76
  669.4 0.9 convolution_bitcast_fusion.9
  670.3 0.9 convolution_bitcast_fusion.8
  671.2 3.5 copy.77
  (92 shorter events, 15.1 us)
Async XLA Ops:
  7.2 662.2 %copy-start = (f32[1024]{0:T(1024)S(1)}, f32[1024]{0:T(1024)}, u32[]{:S(2)}) copy-start(f32[1024]{0:T(1024)} %param.25) | copy-start | bytes 12292
  7.2 1.8 copy-start.7
  7.2 156.1 %all-gather.11.cloned.1.call-start = ((), (), s32[]{:S(2)}) async-start(), calls=%async_computation.8 | async-start | bytes 14417920 | tf_op jit(solution)/shard_map/all_gather | solution.py:77
  7.9 170.1 %all-gather.9.cloned.1.call-start = ((), (), s32[]{:S(2)}) async-start(), calls=%async_computation.7 | async-start | bytes 14417920 | tf_op jit(solution)/shard_map/all_gather | solution.py:76
  8.7 203.1 %all-gather.17.cloned.1.call-start = ((), (), s32[]{:S(2)}) async-start(), calls=%async_computation.11 | async-start | bytes 7208960 | tf_op jit(solution)/shard_map/all_gather | solution.py:79
  10.8 245.7 %all-gather.19.cloned.1.call-start = ((), (), s32[]{:S(2)}) async-start(), calls=%async_computation.12 | async-start | bytes 7208960 | tf_op jit(solution)/shard_map/all_gather | solution.py:79
  11.4 401.5 %all-gather.13.cloned.1.call-start = ((), (), s32[]{:S(2)}) async-start(), calls=%async_computation.9 | async-start | bytes 31457280 | tf_op jit(solution)/shard_map/all_gather | solution.py:81
  22.3 0.7 copy-start.9
  22.3 7.2 %copy-start.2 = (bf16[1,256,2,2048]{3,2,1,0:T(2,128)(2,1)S(1)}, bf16[1,256,2,2048]{3,2,1,0:T(2,128)(2,1)}, u32[]{:S(2)}) copy-start(bf16[1,256,2,2048]{3,2,1,0:T(2,128)(2,1)} %param.13) | copy-start | bytes 6291460
  29.5 5.2 copy-start.16
  211.7 6.4 copy-start.14
  225.3 65.4 %all-to-all-start.1 = ((bf16[8,80,2048]{2,1,0:T(8,128)(2,1)}), bf16[8,80,2048]{2,1,0:T(8,128)(2,1)S(1)}, u32[]{:S(2)}, u32[]{:S(2)}) async-start(bf16[8,80,2048]{2,1,0:T(8,128)(2,1)} %add_convert_fusion.1), calls=%async_computation.1 | async-start | bytes 5242880 | tf_op jit(solution)/shard_map/all_to_all | solution.py:120
  256.6 6.4 copy-start.13
  270.2 24.8 %copy-start.11 = (f32[1,256,2,2]{1,3,2,0:T(2,128)S(1)}, f32[1,256,2,2]{1,3,2,0:T(2,128)}, u32[]{:S(2)}) copy-start(f32[1,256,2,2]{1,3,2,0:T(2,128)} %param.15) | copy-start | bytes 12292
  270.2 25.2 %copy-start.12 = (f32[2,4,128]{2,1,0:T(4,128)S(1)}, f32[2,4,128]{2,1,0:T(4,128)}, u32[]{:S(2)}) copy-start(f32[2,4,128]{2,1,0:T(4,128)} %param.22) | copy-start | bytes 12292
  290.7 63.5 %all-to-all-start.2 = ((bf16[8,80,2048]{2,1,0:T(8,128)(2,1)}), bf16[8,80,2048]{2,1,0:T(8,128)(2,1)}, u32[]{:S(2)}, u32[]{:S(2)}) async-start(bf16[8,80,2048]{2,1,0:T(8,128)(2,1)} %add_convert_fusion), calls=%async_computation.2 | async-start | bytes 5242880 | tf_op jit(solution)/shard_map/all_to_all | solution.py:120
  357.2 3.0 copy-start.6
  360.2 5.5 copy-start.10
  364.4 1.3 copy-start.3
  374.6 38.3 %copy-start.8 = (bf16[256,1,2048]{2,1,0:T(2,128)(2,1)S(1)}, bf16[256,1,2048]{2,1,0:T(2,128)(2,1)}, u32[]{:S(2)}) copy-start(bf16[256,1,2048]{2,1,0:T(2,128)(2,1)} %get-tuple-element.24) | copy-start | bytes 3145732
  429.1 76.6 %all-to-all-start.3 = ((bf16[3,16,256,128]{2,3,0,1:T(8,128)(2,1)}), bf16[3,16,256,128]{2,3,0,1:T(8,128)(2,1)S(1)}, u32[]{:S(2)}, u32[]{:S(2)}) async-start(bf16[3,16,256,128]{2,3,0,1:T(8,128)(2,1)} %copy.68), calls=%async_computation.3 | async-start | bytes 6291456 | tf_op jit(solution)/shard_map/all_to_all | solution.py:174
  434.6 218.2 %all-gather.15.cloned.1.call-start = ((), (), s32[]{:S(2)}) async-start(), calls=%async_computation.10 | async-start | bytes 10485760 | tf_op jit(solution)/shard_map/all_gather | solution.py:83
  505.7 74.8 %all-to-all-start.5 = ((bf16[3,16,256,128]{2,3,0,1:T(8,128)(2,1)}), bf16[3,16,256,128]{2,3,0,1:T(8,128)(2,1)}, u32[]{:S(2)}, u32[]{:S(2)}) async-start(bf16[3,16,256,128]{2,3,0,1:T(8,128)(2,1)} %copy.73), calls=%async_computation.5 | async-start | bytes 6291456 | tf_op jit(solution)/shard_map/all_to_all | solution.py:174
  580.5 39.1 %all-to-all-start.4 = ((bf16[2,2048,128]{2,0,1:T(2,128)(2,1)}), bf16[2,2048,128]{2,0,1:T(2,128)(2,1)S(1)}, u32[]{:S(2)}, u32[]{:S(2)}) async-start(bf16[2,2048,128]{2,0,1:T(2,128)(2,1)} %copy.70), calls=%async_computation.4 | async-start | bytes 2097152 | tf_op jit(solution)/shard_map/all_to_all | solution.py:176
  619.6 31.6 %all-to-all-start.6 = ((bf16[2,2048,128]{2,0,1:T(2,128)(2,1)}), bf16[2,2048,128]{2,0,1:T(2,128)(2,1)}, u32[]{:S(2)}, u32[]{:S(2)}) async-start(bf16[2,2048,128]{2,0,1:T(2,128)(2,1)} %copy.75), calls=%async_computation.6 | async-start | bytes 2097152 | tf_op jit(solution)/shard_map/all_to_all | solution.py:176
  652.7 5.4 copy-start.1
  658.1 1.6 copy-start.5
  659.7 2.2 copy-start.15
  664.9 1.6 copy-start.4
Sparse Core Ops, SparseCore 0:
  9.6 78.8 all-gather.10
  90.0 76.1 all-gather.8
  168.3 43.3 all-gather.16
  213.1 43.3 all-gather.18
  258.0 154.8 all-gather.12
  436.6 58.7 all-gather.14

commit v13 on v12

--- a/solution.py
+++ b/solution.py
@@ -34,7 +34,7 @@
 
 def attention(whole, scale, interpret=False):
     _, pairs, seq_len, head_size = whole.shape
-    block = min(512, seq_len)
+    block = min(128, seq_len)
     return pl.pallas_call(
         functools.partial(attention_kernel, scale=scale),
         grid=(pairs, seq_len // block),

time: 690 us -> 695 us (level)
  Pallas kernels: 54.4 us -> 63.2 us
    pallas_call x2, Pallas kernels: 54.4 us -> 63.2 us  [attention(): pl.pallas_call(functools.partial(attention_kernel, scale=scale), grid=(pa...]
  transfers between devices with their start and end apart: 12 -> 12, of which waited for: 8 -> 8; matrix products, arithmetic and copies ran while one was open for 22% -> 22% of each run, Pallas kernels for 8% -> 9%
where the time goes in v13:
time: 695 us; the launch traced here: 687 us
  waiting for transfers between devices  259 us (37%)
  blocking collectives  129 us (19%)
  matrix products  112 us (16%)
  local copies, waits for them, and re-layouts  63.7 us (9%)
  Pallas kernels  63.2 us (9%)
  starting transfers between devices  29.7 us (4%)
  between operations  15.1 us (2%)
  other arithmetic  14.8 us (2%)
    all_to_all x1, blocking collectives, local(): lax.all_to_all(outgoing, 'expert', split_axis=0, concat_axis=0, tiled=True)  123 us
    all_to_all x2, waiting for transfers between devices, teach(): lax.all_to_all(grouped, 'expert', split_axis=1, concat_axis=2, tiled=True)  86.3 us
    all_to_all x2, waiting for transfers between devices, local(): lax.all_to_all(produced.astype(jnp.bfloat16), 'expert', split_axis=0, con...  73.6 us
    pallas_call x2, Pallas kernels, attention(): pl.pallas_call(functools.partial(attention_kernel, scale=scale), grid=(pa...  63.2 us
    all_gather x2, waiting for transfers between devices, local(): lax.all_gather(expert_down[j], 'rep', axis=0, tiled=True)  42.3 us
    all_gather x1, waiting for transfers between devices, local(): qkv_full = lax.all_gather(teacher_qkv, 'rep', axis=2, tiled=True)  36.7 us
    dot_general x8, matrix products, local(): jnp.einsum('scf,fd->scd', hidden[:, j, :, low:low + ff_part], down_w[low:...  27.2 us
    unnamed x2, matrix products  25.2 us
  transfers between devices with their start and end apart: 12, of which 8 were waited for; matrix products, arithmetic and copies ran while one was open for 22% of the time, Pallas kernels for 9%

profile of v13, /device:TPU:0, one launch (start us, length us, event | category | flops | bytes accessed | tf_op | source)
XLA Modules:
  0.0 686.9 jit_solution(17479205349454992464)
XLA Ops:
  9.0 1.8 fusion.98
  11.5 10.9 %copy.64 = bf16[2048,3,4,128]{0,3,2,1:T(8,128)(2,1)} copy(bf16[2048,3,4,128]{3,2,1,0:T(4,128)(2,1)} %param.21) | data formatting | bytes 12582912 | tf_op args[8]
  23.9 4.5 reduce-window.6
  29.5 2.8 reshape.350
  32.3 2.2 multiply_reduce_fusion
  34.7 5.4 convolution_convert_fusion
  40.2 123.1 %all_to_all.81 = bf16[8,160,2048]{2,1,0:T(8,128)(2,1)} all-to-all(bf16[8,160,2048]{2,1,0:T(8,128)(2,1)S(1)} %bitcast.343), channel_id=1, replica_groups=mesh['expert'=8,'rep'=4] {'expert'}, dimensions={0} | all-to-all | bytes 10485760 | tf_op jit(solution)/shard_map/all_to_all | solution.py:99
  163.3 14.8 %fusion = f32[2,8,80,1408]{3,2,1,0:T(8,128)} fusion(bf16[2,2048,1408]{1,2,0:T(8,128)(2,1)} %all-gather.11.cloned.1.call-done, bf16[8,2,80,2048]{3,2,1,0:T(8,128)(2,1)} %bitcast.339), kind=kOutput, calls=%fused_computation | convolution fusion | flops 7381975040 | bytes 23986176 | tf_op jit(solution)/shard_map/sjcd,jdf->sjcf/dot_general | solution.py:104
  178.1 17.1 %fusion.4 = bf16[8,2,80,1408]{3,2,0,1:T(8,128)(2,1)} fusion(f32[2,8,80,1408]{3,2,1,0:T(8,128)} %fusion, bf16[2,2048,1408]{1,2,0:T(8,128)(2,1)} %all-gather.9.cloned.1.call-done, bf16[8,2,80,2048]{3,2,1,0:T(8,128)(2,1)} %bitcast.340), kind=kOutput, calls=%fused_computation.6 | convolution fusion | flops 7392788480 | bytes 27590656 | tf_op jit(solution)/shard_map/sjcd,jdf->sjcf/dot_general | solution.py:101
  195.2 16.5 %all-gather.17.cloned.1.call-done = bf16[1,1408,2048]{2,1,0:T(8,128)(2,1)} async-done(((bf16[1,352,2048]{2,1,0:T(8,128)(2,1)}), bf16[1,1408,2048]{2,1,0:T(8,128)(2,1)}) %all-gather.17.cloned.1.call-update) | async-done | bytes 5767184 | tf_op jit(solution)/shard_map/all_gather | solution.py:79
  211.7 3.2 convolution_convert_fusion.5
  215.0 3.1 convolution_convert_fusion.6
  218.1 2.7 convolution_convert_fusion.7
  220.8 4.4 add_convert_fusion.1
  225.3 5.5 all-to-all-start.1
  230.8 25.8 %all-gather.19.cloned.1.call-done = bf16[1,1408,2048]{2,1,0:T(8,128)(2,1)} async-done(((bf16[1,352,2048]{2,1,0:T(8,128)(2,1)}), bf16[1,1408,2048]{2,1,0:T(8,128)(2,1)}) %all-gather.19.cloned.1.call-update) | async-done | bytes 5767184 | tf_op jit(solution)/shard_map/all_gather | solution.py:79
  256.6 3.3 convolution_convert_fusion.3
  259.8 3.1 convolution_convert_fusion.2
  263.0 2.7 convolution_convert_fusion.1
  265.7 4.5 add_convert_fusion
  270.2 20.5 %all-to-all-done.1 = bf16[8,80,2048]{2,1,0:T(8,128)(2,1)S(1)} async-done(((bf16[8,80,2048]{2,1,0:T(8,128)(2,1)}), bf16[8,80,2048]{2,1,0:T(8,128)(2,1)S(1)}, u32[]{:S(2)}, u32[]{:S(2)}) %all-to-all-start.1) | async-done | bytes 2621472 | tf_op jit(solution)/shard_map/all_to_all | solution.py:120
  290.7 4.4 all-to-all-start.2
  295.5 5.6 all_gather.26
  301.1 53.1 %all-to-all-done.2 = bf16[8,80,2048]{2,1,0:T(8,128)(2,1)} async-done(((bf16[8,80,2048]{2,1,0:T(8,128)(2,1)}), bf16[8,80,2048]{2,1,0:T(8,128)(2,1)}, u32[]{:S(2)}, u32[]{:S(2)}) %all-to-all-start.2) | async-done | bytes 2621472 | tf_op jit(solution)/shard_map/all_to_all | solution.py:120
  354.2 2.2 pad_maximum_fusion
  356.4 0.8 copy.59
  357.3 3.0 fusion.16
  360.3 4.2 fusion.12
  364.5 1.3 copy-done.3
  365.8 1.9 fusion.14
  367.6 3.2 reshape.331
  370.8 3.8 fusion.100
  374.6 1.6 copy.81
  376.2 36.7 %all-gather.13.cloned.1.call-done = bf16[2048,3,16,128]{0,3,2,1:T(8,128)(2,1)} async-done(((bf16[2048,3,4,128]{0,3,2,1:T(8,128)(2,1)}), bf16[2048,3,16,128]{0,3,2,1:T(8,128)(2,1)}) %all-gather.13.cloned.1.call-update) | async-done | bytes 25165840 | tf_op jit(solution)/shard_map/all_gather | solution.py:81
  412.9 12.5 %fusion.83 = f32[256,6144]{0,1:S(1)} fusion(bf16[2048,6144]{0,1:T(8,128)(2,1)} %bitcast.365, bf16[256,1,2048]{2,1,0:T(2,128)(2,1)S(1)} %copy-done.8), kind=kOutput, calls=%fused_computation.135 | convolution fusion | flops 6442450944 | bytes 32505856
  427.1 2.0 copy.68
  429.1 5.5 all-to-all-start.3
  435.2 12.8 %fusion.92 = f32[256,6144]{0,1:S(1)} fusion(bf16[2048,6144]{0,1:T(8,128)(2,1)} %bitcast.366, bf16[256,1,2048]{2,0,1:T(8,128)(2,1)} %copy.81), kind=kOutput, calls=%fused_computation.140 | convolution fusion | flops 6442450944 | bytes 32505856
  449.6 2.0 copy.73
  451.6 54.1 %all-to-all-done.3 = bf16[3,16,256,128]{2,3,0,1:T(8,128)(2,1)S(1)} async-done(((bf16[3,16,256,128]{2,3,0,1:T(8,128)(2,1)}), bf16[3,16,256,128]{2,3,0,1:T(8,128)(2,1)S(1)}, u32[]{:S(2)}, u32[]{:S(2)}) %all-to-all-start.3) | async-done | bytes 3145760 | tf_op jit(solution)/shard_map/all_to_all | solution.py:174
  505.7 4.5 all-to-all-start.5
  510.2 2.9 copy.69
  513.0 31.6 %shard_map.140 = bf16[2,2048,128]{2,1,0:T(8,128)(2,1)} custom-call(bf16[3,2,2048,128]{3,2,1,0:T(8,128)(2,1)} %bitcast.325, bf16[3,2,2048,128]{3,2,1,0:T(8,128)(2,1)} %bitcast.326, bf16[3,2,2048,128]{3,2,1,0:T(8,128)(2,1)} %bitcast.327), custom_call_target="tpu_custom_call" | custom-call | tf_op jit(solution)/shard_map/pallas_call | solution.py:38
  544.6 3.6 copy.70
  548.2 32.2 %all-to-all-done.5 = bf16[3,16,256,128]{2,3,0,1:T(8,128)(2,1)} async-done(((bf16[3,16,256,128]{2,3,0,1:T(8,128)(2,1)}), bf16[3,16,256,128]{2,3,0,1:T(8,128)(2,1)}, u32[]{:S(2)}, u32[]{:S(2)}) %all-to-all-start.5) | async-done | bytes 3145760 | tf_op jit(solution)/shard_map/all_to_all | solution.py:174
  580.5 3.6 all-to-all-start.4
  584.1 4.7 copy.74
  588.8 31.6 %shard_map.141 = bf16[2,2048,128]{2,1,0:T(8,128)(2,1)} custom-call(bf16[3,2,2048,128]{3,2,1,0:T(8,128)(2,1)} %bitcast.328, bf16[3,2,2048,128]{3,2,1,0:T(8,128)(2,1)} %bitcast.329, bf16[3,2,2048,128]{3,2,1,0:T(8,128)(2,1)} %bitcast.330), custom_call_target="tpu_custom_call" | custom-call | tf_op jit(solution)/shard_map/pallas_call | solution.py:38
  620.3 3.6 copy.75
  624.0 6.0 all-to-all-start.6
  630.0 3.2 reshape.330
  633.2 4.4 fusion.99
  637.8 17.8 %all-to-all-done.6 = bf16[2,2048,128]{2,0,1:T(2,128)(2,1)} async-done(((bf16[2,2048,128]{2,0,1:T(2,128)(2,1)}), bf16[2,2048,128]{2,0,1:T(2,128)(2,1)}, u32[]{:S(2)}, u32[]{:S(2)}) %all-to-all-start.6) | async-done | bytes 1048608 | tf_op jit(solution)/shard_map/all_to_all | solution.py:176
  655.6 1.4 copy.76
  657.1 2.5 fusion.45
  659.6 2.9 fusion.44
  664.1 1.2 fusion.40
  665.2 1.0 copy-done.15
  666.3 1.5 fusion.69
  670.8 1.2 fusion.30
  672.0 1.5 fusion.76
  673.7 0.9 convolution_bitcast_fusion.9
  674.6 0.9 convolution_bitcast_fusion.8
  675.5 3.5 copy.77
  (92 shorter events, 15.1 us)
Async XLA Ops:
  7.2 666.5 %copy-start = (f32[1024]{0:T(1024)S(1)}, f32[1024]{0:T(1024)}, u32[]{:S(2)}) copy-start(f32[1024]{0:T(1024)} %param.25) | copy-start | bytes 12292
  7.2 1.8 copy-start.7
  7.2 156.1 %all-gather.11.cloned.1.call-start = ((), (), s32[]{:S(2)}) async-start(), calls=%async_computation.8 | async-start | bytes 14417920 | tf_op jit(solution)/shard_map/all_gather | solution.py:77
  7.9 170.1 %all-gather.9.cloned.1.call-start = ((), (), s32[]{:S(2)}) async-start(), calls=%async_computation.7 | async-start | bytes 14417920 | tf_op jit(solution)/shard_map/all_gather | solution.py:76
  8.7 203.1 %all-gather.17.cloned.1.call-start = ((), (), s32[]{:S(2)}) async-start(), calls=%async_computation.11 | async-start | bytes 7208960 | tf_op jit(solution)/shard_map/all_gather | solution.py:79
  10.8 245.7 %all-gather.19.cloned.1.call-start = ((), (), s32[]{:S(2)}) async-start(), calls=%async_computation.12 | async-start | bytes 7208960 | tf_op jit(solution)/shard_map/all_gather | solution.py:79
  11.4 401.5 %all-gather.13.cloned.1.call-start = ((), (), s32[]{:S(2)}) async-start(), calls=%async_computation.9 | async-start | bytes 31457280 | tf_op jit(solution)/shard_map/all_gather | solution.py:81
  22.3 0.7 copy-start.9
  22.3 7.2 %copy-start.2 = (bf16[1,256,2,2048]{3,2,1,0:T(2,128)(2,1)S(1)}, bf16[1,256,2,2048]{3,2,1,0:T(2,128)(2,1)}, u32[]{:S(2)}) copy-start(bf16[1,256,2,2048]{3,2,1,0:T(2,128)(2,1)} %param.13) | copy-start | bytes 6291460
  29.5 5.2 copy-start.16
  211.7 6.4 copy-start.14
  225.3 65.4 %all-to-all-start.1 = ((bf16[8,80,2048]{2,1,0:T(8,128)(2,1)}), bf16[8,80,2048]{2,1,0:T(8,128)(2,1)S(1)}, u32[]{:S(2)}, u32[]{:S(2)}) async-start(bf16[8,80,2048]{2,1,0:T(8,128)(2,1)} %add_convert_fusion.1), calls=%async_computation.1 | async-start | bytes 5242880 | tf_op jit(solution)/shard_map/all_to_all | solution.py:120
  256.6 6.4 copy-start.13
  270.2 24.9 %copy-start.11 = (f32[1,256,2,2]{1,3,2,0:T(2,128)S(1)}, f32[1,256,2,2]{1,3,2,0:T(2,128)}, u32[]{:S(2)}) copy-start(f32[1,256,2,2]{1,3,2,0:T(2,128)} %param.15) | copy-start | bytes 12292
  270.2 25.2 %copy-start.12 = (f32[2,4,128]{2,1,0:T(4,128)S(1)}, f32[2,4,128]{2,1,0:T(4,128)}, u32[]{:S(2)}) copy-start(f32[2,4,128]{2,1,0:T(4,128)} %param.22) | copy-start | bytes 12292
  290.7 63.5 %all-to-all-start.2 = ((bf16[8,80,2048]{2,1,0:T(8,128)(2,1)}), bf16[8,80,2048]{2,1,0:T(8,128)(2,1)}, u32[]{:S(2)}, u32[]{:S(2)}) async-start(bf16[8,80,2048]{2,1,0:T(8,128)(2,1)} %add_convert_fusion), calls=%async_computation.2 | async-start | bytes 5242880 | tf_op jit(solution)/shard_map/all_to_all | solution.py:120
  357.2 3.0 copy-start.6
  360.3 5.5 copy-start.10
  364.4 1.3 copy-start.3
  374.6 38.3 %copy-start.8 = (bf16[256,1,2048]{2,1,0:T(2,128)(2,1)S(1)}, bf16[256,1,2048]{2,1,0:T(2,128)(2,1)}, u32[]{:S(2)}) copy-start(bf16[256,1,2048]{2,1,0:T(2,128)(2,1)} %get-tuple-element.24) | copy-start | bytes 3145732
  429.1 76.6 %all-to-all-start.3 = ((bf16[3,16,256,128]{2,3,0,1:T(8,128)(2,1)}), bf16[3,16,256,128]{2,3,0,1:T(8,128)(2,1)S(1)}, u32[]{:S(2)}, u32[]{:S(2)}) async-start(bf16[3,16,256,128]{2,3,0,1:T(8,128)(2,1)} %copy.68), calls=%async_computation.3 | async-start | bytes 6291456 | tf_op jit(solution)/shard_map/all_to_all | solution.py:174
  434.6 222.5 %all-gather.15.cloned.1.call-start = ((), (), s32[]{:S(2)}) async-start(), calls=%async_computation.10 | async-start | bytes 10485760 | tf_op jit(solution)/shard_map/all_gather | solution.py:83
  505.7 74.8 %all-to-all-start.5 = ((bf16[3,16,256,128]{2,3,0,1:T(8,128)(2,1)}), bf16[3,16,256,128]{2,3,0,1:T(8,128)(2,1)}, u32[]{:S(2)}, u32[]{:S(2)}) async-start(bf16[3,16,256,128]{2,3,0,1:T(8,128)(2,1)} %copy.73), calls=%async_computation.5 | async-start | bytes 6291456 | tf_op jit(solution)/shard_map/all_to_all | solution.py:174
  580.5 43.5 %all-to-all-start.4 = ((bf16[2,2048,128]{2,0,1:T(2,128)(2,1)}), bf16[2,2048,128]{2,0,1:T(2,128)(2,1)S(1)}, u32[]{:S(2)}, u32[]{:S(2)}) async-start(bf16[2,2048,128]{2,0,1:T(2,128)(2,1)} %copy.70), calls=%async_computation.4 | async-start | bytes 2097152 | tf_op jit(solution)/shard_map/all_to_all | solution.py:176
  624.0 31.6 %all-to-all-start.6 = ((bf16[2,2048,128]{2,0,1:T(2,128)(2,1)}), bf16[2,2048,128]{2,0,1:T(2,128)(2,1)}, u32[]{:S(2)}, u32[]{:S(2)}) async-start(bf16[2,2048,128]{2,0,1:T(2,128)(2,1)} %copy.75), calls=%async_computation.6 | async-start | bytes 2097152 | tf_op jit(solution)/shard_map/all_to_all | solution.py:176
  657.1 5.4 copy-start.1
  662.5 1.6 copy-start.5
  664.1 2.2 copy-start.15
  669.2 1.6 copy-start.4
Sparse Core Ops, SparseCore 0:
  9.6 78.8 all-gather.10
  90.0 76.1 all-gather.8
  168.3 43.3 all-gather.16
  213.1 43.3 all-gather.18
  258.0 154.8 all-gather.12
  436.6 58.7 all-gather.14

commit v14 on v10

--- a/solution.py
+++ b/solution.py
@@ -26,7 +26,8 @@
     ) * scale
     scores = scores - jnp.max(scores, axis=-1, keepdims=True)
     weights = jnp.exp(scores)
-    probs = (weights / jnp.sum(weights, axis=-1, keepdims=True)).astype(jnp.bfloat16)
+    inverse = 1.0 / jnp.sum(weights, axis=-1, keepdims=True)
+    probs = (weights * inverse).astype(jnp.bfloat16)
     out_ref[...] = jnp.dot(probs, value_ref[...], preferred_element_type=jnp.float32).astype(
         out_ref.dtype
     )

time: 686 us -> 686 us (level)
  no operation moved by 1% of the time
where the time goes in v14:
time: 686 us; the launch traced here: 678 us
  waiting for transfers between devices  267 us (39%)
  blocking collectives  129 us (19%)
  matrix products  112 us (16%)
  local copies, waits for them, and re-layouts  63.7 us (9%)
  Pallas kernels  46.5 us (7%)
  starting transfers between devices  29.7 us (4%)
  between operations  14.9 us (2%)
  other arithmetic  14.8 us (2%)
    all_to_all x1, blocking collectives, local(): lax.all_to_all(outgoing, 'expert', split_axis=0, concat_axis=0, tiled=True)  123 us
    all_to_all x2, waiting for transfers between devices, teach(): lax.all_to_all(grouped, 'expert', split_axis=1, concat_axis=2, tiled=True)  94.3 us
    all_to_all x2, waiting for transfers between devices, local(): lax.all_to_all(produced.astype(jnp.bfloat16), 'expert', split_axis=0, con...  73.5 us
    pallas_call x2, Pallas kernels, attention(): pl.pallas_call(functools.partial(attention_kernel, scale=scale), grid=(pa...  46.5 us
    all_gather x2, waiting for transfers between devices, local(): lax.all_gather(expert_down[j], 'rep', axis=0, tiled=True)  42.4 us
    all_gather x1, waiting for transfers between devices, local(): qkv_full = lax.all_gather(teacher_qkv, 'rep', axis=2, tiled=True)  36.7 us
    dot_general x8, matrix products, local(): jnp.einsum('scf,fd->scd', hidden[:, j, :, low:low + ff_part], down_w[low:...  27.2 us
    unnamed x2, matrix products  25.6 us
  transfers between devices with their start and end apart: 12, of which 8 were waited for; matrix products, arithmetic and copies ran while one was open for 22% of the time, Pallas kernels for 7%

profile of v14, /device:TPU:0, one launch (start us, length us, event | category | flops | bytes accessed | tf_op | source)
XLA Modules:
  0.0 678.3 jit_solution(2944934210767052312)
XLA Ops:
  9.0 1.8 fusion.98
  11.5 10.9 %copy.64 = bf16[2048,3,4,128]{0,3,2,1:T(8,128)(2,1)} copy(bf16[2048,3,4,128]{3,2,1,0:T(4,128)(2,1)} %param.21) | data formatting | bytes 12582912 | tf_op args[8]
  23.9 4.5 reduce-window.6
  29.5 2.8 reshape.350
  32.3 2.2 multiply_reduce_fusion
  34.7 5.4 convolution_convert_fusion
  40.2 123.4 %all_to_all.81 = bf16[8,160,2048]{2,1,0:T(8,128)(2,1)} all-to-all(bf16[8,160,2048]{2,1,0:T(8,128)(2,1)S(1)} %bitcast.343), channel_id=1, replica_groups=mesh['expert'=8,'rep'=4] {'expert'}, dimensions={0} | all-to-all | bytes 10485760 | tf_op jit(solution)/shard_map/all_to_all | solution.py:100
  163.5 14.8 %fusion = f32[2,8,80,1408]{3,2,1,0:T(8,128)} fusion(bf16[2,2048,1408]{1,2,0:T(8,128)(2,1)} %all-gather.11.cloned.1.call-done, bf16[8,2,80,2048]{3,2,1,0:T(8,128)(2,1)} %bitcast.339), kind=kOutput, calls=%fused_computation | convolution fusion | flops 7381975040 | bytes 23986176 | tf_op jit(solution)/shard_map/sjcd,jdf->sjcf/dot_general | solution.py:105
  178.3 16.8 %fusion.4 = bf16[8,2,80,1408]{3,2,0,1:T(8,128)(2,1)} fusion(f32[2,8,80,1408]{3,2,1,0:T(8,128)} %fusion, bf16[2,2048,1408]{1,2,0:T(8,128)(2,1)} %all-gather.9.cloned.1.call-done, bf16[8,2,80,2048]{3,2,1,0:T(8,128)(2,1)} %bitcast.340), kind=kOutput, calls=%fused_computation.6 | convolution fusion | flops 7392788480 | bytes 27590656 | tf_op jit(solution)/shard_map/sjcd,jdf->sjcf/dot_general | solution.py:102
  195.1 16.6 %all-gather.17.cloned.1.call-done = bf16[1,1408,2048]{2,1,0:T(8,128)(2,1)} async-done(((bf16[1,352,2048]{2,1,0:T(8,128)(2,1)}), bf16[1,1408,2048]{2,1,0:T(8,128)(2,1)}) %all-gather.17.cloned.1.call-update) | async-done | bytes 5767184 | tf_op jit(solution)/shard_map/all_gather | solution.py:80
  211.7 3.2 convolution_convert_fusion.5
  215.0 3.1 convolution_convert_fusion.6
  218.1 2.7 convolution_convert_fusion.7
  220.8 4.4 add_convert_fusion.1
  225.3 5.5 all-to-all-start.1
  230.8 25.8 %all-gather.19.cloned.1.call-done = bf16[1,1408,2048]{2,1,0:T(8,128)(2,1)} async-done(((bf16[1,352,2048]{2,1,0:T(8,128)(2,1)}), bf16[1,1408,2048]{2,1,0:T(8,128)(2,1)}) %all-gather.19.cloned.1.call-update) | async-done | bytes 5767184 | tf_op jit(solution)/shard_map/all_gather | solution.py:80
  256.6 3.3 convolution_convert_fusion.3
  259.8 3.1 convolution_convert_fusion.2
  263.0 2.7 convolution_convert_fusion.1
  265.7 4.5 add_convert_fusion
  270.2 20.5 %all-to-all-done.1 = bf16[8,80,2048]{2,1,0:T(8,128)(2,1)S(1)} async-done(((bf16[8,80,2048]{2,1,0:T(8,128)(2,1)}), bf16[8,80,2048]{2,1,0:T(8,128)(2,1)S(1)}, u32[]{:S(2)}, u32[]{:S(2)}) %all-to-all-start.1) | async-done | bytes 2621472 | tf_op jit(solution)/shard_map/all_to_all | solution.py:121
  290.7 4.4 all-to-all-start.2
  295.5 5.6 all_gather.26
  301.1 53.1 %all-to-all-done.2 = bf16[8,80,2048]{2,1,0:T(8,128)(2,1)} async-done(((bf16[8,80,2048]{2,1,0:T(8,128)(2,1)}), bf16[8,80,2048]{2,1,0:T(8,128)(2,1)}, u32[]{:S(2)}, u32[]{:S(2)}) %all-to-all-start.2) | async-done | bytes 2621472 | tf_op jit(solution)/shard_map/all_to_all | solution.py:121
  354.2 2.2 pad_maximum_fusion
  356.4 0.8 copy.59
  357.2 3.0 fusion.16
  360.3 4.2 fusion.12
  364.5 1.3 copy-done.3
  365.7 1.9 fusion.14
  367.6 3.2 reshape.331
  370.8 3.8 fusion.100
  374.6 1.6 copy.81
  376.2 36.7 %all-gather.13.cloned.1.call-done = bf16[2048,3,16,128]{0,3,2,1:T(8,128)(2,1)} async-done(((bf16[2048,3,4,128]{0,3,2,1:T(8,128)(2,1)}), bf16[2048,3,16,128]{0,3,2,1:T(8,128)(2,1)}) %all-gather.13.cloned.1.call-update) | async-done | bytes 25165840 | tf_op jit(solution)/shard_map/all_gather | solution.py:82
  412.9 12.5 %fusion.83 = f32[256,6144]{0,1:S(1)} fusion(bf16[2048,6144]{0,1:T(8,128)(2,1)} %bitcast.365, bf16[256,1,2048]{2,1,0:T(2,128)(2,1)S(1)} %copy-done.8), kind=kOutput, calls=%fused_computation.135 | convolution fusion | flops 6442450944 | bytes 32505856
  427.1 2.0 copy.68
  429.1 5.5 all-to-all-start.3
  435.2 13.1 %fusion.92 = f32[256,6144]{0,1:S(1)} fusion(bf16[2048,6144]{0,1:T(8,128)(2,1)} %bitcast.366, bf16[256,1,2048]{2,0,1:T(8,128)(2,1)} %copy.81), kind=kOutput, calls=%fused_computation.140 | convolution fusion | flops 6442450944 | bytes 32505856
  450.0 2.0 copy.73
  452.0 53.7 %all-to-all-done.3 = bf16[3,16,256,128]{2,3,0,1:T(8,128)(2,1)S(1)} async-done(((bf16[3,16,256,128]{2,3,0,1:T(8,128)(2,1)}), bf16[3,16,256,128]{2,3,0,1:T(8,128)(2,1)S(1)}, u32[]{:S(2)}, u32[]{:S(2)}) %all-to-all-start.3) | async-done | bytes 3145760 | tf_op jit(solution)/shard_map/all_to_all | solution.py:175
  505.7 4.5 all-to-all-start.5
  510.2 2.9 copy.69
  513.0 23.2 %shard_map.140 = bf16[2,2048,128]{2,1,0:T(8,128)(2,1)} custom-call(bf16[3,2,2048,128]{3,2,1,0:T(8,128)(2,1)} %bitcast.325, bf16[3,2,2048,128]{3,2,1,0:T(8,128)(2,1)} %bitcast.326, bf16[3,2,2048,128]{3,2,1,0:T(8,128)(2,1)} %bitcast.327), custom_call_target="tpu_custom_call" | custom-call | tf_op jit(solution)/shard_map/pallas_call | solution.py:39
  536.3 3.6 copy.70
  539.9 40.6 %all-to-all-done.5 = bf16[3,16,256,128]{2,3,0,1:T(8,128)(2,1)} async-done(((bf16[3,16,256,128]{2,3,0,1:T(8,128)(2,1)}), bf16[3,16,256,128]{2,3,0,1:T(8,128)(2,1)}, u32[]{:S(2)}, u32[]{:S(2)}) %all-to-all-start.5) | async-done | bytes 3145760 | tf_op jit(solution)/shard_map/all_to_all | solution.py:175
  580.5 3.6 all-to-all-start.4
  584.1 4.7 copy.74
  588.8 23.2 %shard_map.141 = bf16[2,2048,128]{2,1,0:T(8,128)(2,1)} custom-call(bf16[3,2,2048,128]{3,2,1,0:T(8,128)(2,1)} %bitcast.328, bf16[3,2,2048,128]{3,2,1,0:T(8,128)(2,1)} %bitcast.329, bf16[3,2,2048,128]{3,2,1,0:T(8,128)(2,1)} %bitcast.330), custom_call_target="tpu_custom_call" | custom-call | tf_op jit(solution)/shard_map/pallas_call | solution.py:39
  612.0 3.6 copy.75
  615.6 6.0 all-to-all-start.6
  621.6 3.2 reshape.330
  624.8 4.3 fusion.99
  629.4 17.9 %all-to-all-done.6 = bf16[2,2048,128]{2,0,1:T(2,128)(2,1)} async-done(((bf16[2,2048,128]{2,0,1:T(2,128)(2,1)}), bf16[2,2048,128]{2,0,1:T(2,128)(2,1)}, u32[]{:S(2)}, u32[]{:S(2)}) %all-to-all-start.6) | async-done | bytes 1048608 | tf_op jit(solution)/shard_map/all_to_all | solution.py:177
  647.3 1.4 copy.76
  648.8 2.5 fusion.45
  651.3 2.9 fusion.44
  655.7 1.2 fusion.40
  656.9 1.0 copy-done.15
  657.9 1.5 fusion.69
  662.5 1.2 fusion.30
  663.7 1.5 fusion.76
  665.4 0.9 convolution_bitcast_fusion.9
  666.3 0.9 convolution_bitcast_fusion.8
  667.2 3.5 copy.77
  (92 shorter events, 15.1 us)
Async XLA Ops:
  7.2 658.2 %copy-start = (f32[1024]{0:T(1024)S(1)}, f32[1024]{0:T(1024)}, u32[]{:S(2)}) copy-start(f32[1024]{0:T(1024)} %param.25) | copy-start | bytes 12292
  7.2 1.8 copy-start.7
  7.2 156.4 %all-gather.11.cloned.1.call-start = ((), (), s32[]{:S(2)}) async-start(), calls=%async_computation.8 | async-start | bytes 14417920 | tf_op jit(solution)/shard_map/all_gather | solution.py:78
  7.9 170.4 %all-gather.9.cloned.1.call-start = ((), (), s32[]{:S(2)}) async-start(), calls=%async_computation.7 | async-start | bytes 14417920 | tf_op jit(solution)/shard_map/all_gather | solution.py:77
  8.7 203.1 %all-gather.17.cloned.1.call-start = ((), (), s32[]{:S(2)}) async-start(), calls=%async_computation.11 | async-start | bytes 7208960 | tf_op jit(solution)/shard_map/all_gather | solution.py:80
  10.8 245.7 %all-gather.19.cloned.1.call-start = ((), (), s32[]{:S(2)}) async-start(), calls=%async_computation.12 | async-start | bytes 7208960 | tf_op jit(solution)/shard_map/all_gather | solution.py:80
  11.4 401.5 %all-gather.13.cloned.1.call-start = ((), (), s32[]{:S(2)}) async-start(), calls=%async_computation.9 | async-start | bytes 31457280 | tf_op jit(solution)/shard_map/all_gather | solution.py:82
  22.3 0.7 copy-start.9
  22.3 7.2 %copy-start.2 = (bf16[1,256,2,2048]{3,2,1,0:T(2,128)(2,1)S(1)}, bf16[1,256,2,2048]{3,2,1,0:T(2,128)(2,1)}, u32[]{:S(2)}) copy-start(bf16[1,256,2,2048]{3,2,1,0:T(2,128)(2,1)} %param.13) | copy-start | bytes 6291460
  29.5 5.2 copy-start.16
  211.7 6.4 copy-start.14
  225.3 65.4 %all-to-all-start.1 = ((bf16[8,80,2048]{2,1,0:T(8,128)(2,1)}), bf16[8,80,2048]{2,1,0:T(8,128)(2,1)S(1)}, u32[]{:S(2)}, u32[]{:S(2)}) async-start(bf16[8,80,2048]{2,1,0:T(8,128)(2,1)} %add_convert_fusion.1), calls=%async_computation.1 | async-start | bytes 5242880 | tf_op jit(solution)/shard_map/all_to_all | solution.py:121
  256.6 6.4 copy-start.13
  270.2 24.9 %copy-start.11 = (f32[1,256,2,2]{1,3,2,0:T(2,128)S(1)}, f32[1,256,2,2]{1,3,2,0:T(2,128)}, u32[]{:S(2)}) copy-start(f32[1,256,2,2]{1,3,2,0:T(2,128)} %param.15) | copy-start | bytes 12292
  270.2 25.2 %copy-start.12 = (f32[2,4,128]{2,1,0:T(4,128)S(1)}, f32[2,4,128]{2,1,0:T(4,128)}, u32[]{:S(2)}) copy-start(f32[2,4,128]{2,1,0:T(4,128)} %param.22) | copy-start | bytes 12292
  290.7 63.5 %all-to-all-start.2 = ((bf16[8,80,2048]{2,1,0:T(8,128)(2,1)}), bf16[8,80,2048]{2,1,0:T(8,128)(2,1)}, u32[]{:S(2)}, u32[]{:S(2)}) async-start(bf16[8,80,2048]{2,1,0:T(8,128)(2,1)} %add_convert_fusion), calls=%async_computation.2 | async-start | bytes 5242880 | tf_op jit(solution)/shard_map/all_to_all | solution.py:121
  357.2 3.0 copy-start.6
  360.3 5.5 copy-start.10
  364.4 1.3 copy-start.3
  374.6 38.3 %copy-start.8 = (bf16[256,1,2048]{2,1,0:T(2,128)(2,1)S(1)}, bf16[256,1,2048]{2,1,0:T(2,128)(2,1)}, u32[]{:S(2)}) copy-start(bf16[256,1,2048]{2,1,0:T(2,128)(2,1)} %get-tuple-element.24) | copy-start | bytes 3145732
  429.1 76.6 %all-to-all-start.3 = ((bf16[3,16,256,128]{2,3,0,1:T(8,128)(2,1)}), bf16[3,16,256,128]{2,3,0,1:T(8,128)(2,1)S(1)}, u32[]{:S(2)}, u32[]{:S(2)}) async-start(bf16[3,16,256,128]{2,3,0,1:T(8,128)(2,1)} %copy.68), calls=%async_computation.3 | async-start | bytes 6291456 | tf_op jit(solution)/shard_map/all_to_all | solution.py:175
  434.6 214.2 %all-gather.15.cloned.1.call-start = ((), (), s32[]{:S(2)}) async-start(), calls=%async_computation.10 | async-start | bytes 10485760 | tf_op jit(solution)/shard_map/all_gather | solution.py:84
  505.7 74.8 %all-to-all-start.5 = ((bf16[3,16,256,128]{2,3,0,1:T(8,128)(2,1)}), bf16[3,16,256,128]{2,3,0,1:T(8,128)(2,1)}, u32[]{:S(2)}, u32[]{:S(2)}) async-start(bf16[3,16,256,128]{2,3,0,1:T(8,128)(2,1)} %copy.73), calls=%async_computation.5 | async-start | bytes 6291456 | tf_op jit(solution)/shard_map/all_to_all | solution.py:175
  580.5 35.2 %all-to-all-start.4 = ((bf16[2,2048,128]{2,0,1:T(2,128)(2,1)}), bf16[2,2048,128]{2,0,1:T(2,128)(2,1)S(1)}, u32[]{:S(2)}, u32[]{:S(2)}) async-start(bf16[2,2048,128]{2,0,1:T(2,128)(2,1)} %copy.70), calls=%async_computation.4 | async-start | bytes 2097152 | tf_op jit(solution)/shard_map/all_to_all | solution.py:177
  615.6 31.7 %all-to-all-start.6 = ((bf16[2,2048,128]{2,0,1:T(2,128)(2,1)}), bf16[2,2048,128]{2,0,1:T(2,128)(2,1)}, u32[]{:S(2)}, u32[]{:S(2)}) async-start(bf16[2,2048,128]{2,0,1:T(2,128)(2,1)} %copy.75), calls=%async_computation.6 | async-start | bytes 2097152 | tf_op jit(solution)/shard_map/all_to_all | solution.py:177
  648.8 5.4 copy-start.1
  654.2 1.6 copy-start.5
  655.7 2.2 copy-start.15
  660.9 1.6 copy-start.4
Sparse Core Ops, SparseCore 0:
  9.6 78.8 all-gather.10
  90.0 76.1 all-gather.8
  168.3 43.3 all-gather.16
  213.1 43.3 all-gather.18
  258.0 154.8 all-gather.12
  436.6 58.7 all-gather.14
